TPU v7x, 32 devices: a whole 2x2x4 slice. The times are simulated.
32 devices in a mesh: row: 8 (over z, core), col: 4 (over y, x).
Axes of the slice: x: 2, y: 2, z: 4, core: 2. Of those that a mesh axis runs over, the one named last changes fastest.
Arguments:
- activations: bfloat16 [1024, 8192], P('col', 'row'), may hold values from -6 to 6
- out_grad: bfloat16 [1024, 8192], P('col', 'row'), may hold values from -6 to 6
- gate_pre: bfloat16 [1024, 16384], P('row', 'col'), may hold values from -8 to 8
- up_proj: bfloat16 [1024, 16384], P('row', 'col'), may hold values from -6 to 6
- gate_weight: bfloat16 [8192, 16384], P('row', 'col'), may hold values from -0.0625 to 0.0625
- up_weight: bfloat16 [8192, 16384], P('row', 'col'), may hold values from -0.0625 to 0.0625
- down_weight: bfloat16 [16384, 8192], P('col', 'row'), may hold values from -0.046875 to 0.046875
Outputs:
- input_grad: bfloat16 [1024, 8192], P('col', 'row')
- gate_grad: bfloat16 [8192, 16384], P('row', 'col')
- up_grad: bfloat16 [8192, 16384], P('row', 'col')
- down_grad: bfloat16 [16384, 8192], P('col', 'row')
All inputs are finite; a program needn't handle non-finite values.
Results may differ from a plain program's by a relative error of at most 0.0051.
Values may be sent and summed in bfloat16 or wider, within the bound.
No kernel may reach another device: no remote copies, remote signals or barrier semaphores. Data moves between devices by JAX's collectives and lax.ppermute only.
A program may use at most 192 MiB of HBM per device.

v0:
```python
import jax
import jax.numpy as jnp
from jax import lax
from jax.sharding import PartitionSpec as P


def local_grads(gate_rows, up_rows, grad_rows):
    gate_float = gate_rows.astype(jnp.float32)
    up_float = up_rows.astype(jnp.float32)
    sigmoid_gate = jax.nn.sigmoid(gate_float)
    silu_gate = gate_float * sigmoid_gate
    hidden_act = (silu_gate * up_float).astype(jnp.bfloat16)
    gate_delta = (
        grad_rows * up_float * sigmoid_gate * (1.0 + gate_float * (1.0 - sigmoid_gate))
    ).astype(jnp.bfloat16)
    up_delta = (grad_rows * silu_gate).astype(jnp.bfloat16)
    return (hidden_act, gate_delta, up_delta)


def body(activations, out_grad, gate_pre, up_proj, gate_weight, up_weight, down_weight):
    act_full, grad_full = (
        lax.all_gather(activations, "col", axis=0, tiled=True),
        lax.all_gather(out_grad, "col", axis=0, tiled=True),
    )
    tokens_all = act_full.shape[0]
    contract_last = (((1,), (1,)), ((), ()))
    contract_first = (((0,), (0,)), ((), ()))
    grad_rows = grad_full
    hid_rows = lax.psum_scatter(
        lax.dot_general(grad_rows, down_weight, contract_last, preferred_element_type=jnp.float32),
        "row",
        scatter_dimension=0,
        tiled=True,
    )
    products = local_grads(gate_pre, up_proj, hid_rows)
    hidden_act = lax.all_gather(products[0], "row", axis=0, tiled=True)
    gate_delta = lax.all_gather(products[1], "row", axis=0, tiled=True)
    up_delta = lax.all_gather(products[2], "row", axis=0, tiled=True)
    grad_rows = grad_full
    acc_down = lax.dot_general(
        hidden_act, grad_rows, contract_first, preferred_element_type=jnp.float32
    )
    acc_gate = lax.dot_general(
        act_full, gate_delta, contract_first, preferred_element_type=jnp.float32
    )
    acc_up = lax.dot_general(act_full, up_delta, contract_first, preferred_element_type=jnp.float32)
    input_rows = lax.dot_general(
        gate_delta, gate_weight, contract_last, preferred_element_type=jnp.float32
    )
    input_rows = input_rows + lax.dot_general(
        up_delta, up_weight, contract_last, preferred_element_type=jnp.float32
    )
    acc_input = input_rows
    totals = (acc_down, acc_gate, acc_up, acc_input)
    acc_down, acc_gate, acc_up, acc_input = totals
    input_rows = lax.psum_scatter(acc_input, "col", scatter_dimension=0, tiled=True).astype(
        jnp.bfloat16
    )
    factor = float(tokens_all) ** (-0.5)
    return (
        input_rows,
        (acc_gate * factor).astype(jnp.bfloat16),
        (acc_up * factor).astype(jnp.bfloat16),
        (acc_down * factor).astype(jnp.bfloat16),
    )


def solution(mesh):
    in_specs = (
        P("col", "row"),
        P("col", "row"),
        P("row", "col"),
        P("row", "col"),
        P("row", "col"),
        P("row", "col"),
        P("col", "row"),
    )
    out_specs = (P("col", "row"), P("row", "col"), P("row", "col"), P("col", "row"))
    return jax.shard_map(body, mesh=mesh, in_specs=in_specs, out_specs=out_specs, check_vma=False)
```

profile of v0, /device:TPU:10, one launch (start us, length us, event | category | flops | bytes accessed | tf_op | source)
XLA Modules:
  0.0 580.6 jit_solution(11149804209979248327)
XLA Ops:
  7.2 0.7 all-gather.6.cloned.1.call-update
  7.9 38.4 %all-gather.6.cloned.1.call-done = bf16[1024,1024]{1,0:T(8,128)(2,1)} async-done(((bf16[256,1024]{1,0:T(8,128)(2,1)}), bf16[1024,1024]{1,0:T(8,128)(2,1)}) %all-gather.6.cloned.1.call-update) | async-done | bytes 2097168 | tf_op jit(solution)/shard_map/all_gather | solution.py:23
  46.3 16.0 %fusion.10 = f32[1024,4096]{1,0:T(8,128)} fusion(bf16[1024,1024]{1,0:T(8,128)(2,1)} %all-gather.6.cloned.1.call-done, bf16[4096,1024]{1,0:T(8,128)(2,1)} %param.13), kind=kOutput, calls=%fused_computation.20 | convolution fusion | flops 8589934592 | bytes 27262976 | tf_op jit(solution)/shard_map/dot_general | solution.py:30
  62.4 0.0 all-gather.8.cloned.1.call-start
  62.4 165.6 %reduce-scatter.3.cloned.1.call-done = f32[128,4096]{1,0:T(8,128)} async-done(((f32[1024,4096]{1,0:T(8,128)}), f32[128,4096]{1,0:T(8,128)}) %reduce-scatter.3.cloned.1.call-update) | async-done | bytes 2097168 | tf_op jit(solution)/shard_map/reduce_scatter | solution.py:29
  228.0 4.4 multiply_convert_fusion.3
  232.4 0.0 all-gather.10.cloned.1.call-start
  232.5 0.5 all-gather.10.cloned.1.call-update
  233.0 0.5 all-gather.12.cloned.1.call-update
  233.6 0.5 all-gather.14.cloned.1.call-update
  234.2 0.2 reduce-scatter.5.cloned.1.call-start
  234.4 78.9 %all-gather.8.cloned.1.call-done = bf16[1024,4096]{1,0:T(8,128)(2,1)} async-done(((bf16[128,4096]{1,0:T(8,128)(2,1)}), bf16[1024,4096]{1,0:T(8,128)(2,1)}) %all-gather.8.cloned.1.call-update) | async-done | bytes 8388624 | tf_op jit(solution)/shard_map/all_gather | solution.py:37
  313.3 15.0 %fusion.11 = f32[1024,1024]{1,0:T(8,128)} fusion(bf16[1024,4096]{1,0:T(8,128)(2,1)} %all-gather.8.cloned.1.call-done, bf16[1024,4096]{1,0:T(8,128)(2,1)} %param.11), kind=kOutput, calls=%fused_computation.21 | convolution fusion | flops 8589934592 | bytes 20971520 | tf_op jit(solution)/shard_map/dot_general | solution.py:47
  328.3 67.6 %all-gather.10.cloned.1.call-done = bf16[1024,4096]{1,0:T(8,128)(2,1)} async-done(((bf16[128,4096]{1,0:T(8,128)(2,1)}), bf16[1024,4096]{1,0:T(8,128)(2,1)}) %all-gather.10.cloned.1.call-update) | async-done | bytes 8388624 | tf_op jit(solution)/shard_map/all_gather | solution.py:38
  396.0 15.7 %convolution_add_fusion = f32[1024,1024]{1,0:T(8,128)} fusion(f32[1024,1024]{1,0:T(8,128)} %fusion.11, bf16[1024,4096]{1,0:T(8,128)(2,1)} %all-gather.10.cloned.1.call-done, bf16[1024,4096]{1,0:T(8,128)(2,1)} %param.12), kind=kOutput, calls=%fused_computation.19 | convolution fusion | flops 8590983168 | bytes 25165824 | tf_op jit(solution)/shard_map/dot_general | solution.py:50
  411.7 22.3 %all-gather.12.cloned.1.call-done = bf16[1024,1024]{1,0:T(8,128)(2,1)} async-done(((bf16[256,1024]{1,0:T(8,128)(2,1)}), bf16[1024,1024]{1,0:T(8,128)(2,1)}) %all-gather.12.cloned.1.call-update) | async-done | bytes 2097168 | tf_op jit(solution)/shard_map/all_gather | solution.py:22
  434.0 14.9 %fusion = bf16[1024,4096]{0,1:T(8,128)(2,1)} fusion(bf16[1024,4096]{1,0:T(8,128)(2,1)} %all-gather.8.cloned.1.call-done, bf16[1024,1024]{1,0:T(8,128)(2,1)} %all-gather.12.cloned.1.call-done), kind=kOutput, calls=%fused_computation.3 | convolution fusion | flops 8598323200 | bytes 18874368 | tf_op jit(solution)/shard_map/dot_general | solution.py:43
  448.9 12.1 %copy.11 = bf16[1024,4096]{1,0:T(8,128)(2,1)} copy(bf16[1024,4096]{0,1:T(8,128)(2,1)} %fusion) | data formatting | bytes 16777216
  461.0 14.7 %fusion.1 = bf16[1024,4096]{0,1:T(8,128)(2,1)} fusion(bf16[1024,4096]{1,0:T(8,128)(2,1)} %all-gather.10.cloned.1.call-done, bf16[1024,1024]{1,0:T(8,128)(2,1)S(1)} %copy-done.3), kind=kOutput, calls=%fused_computation.4 | convolution fusion | flops 8598323200 | bytes 18874368 | tf_op jit(solution)/shard_map/dot_general | solution.py:46
  475.7 12.1 %copy.12 = bf16[1024,4096]{1,0:T(8,128)(2,1)} copy(bf16[1024,4096]{0,1:T(8,128)(2,1)} %fusion.1) | data formatting | bytes 16777216
  487.8 27.3 %all-gather.14.cloned.1.call-done = bf16[1024,4096]{1,0:T(8,128)(2,1)} async-done(((bf16[128,4096]{1,0:T(8,128)(2,1)}), bf16[1024,4096]{1,0:T(8,128)(2,1)}) %all-gather.14.cloned.1.call-update) | async-done | bytes 8388624 | tf_op jit(solution)/shard_map/all_gather | solution.py:36
  515.1 14.6 %multiply_convert_fusion = bf16[4096,1024]{1,0:T(8,128)(2,1)} fusion(bf16[1024,4096]{1,0:T(8,128)(2,1)} %all-gather.14.cloned.1.call-done, bf16[1024,1024]{1,0:T(8,128)(2,1)S(1)} %copy-done.2), kind=kOutput, calls=%fused_computation | convolution fusion | flops 8598323200 | bytes 18874368 | tf_op jit(solution)/shard_map/dot_general | solution.py:40
  529.6 42.0 %reduce-scatter.5.cloned.1.call-done = f32[256,1024]{1,0:T(8,128)} async-done(((f32[1024,1024]{1,0:T(8,128)}), f32[256,1024]{1,0:T(8,128)}) %reduce-scatter.5.cloned.1.call-update) | async-done | bytes 1048592 | tf_op jit(solution)/shard_map/reduce_scatter | solution.py:56
  571.6 2.1 convert_element_type.37
  (15 shorter events, 0.2 us)
Async XLA Ops:
  7.2 39.2 %all-gather.6.cloned.1.call-start = ((), (), s32[]{:S(2)}) async-start(), calls=%async_computation.2 | async-start | bytes 2621440 | tf_op jit(solution)/shard_map/all_gather | solution.py:23
  7.9 220.1 %reduce-scatter.3.cloned.1.call-start = ((), (), s32[]{:S(2)}) async-start(), calls=%async_computation.3 | async-start | bytes 18874368 | tf_op jit(solution)/shard_map/reduce_scatter | solution.py:29
  62.4 165.7 %copy-start = (bf16[128,4096]{1,0:T(8,128)(2,1)S(1)}, bf16[128,4096]{1,0:T(8,128)(2,1)}, u32[]{:S(2)}) copy-start(bf16[128,4096]{1,0:T(8,128)(2,1)} %param.9) | copy-start | bytes 3145732
  62.4 165.7 %copy-start.1 = (bf16[128,4096]{1,0:T(8,128)(2,1)S(1)}, bf16[128,4096]{1,0:T(8,128)(2,1)}, u32[]{:S(2)}) copy-start(bf16[128,4096]{1,0:T(8,128)(2,1)} %param.10) | copy-start | bytes 3145732
  62.4 250.9 %all-gather.8.cloned.1.call-start = ((), (), s32[]{:S(2)}) async-start(), calls=%async_computation.4 | async-start | bytes 9437184 | tf_op jit(solution)/shard_map/all_gather | solution.py:37
  232.4 163.5 %all-gather.10.cloned.1.call-start = ((), (), s32[]{:S(2)}) async-start(), calls=%async_computation.5 | async-start | bytes 9437184 | tf_op jit(solution)/shard_map/all_gather | solution.py:38
  233.0 201.0 %all-gather.12.cloned.1.call-start = ((), (), s32[]{:S(2)}) async-start(), calls=%async_computation.7 | async-start | bytes 2621440 | tf_op jit(solution)/shard_map/all_gather | solution.py:22
  233.6 281.5 %all-gather.14.cloned.1.call-start = ((), (), s32[]{:S(2)}) async-start(), calls=%async_computation.8 | async-start | bytes 9437184 | tf_op jit(solution)/shard_map/all_gather | solution.py:36
  234.2 337.5 %reduce-scatter.5.cloned.1.call-start = ((), (), s32[]{:S(2)}) async-start(), calls=%async_computation.6 | async-start | bytes 5242880 | tf_op jit(solution)/shard_map/reduce_scatter | solution.py:56
  448.9 12.1 %copy-start.3 = (bf16[1024,1024]{1,0:T(8,128)(2,1)S(1)}, bf16[1024,1024]{1,0:T(8,128)(2,1)}, u32[]{:S(2)}) copy-start(bf16[1024,1024]{1,0:T(8,128)(2,1)} %all-gather.12.cloned.1.call-done) | copy-start | bytes 6291460
  475.7 39.4 %copy-start.2 = (bf16[1024,1024]{1,0:T(8,128)(2,1)S(1)}, bf16[1024,1024]{1,0:T(8,128)(2,1)}, u32[]{:S(2)}) copy-start(bf16[1024,1024]{1,0:T(8,128)(2,1)} %all-gather.6.cloned.1.call-done) | copy-start | bytes 6291460
Sparse Core Ops, SparseCore 0:
  9.8 36.4 all-gather.5
  62.5 165.4 reduce-scatter.2
  232.5 80.7 all-gather.7
  315.3 80.5 all-gather.9
  397.6 36.2 all-gather.11
  435.4 79.5 all-gather.13
  518.0 53.5 reduce-scatter.4
where the time goes:
time: 583 us; the launch traced here: 581 us
  waiting for transfers between devices  444 us (76%)
  matrix products  91 us (16%)
  local copies, waits for them, and re-layouts  24.2 us (4%)
  between operations  14.1 us (2%)
  other arithmetic  6.46 us (1%)
    reduce_scatter x1, waiting for transfers between devices, body(): lax.psum_scatter(lax.dot_general(grad_rows, down_weight, contract_last, p...  166 us
    all_gather x1, waiting for transfers between devices, body(): gate_delta = lax.all_gather(products[1], 'row', axis=0, tiled=True)  78.9 us
    all_gather x1, waiting for transfers between devices, body(): up_delta = lax.all_gather(products[2], 'row', axis=0, tiled=True)  67.6 us
    reduce_scatter x1, waiting for transfers between devices, body(): lax.psum_scatter(acc_input, 'col', scatter_dimension=0, tiled=True)  42 us
    all_gather x1, waiting for transfers between devices, body(): lax.all_gather(out_grad, 'col', axis=0, tiled=True)  38.4 us
    all_gather x1, waiting for transfers between devices, body(): hidden_act = lax.all_gather(products[0], 'row', axis=0, tiled=True)  27.3 us
    unnamed x10, local copies, waits for them, and re-layouts  24.2 us
    all_gather x1, waiting for transfers between devices, body(): lax.all_gather(activations, 'col', axis=0, tiled=True)  22.3 us
  transfers between devices with their start and end apart: 7, of which 7 were waited for; matrix products, arithmetic and copies ran while one was open for 17% of the time, Pallas kernels for 0%

commit v1 on v0

v1 whole, which is shorter than its diff:
```python
import jax
import jax.numpy as jnp
from jax import lax
from jax.sharding import PartitionSpec as P


CONTRACT_LAST = (((1,), (1,)), ((), ()))
CONTRACT_FIRST = (((0,), (0,)), ((), ()))
ROW = ("z", "core")


def body(activations, out_grad, gate_pre, up_proj, gate_weight, up_weight, down_weight):
    gate_float = gate_pre.astype(jnp.float32)
    up_float = up_proj.astype(jnp.float32)
    sigmoid_gate = jax.nn.sigmoid(gate_float)
    silu_gate = gate_float * sigmoid_gate
    hidden_local = (silu_gate * up_float).astype(jnp.bfloat16)
    hidden_act = lax.all_gather(hidden_local, ROW, axis=0, tiled=True)

    grad_full = lax.all_gather(out_grad, "col", axis=0, tiled=True)
    act_full = lax.all_gather(activations, "col", axis=0, tiled=True)
    tokens_all = act_full.shape[0]

    hid_partial = lax.dot_general(
        grad_full, down_weight, CONTRACT_LAST, preferred_element_type=jnp.float32
    )
    hid_partial, hidden_act = lax.optimization_barrier((hid_partial, hidden_act))
    chips = lax.axis_size("z")
    hid_partial = hid_partial.reshape(chips, 2, -1, hid_partial.shape[1])
    hid_partial = jnp.swapaxes(hid_partial, 0, 1)
    hid_pair = lax.psum_scatter(hid_partial, "core", scatter_dimension=0, tiled=True)[0]
    hid_rows = lax.psum_scatter(
        hid_pair.astype(jnp.bfloat16), "z", scatter_dimension=0, tiled=True
    )[0].astype(jnp.float32)
    gate_local = (
        hid_rows * up_float * sigmoid_gate * (1.0 + gate_float * (1.0 - sigmoid_gate))
    ).astype(jnp.bfloat16)
    up_local = (hid_rows * silu_gate).astype(jnp.bfloat16)

    acc_down = lax.dot_general(
        hidden_act, grad_full, CONTRACT_FIRST, preferred_element_type=jnp.float32
    )
    gate_delta = lax.all_gather(gate_local, ROW, axis=0, tiled=True)
    up_delta = lax.all_gather(up_local, ROW, axis=0, tiled=True)
    acc_gate = lax.dot_general(
        act_full, gate_delta, CONTRACT_FIRST, preferred_element_type=jnp.float32
    )
    acc_up = lax.dot_general(act_full, up_delta, CONTRACT_FIRST, preferred_element_type=jnp.float32)
    input_rows = lax.dot_general(
        gate_delta, gate_weight, CONTRACT_LAST, preferred_element_type=jnp.float32
    )
    input_rows = input_rows + lax.dot_general(
        up_delta, up_weight, CONTRACT_LAST, preferred_element_type=jnp.float32
    )
    input_rows = lax.psum_scatter(input_rows, "col", scatter_dimension=0, tiled=True).astype(
        jnp.bfloat16
    )
    factor = float(tokens_all) ** (-0.5)
    return (
        input_rows,
        (acc_gate * factor).astype(jnp.bfloat16),
        (acc_up * factor).astype(jnp.bfloat16),
        (acc_down * factor).astype(jnp.bfloat16),
    )


def solution(mesh):
    in_specs = (
        P("col", ROW),
        P("col", ROW),
        P(ROW, "col"),
        P(ROW, "col"),
        P(ROW, "col"),
        P(ROW, "col"),
        P("col", ROW),
    )
    out_specs = (P("col", ROW), P(ROW, "col"), P(ROW, "col"), P("col", ROW))
    devices = mesh.devices.reshape(mesh.shape["row"] // 2, 2, mesh.shape["col"])
    split_mesh = jax.sharding.Mesh(devices, ("z", "core", "col"))
    return jax.shard_map(body, mesh=split_mesh, in_specs=in_specs, out_specs=out_specs, check_vma=False)
```

time: 583 us -> 523 us (0.90)
  waiting for transfers between devices: 444 us -> 364 us
  local copies, waits for them, and re-layouts: 24.2 us -> 35.7 us
  other arithmetic: 6.46 us -> 14.9 us
    reduce_scatter x2 -> x3, waiting for transfers between devices: 208 us -> 107 us  [the longest x1 77.8 us: body(): lax.psum_scatter(hid_pair.astype(jnp.bfloat16), 'z', scatter_dimension=0,...]
    all_gather x5, waiting for transfers between devices: 234 us -> 255 us  [the longest x1 78.7 us: body(): gate_delta = lax.all_gather(gate_local, ROW, axis=0, tiled=True)]
    reshape x0 -> x1, local copies, waits for them, and re-layouts: none -> 11.6 us  [body(): hid_partial = hid_partial.reshape(chips, 2, -1, hid_partial.shape[1])]
    convert_element_type x2 -> x4, other arithmetic: 6.46 us -> 14.9 us  [the longest x1 6.02 us: body(): hid_pair.astype(jnp.bfloat16)]
  transfers between devices with their start and end apart: 7 -> 8, of which waited for: 7 -> 8; matrix products, arithmetic and copies ran while one was open for 17% -> 23% of each run, Pallas kernels for 0% -> 0%
where the time goes in v1:
time: 523 us; the launch traced here: 521 us
  waiting for transfers between devices  364 us (70%)
  matrix products  91.2 us (17%)
  local copies, waits for them, and re-layouts  35.7 us (7%)
  other arithmetic  14.9 us (3%)
  between operations  14.2 us (3%)
    all_gather x1, waiting for transfers between devices, body(): gate_delta = lax.all_gather(gate_local, ROW, axis=0, tiled=True)  78.7 us
    reduce_scatter x1, waiting for transfers between devices, body(): lax.psum_scatter(hid_pair.astype(jnp.bfloat16), 'z', scatter_dimension=0,...  77.8 us
    all_gather x1, waiting for transfers between devices, body(): up_delta = lax.all_gather(up_local, ROW, axis=0, tiled=True)  67.6 us
    all_gather x1, waiting for transfers between devices, body(): hidden_act = lax.all_gather(hidden_local, ROW, axis=0, tiled=True)  65.8 us
    all_gather x1, waiting for transfers between devices, body(): grad_full = lax.all_gather(out_grad, 'col', axis=0, tiled=True)  35.2 us
    reduce_scatter x1, waiting for transfers between devices, body(): lax.psum_scatter(hid_partial, 'core', scatter_dimension=0, tiled=True)[0]  27.7 us
    unnamed x10, local copies, waits for them, and re-layouts  24.2 us
    dot_general x1, matrix products, body(): lax.dot_general(grad_full, down_weight, CONTRACT_LAST, preferred_element_...  16 us
  transfers between devices with their start and end apart: 8, of which 8 were waited for; matrix products, arithmetic and copies ran while one was open for 23% of the time, Pallas kernels for 0%

profile of v1, /device:TPU:10, one launch (start us, length us, event | category | flops | bytes accessed | tf_op | source)
XLA Modules:
  0.0 520.7 jit_solution(16609632898383462598)
XLA Ops:
  7.2 0.7 all-gather.6.cloned.1.call-update
  7.9 3.1 fusion.2
  11.2 35.2 %all-gather.6.cloned.1.call-done = bf16[1024,1024]{1,0:T(8,128)(2,1)} async-done(((bf16[256,1024]{1,0:T(8,128)(2,1)}), bf16[1024,1024]{1,0:T(8,128)(2,1)}) %all-gather.6.cloned.1.call-update) | async-done | bytes 2097168 | tf_op jit(solution)/shard_map/all_gather | solution.py:20
  46.3 16.0 %fusion.11 = f32[1024,4096]{1,0:T(8,128)} fusion(bf16[1024,1024]{1,0:T(8,128)(2,1)} %all-gather.6.cloned.1.call-done, bf16[4096,1024]{1,0:T(8,128)(2,1)} %param.13), kind=kOutput, calls=%fused_computation.23 | convolution fusion | flops 8589934592 | bytes 27262976 | tf_op jit(solution)/shard_map/dot_general | solution.py:24
  62.4 65.8 %all-gather.8.cloned.1.call-done = bf16[1024,4096]{1,0:T(8,128)(2,1)} async-done(((bf16[128,4096]{1,0:T(8,128)(2,1)}), bf16[1024,4096]{1,0:T(8,128)(2,1)}) %all-gather.8.cloned.1.call-update) | async-done | bytes 8388624 | tf_op jit(solution)/shard_map/all_gather | solution.py:18
  128.1 11.6 %copy.15 = f32[4,2,128,4096]{3,2,0,1:T(8,128)} copy(f32[4,2,128,4096]{3,2,1,0:T(8,128)} %bitcast.27) | data formatting | bytes 33554432 | tf_op jit(solution)/shard_map/reshape | solution.py:29
  139.8 27.7 %reduce-scatter.4.cloned.1.call-done = f32[1,4,128,4096]{3,2,1,0:T(8,128)} async-done(((f32[2,4,128,4096]{3,2,1,0:T(8,128)}), f32[1,4,128,4096]{3,2,1,0:T(8,128)}) %reduce-scatter.4.cloned.1.call-update) | async-done | bytes 8388624 | tf_op jit(solution)/shard_map/reduce_scatter | solution.py:31
  167.5 6.0 %convert_bitcast_fusion = bf16[4,128,4096]{2,1,0:T(8,128)(2,1)} fusion(f32[1,4,128,4096]{3,2,1,0:T(8,128)} %reduce-scatter.4.cloned.1.call-done), kind=kLoop, calls=%fused_computation.6 | loop fusion | flops 2097152 | bytes 12582912 | tf_op jit(solution)/shard_map/convert_element_type | solution.py:33
  173.6 77.8 %reduce-scatter.6.cloned.1.call-done = bf16[1,128,4096]{2,1,0:T(8,128)(2,1)} async-done(((bf16[4,128,4096]{2,1,0:T(8,128)(2,1)}), bf16[1,128,4096]{2,1,0:T(8,128)(2,1)}) %reduce-scatter.6.cloned.1.call-update) | async-done | bytes 1048592 | tf_op jit(solution)/shard_map/reduce_scatter | solution.py:32
  251.4 3.7 fusion.6
  255.1 0.5 all-gather.12.cloned.1.call-update
  255.7 0.7 all-gather.14.cloned.1.call-update
  256.6 78.7 %all-gather.10.cloned.1.call-done = bf16[1024,4096]{1,0:T(8,128)(2,1)} async-done(((bf16[128,4096]{1,0:T(8,128)(2,1)}), bf16[1024,4096]{1,0:T(8,128)(2,1)}) %all-gather.10.cloned.1.call-update) | async-done | bytes 8388624 | tf_op jit(solution)/shard_map/all_gather | solution.py:43
  335.3 15.0 %fusion.12 = f32[1024,1024]{1,0:T(8,128)} fusion(bf16[1024,4096]{1,0:T(8,128)(2,1)} %all-gather.10.cloned.1.call-done, bf16[1024,4096]{1,0:T(8,128)(2,1)} %param.11), kind=kOutput, calls=%fused_computation.24 | convolution fusion | flops 8589934592 | bytes 20971520 | tf_op jit(solution)/shard_map/dot_general | solution.py:49
  350.4 67.6 %all-gather.12.cloned.1.call-done = bf16[1024,4096]{1,0:T(8,128)(2,1)} async-done(((bf16[128,4096]{1,0:T(8,128)(2,1)}), bf16[1024,4096]{1,0:T(8,128)(2,1)}) %all-gather.12.cloned.1.call-update) | async-done | bytes 8388624 | tf_op jit(solution)/shard_map/all_gather | solution.py:44
  418.0 15.7 %convolution_add_fusion = f32[1024,1024]{1,0:T(8,128)} fusion(f32[1024,1024]{1,0:T(8,128)} %fusion.12, bf16[1024,4096]{1,0:T(8,128)(2,1)} %all-gather.12.cloned.1.call-done, bf16[1024,4096]{1,0:T(8,128)(2,1)} %param.12), kind=kOutput, calls=%fused_computation.22 | convolution fusion | flops 8590983168 | bytes 25165824 | tf_op jit(solution)/shard_map/dot_general | solution.py:52
  433.7 14.8 %multiply_convert_fusion = bf16[4096,1024]{1,0:T(8,128)(2,1)} fusion(bf16[1024,4096]{1,0:T(8,128)(2,1)} %all-gather.8.cloned.1.call-done, bf16[1024,1024]{1,0:T(8,128)(2,1)S(1)} %copy-done.2), kind=kOutput, calls=%fused_computation.1 | convolution fusion | flops 8598323200 | bytes 18874368 | tf_op jit(solution)/shard_map/dot_general | solution.py:40
  448.5 7.6 %all-gather.14.cloned.1.call-done = bf16[1024,1024]{1,0:T(8,128)(2,1)} async-done(((bf16[256,1024]{1,0:T(8,128)(2,1)}), bf16[1024,1024]{1,0:T(8,128)(2,1)}) %all-gather.14.cloned.1.call-update) | async-done | bytes 2097168 | tf_op jit(solution)/shard_map/all_gather | solution.py:21
  456.1 14.9 %fusion = bf16[1024,4096]{0,1:T(8,128)(2,1)} fusion(bf16[1024,4096]{1,0:T(8,128)(2,1)} %all-gather.10.cloned.1.call-done, bf16[1024,1024]{1,0:T(8,128)(2,1)} %all-gather.14.cloned.1.call-done), kind=kOutput, calls=%fused_computation.4 | convolution fusion | flops 8598323200 | bytes 18874368 | tf_op jit(solution)/shard_map/dot_general | solution.py:45
  471.0 12.2 %copy.12 = bf16[1024,4096]{1,0:T(8,128)(2,1)} copy(bf16[1024,4096]{0,1:T(8,128)(2,1)} %fusion) | data formatting | bytes 16777216
  483.3 14.7 %fusion.1 = bf16[1024,4096]{0,1:T(8,128)(2,1)} fusion(bf16[1024,4096]{1,0:T(8,128)(2,1)} %all-gather.12.cloned.1.call-done, bf16[1024,1024]{1,0:T(8,128)(2,1)S(1)} %copy-done.3), kind=kOutput, calls=%fused_computation.5 | convolution fusion | flops 8598323200 | bytes 18874368 | tf_op jit(solution)/shard_map/dot_general | solution.py:48
  498.0 11.9 %copy.13 = bf16[1024,4096]{1,0:T(8,128)(2,1)} copy(bf16[1024,4096]{0,1:T(8,128)(2,1)} %fusion.1) | data formatting | bytes 16777216
  509.9 1.8 reduce-scatter.8.cloned.1.call-done
  511.7 2.1 convert_element_type.54
  (21 shorter events, 0.6 us)
Async XLA Ops:
  7.2 39.2 %all-gather.6.cloned.1.call-start = ((), (), s32[]{:S(2)}) async-start(), calls=%async_computation.3 | async-start | bytes 2621440 | tf_op jit(solution)/shard_map/all_gather | solution.py:20
  7.9 120.2 %all-gather.8.cloned.1.call-start = ((), (), s32[]{:S(2)}) async-start(), calls=%async_computation.4 | async-start | bytes 9437184 | tf_op jit(solution)/shard_map/all_gather | solution.py:18
  11.1 156.4 %reduce-scatter.4.cloned.1.call-start = ((), (), s32[]{:S(2)}) async-start(), calls=%async_computation.5 | async-start | bytes 25165824 | tf_op jit(solution)/shard_map/reduce_scatter | solution.py:31
  139.8 111.6 %copy-start = (bf16[128,4096]{1,0:T(8,128)(2,1)S(1)}, bf16[128,4096]{1,0:T(8,128)(2,1)}, u32[]{:S(2)}) copy-start(bf16[128,4096]{1,0:T(8,128)(2,1)} %param.10) | copy-start | bytes 3145732
  139.8 111.6 %copy-start.1 = (bf16[128,4096]{1,0:T(8,128)(2,1)S(1)}, bf16[128,4096]{1,0:T(8,128)(2,1)}, u32[]{:S(2)}) copy-start(bf16[128,4096]{1,0:T(8,128)(2,1)} %param.9) | copy-start | bytes 3145732
  139.8 111.6 %reduce-scatter.6.cloned.1.call-start = ((), (), s32[]{:S(2)}) async-start(), calls=%async_computation.6 | async-start | bytes 5242880 | tf_op jit(solution)/shard_map/reduce_scatter | solution.py:32
  173.5 161.8 %all-gather.10.cloned.1.call-start = ((), (), s32[]{:S(2)}) async-start(), calls=%async_computation.7 | async-start | bytes 9437184 | tf_op jit(solution)/shard_map/all_gather | solution.py:43
  255.1 162.9 %all-gather.12.cloned.1.call-start = ((), (), s32[]{:S(2)}) async-start(), calls=%async_computation.8 | async-start | bytes 9437184 | tf_op jit(solution)/shard_map/all_gather | solution.py:44
  255.6 200.5 %all-gather.14.cloned.1.call-start = ((), (), s32[]{:S(2)}) async-start(), calls=%async_computation.10 | async-start | bytes 2621440 | tf_op jit(solution)/shard_map/all_gather | solution.py:21
  256.4 255.3 %reduce-scatter.8.cloned.1.call-start = ((), (), s32[]{:S(2)}) async-start(), calls=%async_computation.9 | async-start | bytes 5242880 | tf_op jit(solution)/shard_map/reduce_scatter | solution.py:55
  350.4 83.3 %copy-start.2 = (bf16[1024,1024]{1,0:T(8,128)(2,1)S(1)}, bf16[1024,1024]{1,0:T(8,128)(2,1)}, u32[]{:S(2)}) copy-start(bf16[1024,1024]{1,0:T(8,128)(2,1)} %all-gather.6.cloned.1.call-done) | copy-start | bytes 6291460
  471.0 12.2 %copy-start.3 = (bf16[1024,1024]{1,0:T(8,128)(2,1)S(1)}, bf16[1024,1024]{1,0:T(8,128)(2,1)}, u32[]{:S(2)}) copy-start(bf16[1024,1024]{1,0:T(8,128)(2,1)} %all-gather.14.cloned.1.call-done) | copy-start | bytes 6291460
Sparse Core Ops, SparseCore 0:
  9.8 36.4 all-gather.5
  48.5 79.6 all-gather.7
  139.9 27.5 reduce-scatter.3
  173.7 77.6 reduce-scatter.5
  255.2 80.1 all-gather.9
  337.4 80.5 all-gather.11
  419.8 36.2 all-gather.13
  459.1 52.5 reduce-scatter.7

commit v2 on v1

v2 whole, which is shorter than its diff:
```python
import jax
import jax.numpy as jnp
from jax import lax
from jax.sharding import PartitionSpec as P


CONTRACT_LAST = (((1,), (1,)), ((), ()))
CONTRACT_FIRST = (((0,), (0,)), ((), ()))
ROW = ("z", "core")


def shift_perm(n, s):
    return [(i, (i + s) % n) for i in range(n)]


def gather_col(block):
    n = lax.axis_size("col")
    c = lax.axis_index("col")
    rows = block.shape[0]
    full = jnp.zeros((n * rows,) + block.shape[1:], block.dtype)
    full = lax.dynamic_update_slice_in_dim(full, block, c * rows, axis=0)
    for s in range(1, n):
        part = lax.ppermute(block, "col", shift_perm(n, s))
        full = lax.dynamic_update_slice_in_dim(full, part, ((c - s) % n) * rows, axis=0)
    return full


def reduce_scatter_col(partial):
    n = lax.axis_size("col")
    c = lax.axis_index("col")
    blocks = partial.reshape((n, -1) + partial.shape[1:])
    total = lax.dynamic_index_in_dim(blocks, c, axis=0, keepdims=False)
    for s in range(1, n):
        piece = lax.dynamic_index_in_dim(blocks, (c + s) % n, axis=0, keepdims=False)
        total = total + lax.ppermute(piece, "col", shift_perm(n, s))
    return total


def body(activations, out_grad, gate_pre, up_proj, gate_weight, up_weight, down_weight):
    gate_float = gate_pre.astype(jnp.float32)
    up_float = up_proj.astype(jnp.float32)
    sigmoid_gate = jax.nn.sigmoid(gate_float)
    silu_gate = gate_float * sigmoid_gate
    hidden_local = (silu_gate * up_float).astype(jnp.bfloat16)
    hidden_act = lax.all_gather(hidden_local, ROW, axis=0, tiled=True)

    grad_full = gather_col(out_grad)
    act_full = gather_col(activations)
    tokens_all = act_full.shape[0]

    chips = lax.axis_size("z")
    z = lax.axis_index("z")
    core = lax.axis_index("core")
    width = grad_full.shape[1]
    grad_blocks = grad_full.reshape(chips, 2, -1, width)
    grad_send = lax.dynamic_index_in_dim(grad_blocks, 1 - core, axis=1, keepdims=False)
    grad_keep = lax.dynamic_index_in_dim(grad_blocks, core, axis=1, keepdims=False)
    hid_send = lax.dot_general(
        grad_send.reshape(-1, width), down_weight, CONTRACT_LAST,
        preferred_element_type=jnp.float32,
    )
    hid_recv = lax.ppermute(hid_send, "core", [(0, 1), (1, 0)])
    hid_keep = lax.dot_general(
        grad_keep.reshape(-1, width), down_weight, CONTRACT_LAST,
        preferred_element_type=jnp.float32,
    )
    chip_sum = (hid_keep + hid_recv).reshape(chips, -1, hid_keep.shape[1])
    chip_sum, hidden_act = lax.optimization_barrier((chip_sum, hidden_act))
    hid_rows = lax.dynamic_index_in_dim(chip_sum, z, axis=0, keepdims=False)
    for s in range(1, chips):
        piece = lax.dynamic_index_in_dim(chip_sum, (z + s) % chips, axis=0, keepdims=False)
        piece = lax.ppermute(piece.astype(jnp.bfloat16), "z", shift_perm(chips, s))
        hid_rows = hid_rows + piece.astype(jnp.float32)

    gate_local = (
        hid_rows * up_float * sigmoid_gate * (1.0 + gate_float * (1.0 - sigmoid_gate))
    ).astype(jnp.bfloat16)
    up_local = (hid_rows * silu_gate).astype(jnp.bfloat16)

    acc_down = lax.dot_general(
        hidden_act, grad_full, CONTRACT_FIRST, preferred_element_type=jnp.float32
    )
    gate_delta = lax.all_gather(gate_local, ROW, axis=0, tiled=True)
    up_delta = lax.all_gather(up_local, ROW, axis=0, tiled=True)
    acc_gate = lax.dot_general(
        act_full, gate_delta, CONTRACT_FIRST, preferred_element_type=jnp.float32
    )
    input_gate = reduce_scatter_col(
        lax.dot_general(gate_delta, gate_weight, CONTRACT_LAST, preferred_element_type=jnp.float32)
    )
    acc_up = lax.dot_general(act_full, up_delta, CONTRACT_FIRST, preferred_element_type=jnp.float32)
    input_up = reduce_scatter_col(
        lax.dot_general(up_delta, up_weight, CONTRACT_LAST, preferred_element_type=jnp.float32)
    )
    input_rows = (input_gate + input_up).astype(jnp.bfloat16)
    factor = float(tokens_all) ** (-0.5)
    return (
        input_rows,
        (acc_gate * factor).astype(jnp.bfloat16),
        (acc_up * factor).astype(jnp.bfloat16),
        (acc_down * factor).astype(jnp.bfloat16),
    )


def solution(mesh):
    in_specs = (
        P("col", ROW),
        P("col", ROW),
        P(ROW, "col"),
        P(ROW, "col"),
        P(ROW, "col"),
        P(ROW, "col"),
        P("col", ROW),
    )
    out_specs = (P("col", ROW), P(ROW, "col"), P(ROW, "col"), P("col", ROW))
    devices = mesh.devices.reshape(mesh.shape["row"] // 2, 2, mesh.shape["col"])
    split_mesh = jax.sharding.Mesh(devices, ("z", "core", "col"))
    return jax.shard_map(body, mesh=split_mesh, in_specs=in_specs, out_specs=out_specs, check_vma=False)
```

time: 523 us -> 435 us (0.83)
  waiting for transfers between devices: 364 us -> 281 us
  starting transfers between devices: 0.5 us -> 20.1 us
  local copies, waits for them, and re-layouts: 35.7 us -> 18.2 us
    ppermute x0 -> x16, waiting for transfers between devices: none -> 160 us  [the longest x3 90.2 us: body(): piece = lax.ppermute(piece.astype(jnp.bfloat16), 'z', shift_perm(chips, s))]
    reduce_scatter x3 -> x0, waiting for transfers between devices: 107 us -> none  [the longest x1 77.8 us: body(): lax.psum_scatter(hid_pair.astype(jnp.bfloat16), 'z', scatter_dimension=0,...]
    all_gather x1, waiting for transfers between devices: 65.8 us -> 21.3 us  [body(): hidden_act = lax.all_gather(hidden_local, ROW, axis=0, tiled=True)]
    all_gather x1, waiting for transfers between devices: 78.7 us -> 35 us  [body(): gate_delta = lax.all_gather(gate_local, ROW, axis=0, tiled=True)]
    all_gather x2 -> x0, waiting for transfers between devices: 42.8 us -> none  [the longest x1 35.2 us: body(): grad_full = lax.all_gather(out_grad, 'col', axis=0, tiled=True)]
    unnamed x10 -> x14, local copies, waits for them, and re-layouts: 24.2 us -> 1.41 us
    ppermute x0 -> x16, starting transfers between devices: none -> 20 us  [the longest x6 7.54 us: reduce_scatter_col(): total = total + lax.ppermute(piece, 'col', shift_perm(n, s))]
    reshape x1 -> x0, local copies, waits for them, and re-layouts: 11.6 us -> none  [body(): hid_partial = hid_partial.reshape(chips, 2, -1, hid_partial.shape[1])]
  transfers between devices with their start and end apart: 8 -> 19, of which waited for: 8 -> 12; matrix products, arithmetic and copies ran while one was open for 23% -> 23% of each run, Pallas kernels for 0% -> 0%
where the time goes in v2:
time: 435 us; the launch traced here: 431 us
  waiting for transfers between devices  281 us (65%)
  matrix products  86.1 us (20%)
  starting transfers between devices  20.1 us (5%)
  local copies, waits for them, and re-layouts  18.2 us (4%)
  between operations  13.9 us (3%)
  other arithmetic  11.6 us (3%)
    ppermute x3, waiting for transfers between devices, body(): piece = lax.ppermute(piece.astype(jnp.bfloat16), 'z', shift_perm(chips, s))  90.2 us
    all_gather x1, waiting for transfers between devices, body(): up_delta = lax.all_gather(up_local, ROW, axis=0, tiled=True)  63.7 us
    ppermute x6, waiting for transfers between devices, gather_col(): part = lax.ppermute(block, 'col', shift_perm(n, s))  39.1 us
    all_gather x1, waiting for transfers between devices, body(): gate_delta = lax.all_gather(gate_local, ROW, axis=0, tiled=True)  35 us
    all_gather x1, waiting for transfers between devices, body(): hidden_act = lax.all_gather(hidden_local, ROW, axis=0, tiled=True)  21.3 us
    ppermute x6, waiting for transfers between devices, reduce_scatter_col(): total = total + lax.ppermute(piece, 'col', shift_perm(n, s))  17.1 us
    dot_general x1, matrix products, body(): lax.dot_general(act_full, up_delta, CONTRACT_FIRST, preferred_element_typ...  15.1 us
    dot_general x1, matrix products, body(): lax.dot_general(hidden_act, grad_full, CONTRACT_FIRST, preferred_element_...  14.6 us
  transfers between devices with their start and end apart: 19, of which 12 were waited for; matrix products, arithmetic and copies ran while one was open for 23% of the time, Pallas kernels for 0%

profile of v2, /device:TPU:10, one launch (start us, length us, event | category | flops | bytes accessed | tf_op | source)
XLA Modules:
  0.0 430.6 jit_solution(15599078574912648902)
XLA Ops:
  7.2 3.2 fusion
  14.4 11.0 %collective-permute-done = bf16[256,1024]{1,0:T(8,128)(2,1)} collective-permute-done((bf16[256,1024]{1,0:T(8,128)(2,1)S(1)}, bf16[256,1024]{1,0:T(8,128)(2,1)}, u32[]{:S(2)}, u32[]{:S(2)}) %collective-permute-start) | collective-permute-done | bytes 524320 | tf_op jit(solution)/shard_map/ppermute | solution.py:23
  26.5 10.2 %collective-permute-done.1 = bf16[256,1024]{1,0:T(8,128)(2,1)} collective-permute-done((bf16[256,1024]{1,0:T(8,128)(2,1)S(1)}, bf16[256,1024]{1,0:T(8,128)(2,1)}, u32[]{:S(2)}, u32[]{:S(2)}) %collective-permute-start.1) | collective-permute-done | bytes 524320 | tf_op jit(solution)/shard_map/ppermute | solution.py:23
  38.2 6.8 %fusion.19 = f32[512,4096]{1,0:T(8,128)} fusion(bf16[512,1024]{1,0:T(8,128)(2,1)S(1)} %bitcast.74, bf16[4096,1024]{1,0:T(8,128)(2,1)S(1)} %copy-done.4), kind=kOutput, calls=%fused_computation.51 | convolution fusion | flops 4294967296 | bytes 17825792 | tf_op jit(solution)/shard_map/dot_general | solution.py:58
  45.0 13.5 %collective-permute-done.3 = f32[512,4096]{1,0:T(8,128)} collective-permute-done((f32[512,4096]{1,0:T(8,128)}, f32[512,4096]{1,0:T(8,128)}, u32[]{:S(2)}, u32[]{:S(2)}) %collective-permute-start.3) | collective-permute-done | bytes 8388640 | tf_op jit(solution)/shard_map/ppermute | solution.py:62
  58.5 11.6 %convolution_add_fusion = f32[512,4096]{1,0:T(8,128)} fusion(f32[512,4096]{1,0:T(8,128)} %collective-permute-done.3, bf16[512,1024]{1,0:T(8,128)(2,1)S(1)} %bitcast.73, bf16[4096,1024]{1,0:T(8,128)(2,1)} %param.13), kind=kOutput, calls=%fused_computation.3 | convolution fusion | flops 4297064448 | bytes 26214400 | tf_op jit(solution)/shard_map/dot_general | solution.py:63
  70.0 21.3 %all-gather.4.cloned.1.call-done = bf16[1024,4096]{1,0:T(8,128)(2,1)} async-done(((bf16[128,4096]{1,0:T(8,128)(2,1)}), bf16[1024,4096]{1,0:T(8,128)(2,1)}) %all-gather.4.cloned.1.call-update) | async-done | bytes 8388624 | tf_op jit(solution)/shard_map/all_gather | solution.py:45
  91.3 4.8 %fusion.10 = (bf16[128,4096]{1,0:T(8,128)(2,1)}, bf16[128,4096]{1,0:T(8,128)(2,1)}, bf16[128,4096]{1,0:T(8,128)(2,1)}) fusion(f32[4,128,4096]{2,1,0:T(8,128)} %bitcast.71, s32[]{:T(128)S(6)} %select_n.115, s32[]{:T(128)S(6)} %select_n.119, s32[]{:T(128)S(6)} %select_n.117), kind=kLoop, calls=%fused_computation.24 | loop fusion | bytes 6291468 | tf_op jit(solution)/shard_map/convert_element_type | solution.py:72
  98.6 2.9 collective-permute-start.5
  101.5 21.9 %collective-permute-done.4 = bf16[128,4096]{1,0:T(8,128)(2,1)} collective-permute-done((bf16[128,4096]{1,0:T(8,128)(2,1)}, bf16[128,4096]{1,0:T(8,128)(2,1)}, u32[]{:S(2)}, u32[]{:S(2)}) %collective-permute-start.4) | collective-permute-done | bytes 1048608 | tf_op jit(solution)/shard_map/ppermute | solution.py:72
  123.4 65.8 %collective-permute-done.5 = bf16[128,4096]{1,0:T(8,128)(2,1)} collective-permute-done((bf16[128,4096]{1,0:T(8,128)(2,1)}, bf16[128,4096]{1,0:T(8,128)(2,1)}, u32[]{:S(2)}, u32[]{:S(2)}) %collective-permute-start.5) | collective-permute-done | bytes 1048608 | tf_op jit(solution)/shard_map/ppermute | solution.py:72
  189.1 2.5 collective-permute-done.6
  191.7 5.6 %fusion.3 = (bf16[128,4096]{1,0:T(8,128)(2,1)}, bf16[128,4096]{1,0:T(8,128)(2,1)}) fusion(bf16[128,4096]{1,0:T(8,128)(2,1)S(1)} %copy-done, bf16[128,4096]{1,0:T(8,128)(2,1)} %param.9, bf16[128,4096]{1,0:T(8,128)(2,1)} %collective-permute-done.6, bf16[128,4096]{1,0:T(8,128)(2,1)} %collective-permute-done.5, bf16[128,4096]{1,0:T(8,128)(2,1)} %collective-permute-done.4, ...), kind=kLoop, calls=%fused_computation.12 | loop fusion | flops 11010048 | bytes 9437188 | tf_op jit(solution)/shard_map/convert_element_type | solution.py:77
  204.3 9.0 %collective-permute-done.13 = bf16[256,1024]{1,0:T(8,128)(2,1)} collective-permute-done((bf16[256,1024]{1,0:T(8,128)(2,1)S(1)}, bf16[256,1024]{1,0:T(8,128)(2,1)}, u32[]{:S(2)}, u32[]{:S(2)}) %collective-permute-start.13) | collective-permute-done | bytes 524320 | tf_op jit(solution)/shard_map/ppermute | solution.py:23
  215.3 8.9 %collective-permute-done.14 = bf16[256,1024]{1,0:T(8,128)(2,1)} collective-permute-done((bf16[256,1024]{1,0:T(8,128)(2,1)S(1)}, bf16[256,1024]{1,0:T(8,128)(2,1)}, u32[]{:S(2)}, u32[]{:S(2)}) %collective-permute-start.14) | collective-permute-done | bytes 524320 | tf_op jit(solution)/shard_map/ppermute | solution.py:23
  226.9 14.6 %multiply_convert_fusion = bf16[4096,1024]{1,0:T(8,128)(2,1)} fusion(bf16[1024,4096]{1,0:T(8,128)(2,1)} %all-gather.4.cloned.1.call-done, bf16[1024,1024]{1,0:T(8,128)(2,1)S(1)} %constant_dynamic-update-slice_fusion.4), kind=kOutput, calls=%fused_computation | convolution fusion | flops 8598323200 | bytes 18874368 | tf_op jit(solution)/shard_map/dot_general | solution.py:80
  241.4 35.0 %all-gather.6.cloned.1.call-done = bf16[1024,4096]{1,0:T(8,128)(2,1)} async-done(((bf16[128,4096]{1,0:T(8,128)(2,1)}), bf16[1024,4096]{1,0:T(8,128)(2,1)}) %all-gather.6.cloned.1.call-update) | async-done | bytes 8388624 | tf_op jit(solution)/shard_map/all_gather | solution.py:83
  276.5 12.6 %fusion.20 = f32[1024,1024]{1,0:T(8,128)S(1)} fusion(bf16[1024,4096]{1,0:T(8,128)(2,1)} %all-gather.6.cloned.1.call-done, bf16[1024,4096]{1,0:T(8,128)(2,1)} %param.11), kind=kOutput, calls=%fused_computation.52 | convolution fusion | flops 8589934592 | bytes 20971520 | tf_op jit(solution)/shard_map/dot_general | solution.py:89
  295.5 63.7 %all-gather.8.cloned.1.call-done = bf16[1024,4096]{1,0:T(8,128)(2,1)} async-done(((bf16[128,4096]{1,0:T(8,128)(2,1)}), bf16[1024,4096]{1,0:T(8,128)(2,1)}) %all-gather.8.cloned.1.call-update) | async-done | bytes 8388624 | tf_op jit(solution)/shard_map/all_gather | solution.py:84
  359.3 12.6 %fusion.21 = f32[1024,1024]{1,0:T(8,128)S(1)} fusion(bf16[1024,4096]{1,0:T(8,128)(2,1)} %all-gather.8.cloned.1.call-done, bf16[1024,4096]{1,0:T(8,128)(2,1)} %param.12), kind=kOutput, calls=%fused_computation.53 | convolution fusion | flops 8589934592 | bytes 20971520 | tf_op jit(solution)/shard_map/dot_general | solution.py:93
  374.2 15.1 %multiply_convert_fusion.1 = bf16[1024,4096]{1,0:T(8,128)(2,1)} fusion(bf16[1024,1024]{1,0:T(8,128)(2,1)} %constant_dynamic-update-slice_fusion.3, bf16[1024,4096]{1,0:T(8,128)(2,1)} %all-gather.8.cloned.1.call-done), kind=kOutput, calls=%fused_computation.1 | convolution fusion | flops 8598323200 | bytes 18874368 | tf_op jit(solution)/shard_map/dot_general | solution.py:91
  391.4 12.8 %multiply_convert_fusion.2 = bf16[1024,4096]{1,0:T(8,128)(2,1)} fusion(bf16[1024,1024]{1,0:T(8,128)(2,1)} %constant_dynamic-update-slice_fusion.3, bf16[1024,4096]{1,0:T(8,128)(2,1)S(1)} %bitcast.76), kind=kOutput, calls=%fused_computation.2 | convolution fusion | flops 8598323200 | bytes 18874368 | tf_op jit(solution)/shard_map/dot_general | solution.py:85
  404.2 17.1 %collective-permute-done.11 = f32[256,1024]{1,0:T(8,128)S(1)} collective-permute-done((f32[256,1024]{1,0:T(8,128)S(1)}, f32[256,1024]{1,0:T(8,128)S(1)}, u32[]{:S(2)}, u32[]{:S(2)}) %collective-permute-start.11) | collective-permute-done | bytes 1048608 | tf_op jit(solution)/shard_map/ppermute | solution.py:35
  421.3 2.8 fusion.16
  (56 shorter events, 31.4 us)
Async XLA Ops:
  7.2 3.3 copy-start.2
  7.2 84.2 %all-gather.4.cloned.1.call-start = ((), (), s32[]{:S(2)}) async-start(), calls=%async_computation | async-start | bytes 9437184 | tf_op jit(solution)/shard_map/all_gather | solution.py:45
  10.4 266.0 %all-gather.6.cloned.1.call-start = ((), (), s32[]{:S(2)}) async-start(), calls=%async_computation.1 | async-start | bytes 9437184 | tf_op jit(solution)/shard_map/all_gather | solution.py:83
  10.5 15.0 %collective-permute-start = (bf16[256,1024]{1,0:T(8,128)(2,1)S(1)}, bf16[256,1024]{1,0:T(8,128)(2,1)}, u32[]{:S(2)}, u32[]{:S(2)}) collective-permute-start(bf16[256,1024]{1,0:T(8,128)(2,1)S(1)} %copy-done.2), channel_id=1, source_target_pairs={{0,1},{1,2},{2,3},{3,0},{4,5},{5,6},{6,7},{7,4},{8,9},{9,10},{10,1... | collective-permute-start | bytes 1572872 | tf_op jit(solution)/shard_map/ppermute | solution.py:23
  12.0 24.7 %collective-permute-start.1 = (bf16[256,1024]{1,0:T(8,128)(2,1)S(1)}, bf16[256,1024]{1,0:T(8,128)(2,1)}, u32[]{:S(2)}, u32[]{:S(2)}) collective-permute-start(bf16[256,1024]{1,0:T(8,128)(2,1)S(1)} %copy-done.2), channel_id=1, source_target_pairs={{0,2},{1,3},{2,0},{3,1},{4,6},{5,7},{6,4},{7,5},{8,10},{9,11},{10,... | collective-permute-start | bytes 1572872 | tf_op jit(solution)/shard_map/ppermute | solution.py:23
  12.5 25.3 %collective-permute-start.2 = (bf16[256,1024]{1,0:T(8,128)(2,1)S(1)}, bf16[256,1024]{1,0:T(8,128)(2,1)S(1)}, u32[]{:S(2)}, u32[]{:S(2)}) collective-permute-start(bf16[256,1024]{1,0:T(8,128)(2,1)S(1)} %copy-done.2), channel_id=1, source_target_pairs={{0,3},{1,0},{2,1},{3,2},{4,7},{5,4},{6,5},{7,6},{8,11},{9,8},{10,9... | collective-permute-start | bytes 1572872 | tf_op jit(solution)/shard_map/ppermute | solution.py:23
  14.4 23.8 %copy-start.4 = (bf16[4096,1024]{1,0:T(8,128)(2,1)S(1)}, bf16[4096,1024]{1,0:T(8,128)(2,1)}, u32[]{:S(2)}) copy-start(bf16[4096,1024]{1,0:T(8,128)(2,1)} %param.13) | copy-start | bytes 25165828
  45.0 13.5 %collective-permute-start.3 = (f32[512,4096]{1,0:T(8,128)}, f32[512,4096]{1,0:T(8,128)}, u32[]{:S(2)}, u32[]{:S(2)}) collective-permute-start(f32[512,4096]{1,0:T(8,128)} %fusion.19), channel_id=1, source_target_pairs={{0,4},{4,0},{1,5},{5,1},{2,6},{6,2},{3,7},{7,3},{8,12},{12,8},{9,1... | collective-permute-start | bytes 25165832 | tf_op jit(solution)/shard_map/ppermute | solution.py:62
  91.3 100.3 %copy-start = (bf16[128,4096]{1,0:T(8,128)(2,1)S(1)}, bf16[128,4096]{1,0:T(8,128)(2,1)}, u32[]{:S(2)}) copy-start(bf16[128,4096]{1,0:T(8,128)(2,1)} %param.10) | copy-start | bytes 3145732
  96.1 27.3 %collective-permute-start.4 = (bf16[128,4096]{1,0:T(8,128)(2,1)}, bf16[128,4096]{1,0:T(8,128)(2,1)}, u32[]{:S(2)}, u32[]{:S(2)}) collective-permute-start(bf16[128,4096]{1,0:T(8,128)(2,1)} %get-tuple-element.10), channel_id=1, source_target_pairs={{0,8},{8,16},{16,24},{24,0},{1,9},{9,17},{17,25},{25,1},{2,10},{10... | collective-permute-start | bytes 3145736 | tf_op jit(solution)/shard_map/ppermute | solution.py:72
  98.6 90.6 %collective-permute-start.5 = (bf16[128,4096]{1,0:T(8,128)(2,1)}, bf16[128,4096]{1,0:T(8,128)(2,1)}, u32[]{:S(2)}, u32[]{:S(2)}) collective-permute-start(bf16[128,4096]{1,0:T(8,128)(2,1)} %get-tuple-element.12), channel_id=1, source_target_pairs={{0,16},{8,24},{16,0},{24,8},{1,17},{9,25},{17,1},{25,9},{2,18},{10... | collective-permute-start | bytes 3145736 | tf_op jit(solution)/shard_map/ppermute | solution.py:72
  101.5 90.2 %collective-permute-start.6 = (bf16[128,4096]{1,0:T(8,128)(2,1)}, bf16[128,4096]{1,0:T(8,128)(2,1)}, u32[]{:S(2)}, u32[]{:S(2)}) collective-permute-start(bf16[128,4096]{1,0:T(8,128)(2,1)} %get-tuple-element.11), channel_id=1, source_target_pairs={{0,24},{8,0},{16,8},{24,16},{1,25},{9,1},{17,9},{25,17},{2,26},{10... | collective-permute-start | bytes 3145736 | tf_op jit(solution)/shard_map/ppermute | solution.py:72
  197.3 161.9 %all-gather.8.cloned.1.call-start = ((), (), s32[]{:S(2)}) async-start(), calls=%async_computation.2 | async-start | bytes 9437184 | tf_op jit(solution)/shard_map/all_gather | solution.py:84
  198.3 15.0 %collective-permute-start.13 = (bf16[256,1024]{1,0:T(8,128)(2,1)S(1)}, bf16[256,1024]{1,0:T(8,128)(2,1)}, u32[]{:S(2)}, u32[]{:S(2)}) collective-permute-start(bf16[256,1024]{1,0:T(8,128)(2,1)S(1)} %copy-done.3), channel_id=1, source_target_pairs={{0,1},{1,2},{2,3},{3,0},{4,5},{5,6},{6,7},{7,4},{8,9},{9,10},{10,1... | collective-permute-start | bytes 1572872 | tf_op jit(solution)/shard_map/ppermute | solution.py:23
  199.8 24.3 %collective-permute-start.14 = (bf16[256,1024]{1,0:T(8,128)(2,1)S(1)}, bf16[256,1024]{1,0:T(8,128)(2,1)}, u32[]{:S(2)}, u32[]{:S(2)}) collective-permute-start(bf16[256,1024]{1,0:T(8,128)(2,1)S(1)} %copy-done.3), channel_id=1, source_target_pairs={{0,2},{1,3},{2,0},{3,1},{4,6},{5,7},{6,4},{7,5},{8,10},{9,11},{10,... | collective-permute-start | bytes 1572872 | tf_op jit(solution)/shard_map/ppermute | solution.py:23
  200.3 25.7 %collective-permute-start.15 = (bf16[256,1024]{1,0:T(8,128)(2,1)S(1)}, bf16[256,1024]{1,0:T(8,128)(2,1)S(1)}, u32[]{:S(2)}, u32[]{:S(2)}) collective-permute-start(bf16[256,1024]{1,0:T(8,128)(2,1)S(1)} %copy-done.3), channel_id=1, source_target_pairs={{0,3},{1,0},{2,1},{3,2},{4,7},{5,4},{6,5},{7,6},{8,11},{9,8},{10,9... | collective-permute-start | bytes 1572872 | tf_op jit(solution)/shard_map/ppermute | solution.py:23
  292.0 97.2 %collective-permute-start.7 = (f32[256,1024]{1,0:T(8,128)}, f32[256,1024]{1,0:T(8,128)S(1)}, u32[]{:S(2)}, u32[]{:S(2)}) collective-permute-start(f32[256,1024]{1,0:T(8,128)} %get-tuple-element.13), channel_id=1, source_target_pairs={{0,1},{1,2},{2,3},{3,0},{4,5},{5,6},{6,7},{7,4},{8,9},{9,10},{10,1... | collective-permute-start | bytes 3145736 | tf_op jit(solution)/shard_map/ppermute | solution.py:35
  293.5 110.7 %collective-permute-start.8 = (f32[256,1024]{1,0:T(8,128)}, f32[256,1024]{1,0:T(8,128)S(1)}, u32[]{:S(2)}, u32[]{:S(2)}) collective-permute-start(f32[256,1024]{1,0:T(8,128)} %get-tuple-element.15), channel_id=1, source_target_pairs={{0,2},{1,3},{2,0},{3,1},{4,6},{5,7},{6,4},{7,5},{8,10},{9,11},{10,... | collective-permute-start | bytes 3145736 | tf_op jit(solution)/shard_map/ppermute | solution.py:35
  293.9 110.3 %collective-permute-start.9 = (f32[256,1024]{1,0:T(8,128)}, f32[256,1024]{1,0:T(8,128)S(1)}, u32[]{:S(2)}, u32[]{:S(2)}) collective-permute-start(f32[256,1024]{1,0:T(8,128)} %get-tuple-element.14), channel_id=1, source_target_pairs={{0,3},{1,0},{2,1},{3,2},{4,7},{5,4},{6,5},{7,6},{8,11},{9,8},{10,9... | collective-permute-start | bytes 3145736 | tf_op jit(solution)/shard_map/ppermute | solution.py:35
  372.3 31.9 %collective-permute-start.10 = (f32[256,1024]{1,0:T(8,128)S(1)}, f32[256,1024]{1,0:T(8,128)S(1)}, u32[]{:S(2)}, u32[]{:S(2)}) collective-permute-start(f32[256,1024]{1,0:T(8,128)S(1)} %get-tuple-element.16), channel_id=1, source_target_pairs={{0,1},{1,2},{2,3},{3,0},{4,5},{5,6},{6,7},{7,4},{8,9},{9,10},{10,1... | collective-permute-start | bytes 3145736 | tf_op jit(solution)/shard_map/ppermute | solution.py:35
  373.8 17.6 %slice-start = ((s8[8388608]{0:T(1024)(128)(4,1)}), s8[4194304]{0:T(1024)(128)(4,1)S(1)}, s32[]{:S(2)}) async-start(s8[8388608]{0:T(1024)(128)(4,1)} %bitcast.75), calls=%async_computation.3 | async-start | bytes 8388608
  373.8 17.6 %slice-start.1 = ((s8[8388608]{0:T(1024)(128)(4,1)}), s8[4194304]{0:T(1024)(128)(4,1)S(1)}, s32[]{:S(2)}) async-start(s8[8388608]{0:T(1024)(128)(4,1)} %bitcast.75), calls=%async_computation.4 | async-start | bytes 8388608
  373.8 47.5 %collective-permute-start.11 = (f32[256,1024]{1,0:T(8,128)S(1)}, f32[256,1024]{1,0:T(8,128)S(1)}, u32[]{:S(2)}, u32[]{:S(2)}) collective-permute-start(f32[256,1024]{1,0:T(8,128)S(1)} %get-tuple-element.18), channel_id=1, source_target_pairs={{0,2},{1,3},{2,0},{3,1},{4,6},{5,7},{6,4},{7,5},{8,10},{9,11},{10,... | collective-permute-start | bytes 3145736 | tf_op jit(solution)/shard_map/ppermute | solution.py:35
  389.2 32.1 %collective-permute-start.12 = (f32[256,1024]{1,0:T(8,128)S(1)}, f32[256,1024]{1,0:T(8,128)S(1)}, u32[]{:S(2)}, u32[]{:S(2)}) collective-permute-start(f32[256,1024]{1,0:T(8,128)S(1)} %get-tuple-element.17), channel_id=1, source_target_pairs={{0,3},{1,0},{2,1},{3,2},{4,7},{5,4},{6,5},{7,6},{8,11},{9,8},{10,9... | collective-permute-start | bytes 3145736 | tf_op jit(solution)/shard_map/ppermute | solution.py:35
  (2 other events, 4.0 us)
Sparse Core Ops, SparseCore 0:
  10.6 80.7 all-gather.3
  197.4 78.9 all-gather.5
  278.6 80.5 all-gather.7

commit v3 on v2

--- a/solution.py
+++ b/solution.py
@@ -44,14 +44,15 @@
     hidden_local = (silu_gate * up_float).astype(jnp.bfloat16)
     hidden_act = lax.all_gather(hidden_local, ROW, axis=0, tiled=True)
 
-    grad_full = gather_col(out_grad)
-    act_full = gather_col(activations)
+    width = out_grad.shape[1]
+    both_full = gather_col(jnp.concatenate([out_grad, activations], axis=1))
+    grad_full = both_full[:, :width]
+    act_full = both_full[:, width:]
     tokens_all = act_full.shape[0]
 
     chips = lax.axis_size("z")
     z = lax.axis_index("z")
     core = lax.axis_index("core")
-    width = grad_full.shape[1]
     grad_blocks = grad_full.reshape(chips, 2, -1, width)
     grad_send = lax.dynamic_index_in_dim(grad_blocks, 1 - core, axis=1, keepdims=False)
     grad_keep = lax.dynamic_index_in_dim(grad_blocks, core, axis=1, keepdims=False)
@@ -64,12 +65,18 @@
         grad_keep.reshape(-1, width), down_weight, CONTRACT_LAST,
         preferred_element_type=jnp.float32,
     )
+    (hid_keep,) = lax.optimization_barrier((hid_keep,))
     chip_sum = (hid_keep + hid_recv).reshape(chips, -1, hid_keep.shape[1])
-    chip_sum, hidden_act = lax.optimization_barrier((chip_sum, hidden_act))
     hid_rows = lax.dynamic_index_in_dim(chip_sum, z, axis=0, keepdims=False)
-    for s in range(1, chips):
-        piece = lax.dynamic_index_in_dim(chip_sum, (z + s) % chips, axis=0, keepdims=False)
-        piece = lax.ppermute(piece.astype(jnp.bfloat16), "z", shift_perm(chips, s))
+    pieces = [
+        lax.dynamic_index_in_dim(chip_sum, (z + s) % chips, axis=0, keepdims=False).astype(
+            jnp.bfloat16
+        )
+        for s in range(1, chips)
+    ]
+    pieces, hid_rows, hidden_act = lax.optimization_barrier((pieces, hid_rows, hidden_act))
+    for s, piece in enumerate(pieces, start=1):
+        piece = lax.ppermute(piece, "z", shift_perm(chips, s))
         hid_rows = hid_rows + piece.astype(jnp.float32)
 
     gate_local = (
@@ -81,18 +88,32 @@
         hidden_act, grad_full, CONTRACT_FIRST, preferred_element_type=jnp.float32
     )
     gate_delta = lax.all_gather(gate_local, ROW, axis=0, tiled=True)
-    up_delta = lax.all_gather(up_local, ROW, axis=0, tiled=True)
+    half = up_local.shape[1] // 2
+    up_delta_a = lax.all_gather(up_local[:, :half], ROW, axis=0, tiled=True)
+    up_delta_b = lax.all_gather(up_local[:, half:], ROW, axis=0, tiled=True)
     acc_gate = lax.dot_general(
         act_full, gate_delta, CONTRACT_FIRST, preferred_element_type=jnp.float32
     )
-    input_gate = reduce_scatter_col(
-        lax.dot_general(gate_delta, gate_weight, CONTRACT_LAST, preferred_element_type=jnp.float32)
+    input_part = lax.dot_general(
+        gate_delta, gate_weight, CONTRACT_LAST, preferred_element_type=jnp.float32
     )
-    acc_up = lax.dot_general(act_full, up_delta, CONTRACT_FIRST, preferred_element_type=jnp.float32)
-    input_up = reduce_scatter_col(
-        lax.dot_general(up_delta, up_weight, CONTRACT_LAST, preferred_element_type=jnp.float32)
+    input_part = input_part + lax.dot_general(
+        up_delta_a, up_weight[:, :half], CONTRACT_LAST, preferred_element_type=jnp.float32
     )
-    input_rows = (input_gate + input_up).astype(jnp.bfloat16)
+    input_part = reduce_scatter_col(input_part)
+    acc_up_a = lax.dot_general(
+        act_full, up_delta_a, CONTRACT_FIRST, preferred_element_type=jnp.float32
+    )
+    acc_up_b = lax.dot_general(
+        act_full, up_delta_b, CONTRACT_FIRST, preferred_element_type=jnp.float32
+    )
+    acc_up = jnp.concatenate([acc_up_a, acc_up_b], axis=1)
+    input_rest = reduce_scatter_col(
+        lax.dot_general(
+            up_delta_b, up_weight[:, half:], CONTRACT_LAST, preferred_element_type=jnp.float32
+        )
+    )
+    input_rows = (input_part + input_rest).astype(jnp.bfloat16)
     factor = float(tokens_all) ** (-0.5)
     return (
         input_rows,

time: 435 us -> 454 us (1.044)
  other arithmetic: 11.6 us -> 25.8 us
    all_gather x1, waiting for transfers between devices: 35 us -> 61.3 us  [body(): gate_delta = lax.all_gather(gate_local, ROW, axis=0, tiled=True)]
    all_gather x1, waiting for transfers between devices: 21.3 us -> 0.01 us  [body(): hidden_act = lax.all_gather(hidden_local, ROW, axis=0, tiled=True)]
    ppermute x6, waiting for transfers between devices: 17.1 us -> 29.7 us  [reduce_scatter_col(): total = total + lax.ppermute(piece, 'col', shift_perm(n, s))]
    add x0 -> x1, other arithmetic: none -> 11.4 us  [body(): chip_sum = (hid_keep + hid_recv).reshape(chips, -1, hid_keep.shape[1])]
    ppermute x1, waiting for transfers between devices: 13.5 us -> 3.34 us  [body(): hid_recv = lax.ppermute(hid_send, 'core', [(0, 1), (1, 0)])]
    all_gather x1 -> x2, waiting for transfers between devices: 63.7 us -> 54.5 us  [the longest x1 29.7 us: body(): up_delta_b = lax.all_gather(up_local[:, half:], ROW, axis=0, tiled=True)]
    unnamed x14 -> x29, local copies, waits for them, and re-layouts: 1.41 us -> 7.68 us
    dynamic_update_slice x6 -> x3, local copies, waits for them, and re-layouts: 6.87 us -> 1.55 us  [gather_col(): lax.dynamic_update_slice_in_dim(full, part, (c - s) % n * rows, axis=0)]
  transfers between devices with their start and end apart: 19 -> 17, of which waited for: 12 -> 12; matrix products, arithmetic and copies ran while one was open for 23% -> 26% of each run, Pallas kernels for 0% -> 0%
where the time goes in v3:
time: 454 us; the launch traced here: 448 us
  waiting for transfers between devices  281 us (62%)
  matrix products  89 us (20%)
  other arithmetic  25.8 us (6%)
  local copies, waits for them, and re-layouts  20 us (4%)
  starting transfers between devices  18.3 us (4%)
  between operations  14.1 us (3%)
    ppermute x3, waiting for transfers between devices, body(): piece = lax.ppermute(piece, 'z', shift_perm(chips, s))  87.9 us
    all_gather x1, waiting for transfers between devices, body(): gate_delta = lax.all_gather(gate_local, ROW, axis=0, tiled=True)  61.3 us
    ppermute x3, waiting for transfers between devices, gather_col(): part = lax.ppermute(block, 'col', shift_perm(n, s))  43.1 us
    ppermute x6, waiting for transfers between devices, reduce_scatter_col(): total = total + lax.ppermute(piece, 'col', shift_perm(n, s))  29.7 us
    all_gather x1, waiting for transfers between devices, body(): up_delta_b = lax.all_gather(up_local[:, half:], ROW, axis=0, tiled=True)  29.7 us
    all_gather x1, waiting for transfers between devices, body(): up_delta_a = lax.all_gather(up_local[:, :half], ROW, axis=0, tiled=True)  24.8 us
    dot_general x1, matrix products, body(): lax.dot_general(hidden_act, grad_full, CONTRACT_FIRST, preferred_element_...  14.9 us
    dot_general x1, matrix products, body(): lax.dot_general(act_full, gate_delta, CONTRACT_FIRST, preferred_element_t...  14.6 us
  transfers between devices with their start and end apart: 17, of which 12 were waited for; matrix products, arithmetic and copies ran while one was open for 26% of the time, Pallas kernels for 0%

profile of v3, /device:TPU:10, one launch (start us, length us, event | category | flops | bytes accessed | tf_op | source)
XLA Modules:
  0.0 448.0 jit_solution(14274979775090545437)
XLA Ops:
  14.9 21.9 %collective-permute-done = bf16[256,2048]{1,0:T(8,128)(2,1)} collective-permute-done((bf16[256,2048]{1,0:T(8,128)(2,1)S(1)}, bf16[256,2048]{1,0:T(8,128)(2,1)}, u32[]{:S(2)}, u32[]{:S(2)}) %collective-permute-start) | collective-permute-done | bytes 1048608 | tf_op jit(solution)/shard_map/ppermute | solution.py:23
  38.2 21.1 %collective-permute-done.1 = bf16[256,2048]{1,0:T(8,128)(2,1)S(1)} collective-permute-done((bf16[256,2048]{1,0:T(8,128)(2,1)S(1)}, bf16[256,2048]{1,0:T(8,128)(2,1)S(1)}, u32[]{:S(2)}, u32[]{:S(2)}) %collective-permute-start.1) | collective-permute-done | bytes 1048608 | tf_op jit(solution)/shard_map/ppermute | solution.py:23
  63.4 6.8 %fusion.30 = f32[512,4096]{1,0:T(8,128)} fusion(bf16[512,1024]{1,0:T(8,128)(2,1)S(1)} %bitcast.64, bf16[4096,1024]{1,0:T(8,128)(2,1)S(1)} %bitcast.66), kind=kOutput, calls=%fused_computation.61 | convolution fusion | flops 4294967296 | bytes 17825792 | tf_op jit(solution)/shard_map/dot_general | solution.py:59
  70.1 10.2 %fusion.29 = f32[512,4096]{1,0:T(8,128)} fusion(bf16[512,1024]{1,0:T(8,128)(2,1)S(1)} %bitcast.63, bf16[4096,1024]{1,0:T(8,128)(2,1)} %param.13), kind=kOutput, calls=%fused_computation.60 | convolution fusion | flops 4294967296 | bytes 17825792 | tf_op jit(solution)/shard_map/dot_general | solution.py:64
  80.3 3.3 collective-permute-done.3
  83.6 11.4 %add.156 = f32[512,4096]{1,0:T(8,128)} add(f32[512,4096]{1,0:T(8,128)} %fusion.29, f32[512,4096]{1,0:T(8,128)} %collective-permute-done.3) | non-fusion elementwise | flops 2097152 | bytes 25165824 | tf_op jit(solution)/shard_map/add | solution.py:69
  96.8 4.7 %fusion.20 = (bf16[128,4096]{1,0:T(8,128)(2,1)}, bf16[128,4096]{1,0:T(8,128)(2,1)}, bf16[128,4096]{1,0:T(8,128)(2,1)}) fusion(f32[4,128,4096]{2,1,0:T(8,128)} %bitcast.57, s32[]{:T(128)S(6)} %select_n.108, s32[]{:T(128)S(6)} %select_n.106, s32[]{:T(128)S(6)} %select_n.104), kind=kLoop, calls=%fused_computation.35 | loop fusion | bytes 6291468 | tf_op jit(solution)/shard_map/convert_element_type | solution.py:72
  107.0 20.9 %collective-permute-done.6 = bf16[128,4096]{1,0:T(8,128)(2,1)S(1)} collective-permute-done((bf16[128,4096]{1,0:T(8,128)(2,1)}, bf16[128,4096]{1,0:T(8,128)(2,1)S(1)}, u32[]{:S(2)}, u32[]{:S(2)}) %collective-permute-start.6) | collective-permute-done | bytes 1048608 | tf_op jit(solution)/shard_map/ppermute | solution.py:79
  127.9 45.2 %collective-permute-done.5 = bf16[128,4096]{1,0:T(8,128)(2,1)S(1)} collective-permute-done((bf16[128,4096]{1,0:T(8,128)(2,1)}, bf16[128,4096]{1,0:T(8,128)(2,1)S(1)}, u32[]{:S(2)}, u32[]{:S(2)}) %collective-permute-start.5) | collective-permute-done | bytes 1048608 | tf_op jit(solution)/shard_map/ppermute | solution.py:79
  173.2 21.8 %collective-permute-done.4 = bf16[128,4096]{1,0:T(8,128)(2,1)S(1)} collective-permute-done((bf16[128,4096]{1,0:T(8,128)(2,1)}, bf16[128,4096]{1,0:T(8,128)(2,1)S(1)}, u32[]{:S(2)}, u32[]{:S(2)}) %collective-permute-start.4) | collective-permute-done | bytes 1048608 | tf_op jit(solution)/shard_map/ppermute | solution.py:79
  195.0 3.7 fusion.8
  201.1 14.9 %multiply_convert_fusion = bf16[4096,1024]{1,0:T(8,128)(2,1)} fusion(bf16[1024,4096]{1,0:T(8,128)(2,1)} %all-gather.5.cloned.1.call-done, bf16[1024,2048]{1,0:T(8,128)(2,1)} %copy-done), kind=kOutput, calls=%fused_computation.2 | convolution fusion | flops 8598323200 | bytes 18874368 | tf_op jit(solution)/shard_map/dot_general | solution.py:87
  216.0 29.7 %all-gather.11.cloned.1.call-done = bf16[1024,2048]{1,0:T(8,128)(2,1)} async-done(((bf16[128,2048]{1,0:T(8,128)(2,1)}), bf16[1024,2048]{1,0:T(8,128)(2,1)}) %all-gather.11.cloned.1.call-update) | async-done | bytes 4194320 | tf_op jit(solution)/shard_map/all_gather | solution.py:93
  245.7 8.0 %fusion.1 = f32[1024,1024]{1,0:T(8,128)S(1)} fusion(bf16[1024,2048]{1,0:T(8,128)(2,1)} %all-gather.11.cloned.1.call-done, bf16[1024,4096]{1,0:T(8,128)(2,1)} %param.12), kind=kOutput, calls=%fused_computation.4 | convolution fusion | flops 4294967296 | bytes 12582912 | tf_op jit(solution)/shard_map/dot_general | solution.py:112
  262.1 6.8 %fusion.13 = f32[1024,2048]{1,0:T(8,128)} fusion(bf16[1024,2048]{1,0:T(8,128)(2,1)S(1)} %copy-done.8, bf16[1024,2048]{1,0:T(8,128)(2,1)S(1)} %copy-done.1), kind=kOutput, calls=%fused_computation.28 | convolution fusion | flops 4294967296 | bytes 14680064 | tf_op jit(solution)/shard_map/dot_general | solution.py:107
  268.9 24.8 %all-gather.9.cloned.1.call-done = bf16[1024,2048]{1,0:T(8,128)(2,1)} async-done(((bf16[128,2048]{1,0:T(8,128)(2,1)}), bf16[1024,2048]{1,0:T(8,128)(2,1)}) %all-gather.9.cloned.1.call-update) | async-done | bytes 4194320 | tf_op jit(solution)/shard_map/all_gather | solution.py:92
  293.7 7.3 %fusion.15 = f32[1024,2048]{1,0:T(8,128)S(1)} fusion(bf16[1024,2048]{1,0:T(8,128)(2,1)} %all-gather.9.cloned.1.call-done, bf16[1024,2048]{1,0:T(8,128)(2,1)} %copy-done), kind=kOutput, calls=%fused_computation.30 | convolution fusion | flops 4294967296 | bytes 14680064 | tf_op jit(solution)/shard_map/dot_general | solution.py:104
  301.0 4.7 %fusion = bf16[1024,4096]{1,0:T(8,128)(2,1)} fusion(f32[1024,2048]{1,0:T(8,128)S(1)} %copy-done.3, f32[1024,2048]{1,0:T(8,128)S(1)} %fusion.15), kind=kLoop, calls=%fused_computation.1 | loop fusion | flops 12582912 | bytes 25165824 | tf_op jit(solution)/shard_map/convert_element_type | solution.py:121
  307.7 6.1 %fusion.3 = f32[1024,1024]{1,0:T(8,128)} fusion(bf16[1024,2048]{1,0:T(8,128)(2,1)S(1)} %copy-done.9, bf16[1024,4096]{1,0:T(8,128)(2,1)S(1)} %bitcast.68), kind=kOutput, calls=%fused_computation.6 | convolution fusion | flops 4294967296 | bytes 12582912 | tf_op jit(solution)/shard_map/dot_general | solution.py:100
  313.8 61.3 %all-gather.7.cloned.1.call-done = bf16[1024,4096]{1,0:T(8,128)(2,1)} async-done(((bf16[128,4096]{1,0:T(8,128)(2,1)}), bf16[1024,4096]{1,0:T(8,128)(2,1)}) %all-gather.7.cloned.1.call-update) | async-done | bytes 8388624 | tf_op jit(solution)/shard_map/all_gather | solution.py:90
  375.1 14.4 %convolution_add_fusion = f32[1024,1024]{1,0:T(8,128)S(1)} fusion(f32[1024,1024]{1,0:T(8,128)} %fusion.3, bf16[1024,4096]{1,0:T(8,128)(2,1)} %all-gather.7.cloned.1.call-done, bf16[1024,4096]{1,0:T(8,128)(2,1)} %param.11), kind=kOutput, calls=%fused_computation.27 | convolution fusion | flops 8590983168 | bytes 25165824 | tf_op jit(solution)/shard_map/dot_general | solution.py:97
  394.4 14.6 %multiply_convert_fusion.1 = bf16[1024,4096]{1,0:T(8,128)(2,1)} fusion(bf16[1024,4096]{1,0:T(8,128)(2,1)} %all-gather.7.cloned.1.call-done, bf16[1024,2048]{1,0:T(8,128)(2,1)S(1)} %copy-done.2), kind=kOutput, calls=%fused_computation.3 | convolution fusion | flops 8598323200 | bytes 18874368 | tf_op jit(solution)/shard_map/dot_general | solution.py:94
  409.0 7.9 %collective-permute-done.9 = f32[256,1024]{1,0:T(8,128)S(1)} collective-permute-done((f32[256,1024]{1,0:T(8,128)S(1)}, f32[256,1024]{1,0:T(8,128)S(1)}, u32[]{:S(2)}, u32[]{:S(2)}) %collective-permute-start.9) | collective-permute-done | bytes 1048608 | tf_op jit(solution)/shard_map/ppermute | solution.py:35
  416.9 20.9 %collective-permute-done.8 = f32[256,1024]{1,0:T(8,128)S(1)} collective-permute-done((f32[256,1024]{1,0:T(8,128)S(1)}, f32[256,1024]{1,0:T(8,128)S(1)}, u32[]{:S(2)}, u32[]{:S(2)}) %collective-permute-start.8) | collective-permute-done | bytes 1048608 | tf_op jit(solution)/shard_map/ppermute | solution.py:35
  (72 shorter events, 41.5 us)
Async XLA Ops:
  7.2 94.4 %all-gather.5.cloned.1.call-start = ((), (), s32[]{:S(2)}) async-start(), calls=%async_computation | async-start | bytes 9437184 | tf_op jit(solution)/shard_map/all_gather | solution.py:45
  10.5 235.2 %all-gather.11.cloned.1.call-start = ((), (), s32[]{:S(2)}) async-start(), calls=%async_computation.3 | async-start | bytes 4718592 | tf_op jit(solution)/shard_map/all_gather | solution.py:93
  10.7 26.2 %collective-permute-start = (bf16[256,2048]{1,0:T(8,128)(2,1)S(1)}, bf16[256,2048]{1,0:T(8,128)(2,1)}, u32[]{:S(2)}, u32[]{:S(2)}) collective-permute-start(bf16[256,2048]{1,0:T(8,128)(2,1)S(1)} %constant_dynamic-update-slice_fusion), channel_id=1, source_target_pairs={{0,1},{1,2},{2,3},{3,0},{4,5},{5,6},{6,7},{7,4},{8,9},{9,10},{10,1... | collective-permute-start | bytes 3145736 | tf_op jit(solution)/shard_map/ppermute | solution.py:23
  12.2 47.1 %collective-permute-start.1 = (bf16[256,2048]{1,0:T(8,128)(2,1)S(1)}, bf16[256,2048]{1,0:T(8,128)(2,1)S(1)}, u32[]{:S(2)}, u32[]{:S(2)}) collective-permute-start(bf16[256,2048]{1,0:T(8,128)(2,1)S(1)} %constant_dynamic-update-slice_fusion), channel_id=1, source_target_pairs={{0,2},{1,3},{2,0},{3,1},{4,6},{5,7},{6,4},{7,5},{8,10},{9,11},{10,... | collective-permute-start | bytes 3145736 | tf_op jit(solution)/shard_map/ppermute | solution.py:23
  12.7 46.7 %collective-permute-start.2 = (bf16[256,2048]{1,0:T(8,128)(2,1)S(1)}, bf16[256,2048]{1,0:T(8,128)(2,1)S(1)}, u32[]{:S(2)}, u32[]{:S(2)}) collective-permute-start(bf16[256,2048]{1,0:T(8,128)(2,1)S(1)} %constant_dynamic-update-slice_fusion), channel_id=1, source_target_pairs={{0,3},{1,0},{2,1},{3,2},{4,7},{5,4},{6,5},{7,6},{8,11},{9,8},{10,9... | collective-permute-start | bytes 3145736 | tf_op jit(solution)/shard_map/ppermute | solution.py:23
  14.8 46.9 %slice-start = ((s8[8388608]{0:T(1024)(128)(4,1)}), s8[4194304]{0:T(1024)(128)(4,1)S(1)}, s32[]{:S(2)}) async-start(s8[8388608]{0:T(1024)(128)(4,1)} %bitcast.65), calls=%async_computation.4 | async-start | bytes 8388608
  70.1 13.5 %collective-permute-start.3 = (f32[512,4096]{1,0:T(8,128)}, f32[512,4096]{1,0:T(8,128)}, u32[]{:S(2)}, u32[]{:S(2)}) collective-permute-start(f32[512,4096]{1,0:T(8,128)} %fusion.30), channel_id=1, source_target_pairs={{0,4},{4,0},{1,5},{5,1},{2,6},{6,2},{3,7},{7,3},{8,12},{12,8},{9,1... | collective-permute-start | bytes 25165832 | tf_op jit(solution)/shard_map/ppermute | solution.py:63
  96.8 98.2 %copy-start.4 = (bf16[128,4096]{1,0:T(8,128)(2,1)S(1)}, bf16[128,4096]{1,0:T(8,128)(2,1)}, u32[]{:S(2)}) copy-start(bf16[128,4096]{1,0:T(8,128)(2,1)} %param.10) | copy-start | bytes 3145732
  101.5 26.4 %collective-permute-start.6 = (bf16[128,4096]{1,0:T(8,128)(2,1)}, bf16[128,4096]{1,0:T(8,128)(2,1)S(1)}, u32[]{:S(2)}, u32[]{:S(2)}) collective-permute-start(bf16[128,4096]{1,0:T(8,128)(2,1)} %get-tuple-element.12), channel_id=1, source_target_pairs={{0,24},{8,0},{16,8},{24,16},{1,25},{9,1},{17,9},{25,17},{2,26},{10... | collective-permute-start | bytes 3145736 | tf_op jit(solution)/shard_map/ppermute | solution.py:79
  102.5 70.7 %collective-permute-start.5 = (bf16[128,4096]{1,0:T(8,128)(2,1)}, bf16[128,4096]{1,0:T(8,128)(2,1)S(1)}, u32[]{:S(2)}, u32[]{:S(2)}) collective-permute-start(bf16[128,4096]{1,0:T(8,128)(2,1)} %get-tuple-element.11), channel_id=1, source_target_pairs={{0,16},{8,24},{16,0},{24,8},{1,17},{9,25},{17,1},{25,9},{2,18},{10... | collective-permute-start | bytes 3145736 | tf_op jit(solution)/shard_map/ppermute | solution.py:79
  104.5 90.4 %collective-permute-start.4 = (bf16[128,4096]{1,0:T(8,128)(2,1)}, bf16[128,4096]{1,0:T(8,128)(2,1)S(1)}, u32[]{:S(2)}, u32[]{:S(2)}) collective-permute-start(bf16[128,4096]{1,0:T(8,128)(2,1)} %get-tuple-element.10), channel_id=1, source_target_pairs={{0,8},{8,16},{16,24},{24,0},{1,9},{9,17},{17,25},{25,1},{2,10},{10... | collective-permute-start | bytes 3145736 | tf_op jit(solution)/shard_map/ppermute | solution.py:79
  199.7 94.0 %all-gather.9.cloned.1.call-start = ((), (), s32[]{:S(2)}) async-start(), calls=%async_computation.2 | async-start | bytes 4718592 | tf_op jit(solution)/shard_map/all_gather | solution.py:92
  200.5 174.6 %all-gather.7.cloned.1.call-start = ((), (), s32[]{:S(2)}) async-start(), calls=%async_computation.1 | async-start | bytes 9437184 | tf_op jit(solution)/shard_map/all_gather | solution.py:90
  245.7 16.4 %copy-start.8 = (bf16[1024,2048]{1,0:T(8,128)(2,1)S(1)}, bf16[1024,2048]{1,0:T(8,128)(2,1)}, u32[]{:S(2)}) copy-start(bf16[1024,2048]{1,0:T(8,128)(2,1)} %all-gather.11.cloned.1.call-done) | copy-start | bytes 12582916
  253.7 8.4 %copy-start.1 = (bf16[1024,2048]{1,0:T(8,128)(2,1)S(1)}, bf16[1024,2048]{1,0:T(8,128)(2,1)}, u32[]{:S(2)}) copy-start(bf16[1024,2048]{1,0:T(8,128)(2,1)} %copy-done) | copy-start | bytes 12582916
  257.7 134.3 %collective-permute-start.12 = (f32[256,1024]{1,0:T(8,128)}, f32[256,1024]{1,0:T(8,128)S(1)}, u32[]{:S(2)}, u32[]{:S(2)}) collective-permute-start(f32[256,1024]{1,0:T(8,128)} %get-tuple-element.23), channel_id=1, source_target_pairs={{0,3},{1,0},{2,1},{3,2},{4,7},{5,4},{6,5},{7,6},{8,11},{9,8},{10,9... | collective-permute-start | bytes 3145736 | tf_op jit(solution)/shard_map/ppermute | solution.py:35
  258.2 150.7 %collective-permute-start.11 = (f32[256,1024]{1,0:T(8,128)}, f32[256,1024]{1,0:T(8,128)S(1)}, u32[]{:S(2)}, u32[]{:S(2)}) collective-permute-start(f32[256,1024]{1,0:T(8,128)} %get-tuple-element.24), channel_id=1, source_target_pairs={{0,2},{1,3},{2,0},{3,1},{4,6},{5,7},{6,4},{7,5},{8,10},{9,11},{10,... | collective-permute-start | bytes 3145736 | tf_op jit(solution)/shard_map/ppermute | solution.py:35
  259.7 149.3 %collective-permute-start.10 = (f32[256,1024]{1,0:T(8,128)}, f32[256,1024]{1,0:T(8,128)S(1)}, u32[]{:S(2)}, u32[]{:S(2)}) collective-permute-start(f32[256,1024]{1,0:T(8,128)} %get-tuple-element.22), channel_id=1, source_target_pairs={{0,1},{1,2},{2,3},{3,0},{4,5},{5,6},{6,7},{7,4},{8,9},{9,10},{10,1... | collective-permute-start | bytes 3145736 | tf_op jit(solution)/shard_map/ppermute | solution.py:35
  293.7 7.3 %copy-start.3 = (f32[1024,2048]{1,0:T(8,128)S(1)}, f32[1024,2048]{1,0:T(8,128)}, u32[]{:S(2)}) copy-start(f32[1024,2048]{1,0:T(8,128)} %fusion.13) | copy-start | bytes 25165828
  293.7 12.0 %slice-start.2 = ((s8[8388608]{0:T(1024)(128)(4,1)}), s8[4194304]{0:T(1024)(128)(4,1)S(1)}, s32[]{:S(2)}) async-start(s8[8388608]{0:T(1024)(128)(4,1)} %bitcast.67), calls=%async_computation.6 | async-start | bytes 8388608
  301.0 6.7 %copy-start.9 = (bf16[1024,2048]{1,0:T(8,128)(2,1)S(1)}, bf16[1024,2048]{1,0:T(8,128)(2,1)}, u32[]{:S(2)}) copy-start(bf16[1024,2048]{1,0:T(8,128)(2,1)} %all-gather.9.cloned.1.call-done) | copy-start | bytes 12582916
  389.9 27.0 %collective-permute-start.9 = (f32[256,1024]{1,0:T(8,128)S(1)}, f32[256,1024]{1,0:T(8,128)S(1)}, u32[]{:S(2)}, u32[]{:S(2)}) collective-permute-start(f32[256,1024]{1,0:T(8,128)S(1)} %get-tuple-element.20), channel_id=1, source_target_pairs={{0,3},{1,0},{2,1},{3,2},{4,7},{5,4},{6,5},{7,6},{8,11},{9,8},{10,9... | collective-permute-start | bytes 3145736 | tf_op jit(solution)/shard_map/ppermute | solution.py:35
  390.3 47.5 %collective-permute-start.8 = (f32[256,1024]{1,0:T(8,128)S(1)}, f32[256,1024]{1,0:T(8,128)S(1)}, u32[]{:S(2)}, u32[]{:S(2)}) collective-permute-start(f32[256,1024]{1,0:T(8,128)S(1)} %get-tuple-element.21), channel_id=1, source_target_pairs={{0,2},{1,3},{2,0},{3,1},{4,6},{5,7},{6,4},{7,5},{8,10},{9,11},{10,... | collective-permute-start | bytes 3145736 | tf_op jit(solution)/shard_map/ppermute | solution.py:35
  392.0 46.7 %collective-permute-start.7 = (f32[256,1024]{1,0:T(8,128)S(1)}, f32[256,1024]{1,0:T(8,128)S(1)}, u32[]{:S(2)}, u32[]{:S(2)}) collective-permute-start(f32[256,1024]{1,0:T(8,128)S(1)} %get-tuple-element.19), channel_id=1, source_target_pairs={{0,1},{1,2},{2,3},{3,0},{4,5},{5,6},{6,7},{7,4},{8,9},{9,10},{10,1... | collective-permute-start | bytes 3145736 | tf_op jit(solution)/shard_map/ppermute | solution.py:35
  (7 other events, 24.5 us)
Sparse Core Ops, SparseCore 0:
  10.6 80.7 all-gather.4
  199.8 45.7 all-gather.10
  247.8 45.8 all-gather.8
  295.2 79.8 all-gather.6

commit v4 on v2

--- a/solution.py
+++ b/solution.py
@@ -25,6 +25,24 @@
     return full
 
 
+def gather_row(block):
+    chips = lax.axis_size("z")
+    z = lax.axis_index("z")
+    core = lax.axis_index("core")
+    rows = block.shape[0]
+    mine = jnp.zeros((chips * rows,) + block.shape[1:], block.dtype)
+    mine = lax.dynamic_update_slice_in_dim(mine, block, z * rows, axis=0)
+    for s in range(1, chips):
+        part = lax.ppermute(block, "z", shift_perm(chips, s))
+        mine = lax.dynamic_update_slice_in_dim(mine, part, ((z - s) % chips) * rows, axis=0)
+    other = lax.ppermute(mine, "core", [(0, 1), (1, 0)])
+    pair = jnp.stack([mine, other]).reshape((2, chips, rows) + block.shape[1:])
+    first = jnp.where(core == 0, pair[0], pair[1])
+    second = jnp.where(core == 0, pair[1], pair[0])
+    full = jnp.stack([first, second], axis=1)
+    return full.reshape((2 * chips * rows,) + block.shape[1:])
+
+
 def reduce_scatter_col(partial):
     n = lax.axis_size("col")
     c = lax.axis_index("col")
@@ -45,6 +63,7 @@
     hidden_act = lax.all_gather(hidden_local, ROW, axis=0, tiled=True)
 
     grad_full = gather_col(out_grad)
+    activations, grad_full = lax.optimization_barrier((activations, grad_full))
     act_full = gather_col(activations)
     tokens_all = act_full.shape[0]
 
@@ -65,23 +84,24 @@
         preferred_element_type=jnp.float32,
     )
     chip_sum = (hid_keep + hid_recv).reshape(chips, -1, hid_keep.shape[1])
-    chip_sum, hidden_act = lax.optimization_barrier((chip_sum, hidden_act))
+    chip_sum, hidden_act, act_full = lax.optimization_barrier((chip_sum, hidden_act, act_full))
     hid_rows = lax.dynamic_index_in_dim(chip_sum, z, axis=0, keepdims=False)
     for s in range(1, chips):
         piece = lax.dynamic_index_in_dim(chip_sum, (z + s) % chips, axis=0, keepdims=False)
         piece = lax.ppermute(piece.astype(jnp.bfloat16), "z", shift_perm(chips, s))
         hid_rows = hid_rows + piece.astype(jnp.float32)
 
+    acc_down = lax.dot_general(
+        hidden_act, grad_full, CONTRACT_FIRST, preferred_element_type=jnp.float32
+    )
+    hid_rows, acc_down = lax.optimization_barrier((hid_rows, acc_down))
     gate_local = (
         hid_rows * up_float * sigmoid_gate * (1.0 + gate_float * (1.0 - sigmoid_gate))
     ).astype(jnp.bfloat16)
     up_local = (hid_rows * silu_gate).astype(jnp.bfloat16)
 
-    acc_down = lax.dot_general(
-        hidden_act, grad_full, CONTRACT_FIRST, preferred_element_type=jnp.float32
-    )
     gate_delta = lax.all_gather(gate_local, ROW, axis=0, tiled=True)
-    up_delta = lax.all_gather(up_local, ROW, axis=0, tiled=True)
+    up_delta = gather_row(up_local)
     acc_gate = lax.dot_general(
         act_full, gate_delta, CONTRACT_FIRST, preferred_element_type=jnp.float32
     )

time: 435 us -> 500 us (1.15)
  waiting for transfers between devices: 281 us -> 321 us
  other arithmetic: 11.6 us -> 31.6 us
  local copies, waits for them, and re-layouts: 18.2 us -> 24.9 us
    ppermute x0 -> x4, waiting for transfers between devices: none -> 154 us  [the longest x3 154 us: gather_row(): part = lax.ppermute(block, 'z', shift_perm(chips, s))]
    all_gather x1 -> x0, waiting for transfers between devices: 63.7 us -> none  [body(): up_delta = lax.all_gather(up_local, ROW, axis=0, tiled=True)]
    all_gather x1, waiting for transfers between devices: 35 us -> 0.01 us  [body(): gate_delta = lax.all_gather(gate_local, ROW, axis=0, tiled=True)]
    ppermute x6, waiting for transfers between devices: 17.1 us -> 49.4 us  [reduce_scatter_col(): total = total + lax.ppermute(piece, 'col', shift_perm(n, s))]
    ppermute x3, waiting for transfers between devices: 90.2 us -> 72.7 us  [body(): piece = lax.ppermute(piece.astype(jnp.bfloat16), 'z', shift_perm(chips, s))]
    all_gather x1, waiting for transfers between devices: 21.3 us -> 4.36 us  [body(): hidden_act = lax.all_gather(hidden_local, ROW, axis=0, tiled=True)]
    ppermute x1, waiting for transfers between devices: 13.5 us -> 0.01 us  [body(): hid_recv = lax.ppermute(hid_send, 'core', [(0, 1), (1, 0)])]
    convert_element_type x0 -> x1, other arithmetic: none -> 9.76 us  [body(): (acc_down * factor).astype(jnp.bfloat16)]
  transfers between devices with their start and end apart: 19 -> 22, of which waited for: 12 -> 16; matrix products, arithmetic and copies ran while one was open for 23% -> 25% of each run, Pallas kernels for 0% -> 0%
where the time goes in v4:
time: 500 us
  waiting for transfers between devices  321 us (64%)
  matrix products  84 us (17%)
  other arithmetic  31.6 us (6%)
  local copies, waits for them, and re-layouts  24.9 us (5%)
  starting transfers between devices  24.2 us (5%)
  between operations  14.2 us (3%)
    ppermute x3, waiting for transfers between devices, gather_row(): part = lax.ppermute(block, 'z', shift_perm(chips, s))  154 us
    ppermute x3, waiting for transfers between devices, body(): piece = lax.ppermute(piece.astype(jnp.bfloat16), 'z', shift_perm(chips, s))  72.7 us
    ppermute x6, waiting for transfers between devices, reduce_scatter_col(): total = total + lax.ppermute(piece, 'col', shift_perm(n, s))  49.4 us
    ppermute x6, waiting for transfers between devices, gather_col(): part = lax.ppermute(block, 'col', shift_perm(n, s))  40.2 us
    dot_general x1, matrix products, body(): lax.dot_general(hidden_act, grad_full, CONTRACT_FIRST, preferred_element_...  14.6 us
    dot_general x1, matrix products, body(): lax.dot_general(up_delta, up_weight, CONTRACT_LAST, preferred_element_typ...  12.8 us
    dot_general x1, matrix products, body(): lax.dot_general(gate_delta, gate_weight, CONTRACT_LAST, preferred_element...  12.8 us
    dot_general x1, matrix products, body(): lax.dot_general(act_full, gate_delta, CONTRACT_FIRST, preferred_element_t...  12.8 us
  transfers between devices with their start and end apart: 22, of which 16 were waited for; matrix products, arithmetic and copies ran while one was open for 25% of the time, Pallas kernels for 0%

profile of v4, /device:TPU:10, one launch (start us, length us, event | category | flops | bytes accessed | tf_op | source)
XLA Modules:
  0.0 499.8 jit_solution(17149737959011990441)
XLA Ops:
  14.4 11.0 %collective-permute-done = bf16[256,1024]{1,0:T(8,128)(2,1)} collective-permute-done((bf16[256,1024]{1,0:T(8,128)(2,1)S(1)}, bf16[256,1024]{1,0:T(8,128)(2,1)}, u32[]{:S(2)}, u32[]{:S(2)}) %collective-permute-start) | collective-permute-done | bytes 524320 | tf_op jit(solution)/shard_map/ppermute | solution.py:23
  26.5 10.2 %collective-permute-done.1 = bf16[256,1024]{1,0:T(8,128)(2,1)} collective-permute-done((bf16[256,1024]{1,0:T(8,128)(2,1)S(1)}, bf16[256,1024]{1,0:T(8,128)(2,1)}, u32[]{:S(2)}, u32[]{:S(2)}) %collective-permute-start.1) | collective-permute-done | bytes 524320 | tf_op jit(solution)/shard_map/ppermute | solution.py:23
  38.1 6.8 %fusion.21 = f32[512,4096]{1,0:T(8,128)} fusion(bf16[512,1024]{1,0:T(8,128)(2,1)S(1)} %bitcast.77, bf16[4096,1024]{1,0:T(8,128)(2,1)S(1)} %copy-done.7), kind=kOutput, calls=%fused_computation.60 | convolution fusion | flops 4294967296 | bytes 17825792 | tf_op jit(solution)/shard_map/dot_general | solution.py:77
  50.9 9.1 %collective-permute-done.4 = bf16[256,1024]{1,0:T(8,128)(2,1)} collective-permute-done((bf16[256,1024]{1,0:T(8,128)(2,1)}, bf16[256,1024]{1,0:T(8,128)(2,1)}, u32[]{:S(2)}, u32[]{:S(2)}) %collective-permute-start.4) | collective-permute-done | bytes 524320 | tf_op jit(solution)/shard_map/ppermute | solution.py:23
  61.9 9.9 %collective-permute-done.5 = bf16[256,1024]{1,0:T(8,128)(2,1)} collective-permute-done((bf16[256,1024]{1,0:T(8,128)(2,1)}, bf16[256,1024]{1,0:T(8,128)(2,1)}, u32[]{:S(2)}, u32[]{:S(2)}) %collective-permute-start.5) | collective-permute-done | bytes 524320 | tf_op jit(solution)/shard_map/ppermute | solution.py:23
  75.5 11.5 %convolution_add_fusion = f32[512,4096]{1,0:T(8,128)} fusion(f32[512,4096]{1,0:T(8,128)} %collective-permute-done.3, bf16[512,1024]{1,0:T(8,128)(2,1)S(1)} %bitcast.76, bf16[4096,1024]{1,0:T(8,128)(2,1)} %param.13), kind=kOutput, calls=%fused_computation.6 | convolution fusion | flops 4297064448 | bytes 26214400 | tf_op jit(solution)/shard_map/dot_general | solution.py:82
  87.0 4.4 all-gather.3.cloned.1.call-done
  100.1 14.6 %fusion.22 = f32[4096,1024]{1,0:T(8,128)} fusion(bf16[1024,4096]{1,0:T(8,128)(2,1)} %all-gather.3.cloned.1.call-done, bf16[1024,1024]{1,0:T(8,128)(2,1)S(1)} %constant_dynamic-update-slice_fusion.8), kind=kOutput, calls=%fused_computation.61 | convolution fusion | flops 8589934592 | bytes 27262976 | tf_op jit(solution)/shard_map/dot_general | solution.py:94
  114.7 7.0 %collective-permute-done.7 = bf16[128,4096]{1,0:T(8,128)(2,1)S(1)} collective-permute-done((bf16[128,4096]{1,0:T(8,128)(2,1)S(1)}, bf16[128,4096]{1,0:T(8,128)(2,1)S(1)}, u32[]{:S(2)}, u32[]{:S(2)}) %collective-permute-start.7) | collective-permute-done | bytes 1048608 | tf_op jit(solution)/shard_map/ppermute | solution.py:91
  121.7 24.5 %collective-permute-done.9 = bf16[128,4096]{1,0:T(8,128)(2,1)S(1)} collective-permute-done((bf16[128,4096]{1,0:T(8,128)(2,1)S(1)}, bf16[128,4096]{1,0:T(8,128)(2,1)S(1)}, u32[]{:S(2)}, u32[]{:S(2)}) %collective-permute-start.9) | collective-permute-done | bytes 1048608 | tf_op jit(solution)/shard_map/ppermute | solution.py:91
  146.1 41.3 %collective-permute-done.8 = bf16[128,4096]{1,0:T(8,128)(2,1)S(1)} collective-permute-done((bf16[128,4096]{1,0:T(8,128)(2,1)S(1)}, bf16[128,4096]{1,0:T(8,128)(2,1)S(1)}, u32[]{:S(2)}, u32[]{:S(2)}) %collective-permute-start.8) | collective-permute-done | bytes 1048608 | tf_op jit(solution)/shard_map/ppermute | solution.py:91
  197.3 4.3 collective-permute-start.14
  201.6 81.1 %collective-permute-done.13 = bf16[128,4096]{1,0:T(8,128)(2,1)S(1)} collective-permute-done((bf16[128,4096]{1,0:T(8,128)(2,1)}, bf16[128,4096]{1,0:T(8,128)(2,1)S(1)}, u32[]{:S(2)}, u32[]{:S(2)}) %collective-permute-start.13) | collective-permute-done | bytes 1048608 | tf_op jit(solution)/shard_map/ppermute | solution.py:36
  283.7 70.5 %collective-permute-done.14 = bf16[128,4096]{1,0:T(8,128)(2,1)S(1)} collective-permute-done((bf16[128,4096]{1,0:T(8,128)(2,1)}, bf16[128,4096]{1,0:T(8,128)(2,1)S(1)}, u32[]{:S(2)}, u32[]{:S(2)}) %collective-permute-start.14) | collective-permute-done | bytes 1048608 | tf_op jit(solution)/shard_map/ppermute | solution.py:36
  359.0 9.8 %multiply_convert_fusion = bf16[4096,1024]{1,0:T(8,128)(2,1)} fusion(f32[4096,1024]{1,0:T(8,128)} %fusion.22), kind=kLoop, calls=%fused_computation | loop fusion | flops 8388608 | bytes 25165824 | tf_op jit(solution)/shard_map/convert_element_type | solution.py:121
  368.8 3.9 broadcast_select_fusion.1
  372.6 6.4 %pad_maximum_fusion = bf16[4,2,128,4096]{3,2,1,0:T(8,128)(2,1)} fusion(bf16[4,1,128,4096]{3,2,1,0:T(8,128)(2,1)} %bitcast.68, bf16[4,1,128,4096]{3,2,1,0:T(8,128)(2,1)S(1)} %bitcast.67), kind=kLoop, calls=%fused_computation.3 | loop fusion | flops 4194304 | bytes 16777216 | tf_op jit(solution)/shard_map/stack | solution.py:42
  379.0 12.8 %fusion = f32[4,256,1024]{2,1,0:T(8,128)S(1)} fusion(bf16[4,256,4096]{2,1,0:T(8,128)(2,1)} %bitcast.70, bf16[1024,4096]{1,0:T(8,128)(2,1)} %param.12), kind=kOutput, calls=%fused_computation.4 | convolution fusion | flops 8589934592 | bytes 20971520 | tf_op jit(solution)/shard_map/dot_general | solution.py:113
  399.0 12.8 %multiply_convert_fusion.1 = bf16[1024,4096]{1,0:T(8,128)(2,1)} fusion(bf16[1024,1024]{1,0:T(8,128)(2,1)} %constant_dynamic-update-slice_fusion.4, bf16[1024,4096]{1,0:T(8,128)(2,1)S(1)} %bitcast.71), kind=kOutput, calls=%fused_computation.1 | convolution fusion | flops 8598323200 | bytes 18874368 | tf_op jit(solution)/shard_map/dot_general | solution.py:111
  411.8 12.8 %fusion.23 = f32[1024,1024]{1,0:T(8,128)S(1)} fusion(bf16[1024,4096]{1,0:T(8,128)(2,1)} %all-gather.5.cloned.1.call-done, bf16[1024,4096]{1,0:T(8,128)(2,1)} %param.11), kind=kOutput, calls=%fused_computation.62 | convolution fusion | flops 8589934592 | bytes 20971520 | tf_op jit(solution)/shard_map/dot_general | solution.py:109
  427.9 12.8 %multiply_convert_fusion.2 = bf16[1024,4096]{1,0:T(8,128)(2,1)} fusion(bf16[1024,1024]{1,0:T(8,128)(2,1)} %constant_dynamic-update-slice_fusion.4, bf16[1024,4096]{1,0:T(8,128)(2,1)S(1)} %copy-done.8), kind=kOutput, calls=%fused_computation.2 | convolution fusion | flops 8598323200 | bytes 18874368 | tf_op jit(solution)/shard_map/dot_general | solution.py:105
  440.7 4.4 collective-permute-done.19
  445.6 21.0 %collective-permute-done.10 = f32[256,1024]{1,0:T(8,128)S(1)} collective-permute-done((f32[256,1024]{1,0:T(8,128)S(1)}, f32[256,1024]{1,0:T(8,128)S(1)}, u32[]{:S(2)}, u32[]{:S(2)}) %collective-permute-start.10) | collective-permute-done | bytes 1048608 | tf_op jit(solution)/shard_map/ppermute | solution.py:53
  466.7 23.1 %collective-permute-done.12 = f32[256,1024]{1,0:T(8,128)S(1)} collective-permute-done((f32[256,1024]{1,0:T(8,128)S(1)}, f32[256,1024]{1,0:T(8,128)S(1)}, u32[]{:S(2)}, u32[]{:S(2)}) %collective-permute-start.12) | collective-permute-done | bytes 1048608 | tf_op jit(solution)/shard_map/ppermute | solution.py:53
  (73 shorter events, 60.0 us)
Async XLA Ops:
  7.2 84.2 %all-gather.3.cloned.1.call-start = ((), (), s32[]{:S(2)}) async-start(), calls=%async_computation | async-start | bytes 9437184 | tf_op jit(solution)/shard_map/all_gather | solution.py:63
  10.4 401.3 %all-gather.5.cloned.1.call-start = ((), (), s32[]{:S(2)}) async-start(), calls=%async_computation.1 | async-start | bytes 9437184 | tf_op jit(solution)/shard_map/all_gather | solution.py:103
  10.5 15.0 %collective-permute-start = (bf16[256,1024]{1,0:T(8,128)(2,1)S(1)}, bf16[256,1024]{1,0:T(8,128)(2,1)}, u32[]{:S(2)}, u32[]{:S(2)}) collective-permute-start(bf16[256,1024]{1,0:T(8,128)(2,1)S(1)} %copy-done.6), channel_id=1, source_target_pairs={{0,1},{1,2},{2,3},{3,0},{4,5},{5,6},{6,7},{7,4},{8,9},{9,10},{10,1... | collective-permute-start | bytes 1572872 | tf_op jit(solution)/shard_map/ppermute | solution.py:23
  12.0 24.7 %collective-permute-start.1 = (bf16[256,1024]{1,0:T(8,128)(2,1)S(1)}, bf16[256,1024]{1,0:T(8,128)(2,1)}, u32[]{:S(2)}, u32[]{:S(2)}) collective-permute-start(bf16[256,1024]{1,0:T(8,128)(2,1)S(1)} %copy-done.6), channel_id=1, source_target_pairs={{0,2},{1,3},{2,0},{3,1},{4,6},{5,7},{6,4},{7,5},{8,10},{9,11},{10,... | collective-permute-start | bytes 1572872 | tf_op jit(solution)/shard_map/ppermute | solution.py:23
  12.5 25.3 %collective-permute-start.2 = (bf16[256,1024]{1,0:T(8,128)(2,1)S(1)}, bf16[256,1024]{1,0:T(8,128)(2,1)S(1)}, u32[]{:S(2)}, u32[]{:S(2)}) collective-permute-start(bf16[256,1024]{1,0:T(8,128)(2,1)S(1)} %copy-done.6), channel_id=1, source_target_pairs={{0,3},{1,0},{2,1},{3,2},{4,7},{5,4},{6,5},{7,6},{8,11},{9,8},{10,9... | collective-permute-start | bytes 1572872 | tf_op jit(solution)/shard_map/ppermute | solution.py:23
  44.9 30.5 %collective-permute-start.3 = (f32[512,4096]{1,0:T(8,128)}, f32[512,4096]{1,0:T(8,128)}, u32[]{:S(2)}, u32[]{:S(2)}) collective-permute-start(f32[512,4096]{1,0:T(8,128)} %fusion.21), channel_id=1, source_target_pairs={{0,4},{4,0},{1,5},{5,1},{2,6},{6,2},{3,7},{7,3},{8,12},{12,8},{9,1... | collective-permute-start | bytes 25165832 | tf_op jit(solution)/shard_map/ppermute | solution.py:81
  44.9 15.0 %collective-permute-start.4 = (bf16[256,1024]{1,0:T(8,128)(2,1)}, bf16[256,1024]{1,0:T(8,128)(2,1)}, u32[]{:S(2)}, u32[]{:S(2)}) collective-permute-start(bf16[256,1024]{1,0:T(8,128)(2,1)} %param.7), channel_id=1, source_target_pairs={{0,1},{1,2},{2,3},{3,0},{4,5},{5,6},{6,7},{7,4},{8,9},{9,10},{10,1... | collective-permute-start | bytes 1572872 | tf_op jit(solution)/shard_map/ppermute | solution.py:23
  46.1 25.6 %collective-permute-start.5 = (bf16[256,1024]{1,0:T(8,128)(2,1)}, bf16[256,1024]{1,0:T(8,128)(2,1)}, u32[]{:S(2)}, u32[]{:S(2)}) collective-permute-start(bf16[256,1024]{1,0:T(8,128)(2,1)} %param.7), channel_id=1, source_target_pairs={{0,2},{1,3},{2,0},{3,1},{4,6},{5,7},{6,4},{7,5},{8,10},{9,11},{10,... | collective-permute-start | bytes 1572872 | tf_op jit(solution)/shard_map/ppermute | solution.py:23
  46.6 27.0 %collective-permute-start.6 = (bf16[256,1024]{1,0:T(8,128)(2,1)}, bf16[256,1024]{1,0:T(8,128)(2,1)}, u32[]{:S(2)}, u32[]{:S(2)}) collective-permute-start(bf16[256,1024]{1,0:T(8,128)(2,1)} %param.7), channel_id=1, source_target_pairs={{0,3},{1,0},{2,1},{3,2},{4,7},{5,4},{6,5},{7,6},{8,11},{9,8},{10,9... | collective-permute-start | bytes 1572872 | tf_op jit(solution)/shard_map/ppermute | solution.py:23
  94.6 27.0 %collective-permute-start.7 = (bf16[128,4096]{1,0:T(8,128)(2,1)S(1)}, bf16[128,4096]{1,0:T(8,128)(2,1)S(1)}, u32[]{:S(2)}, u32[]{:S(2)}) collective-permute-start(bf16[128,4096]{1,0:T(8,128)(2,1)S(1)} %get-tuple-element.22), channel_id=1, source_target_pairs={{0,8},{8,16},{16,24},{24,0},{1,9},{9,17},{17,25},{25,1},{2,10},{10... | collective-permute-start | bytes 3145736 | tf_op jit(solution)/shard_map/ppermute | solution.py:91
  97.2 49.0 %collective-permute-start.9 = (bf16[128,4096]{1,0:T(8,128)(2,1)S(1)}, bf16[128,4096]{1,0:T(8,128)(2,1)S(1)}, u32[]{:S(2)}, u32[]{:S(2)}) collective-permute-start(bf16[128,4096]{1,0:T(8,128)(2,1)S(1)} %get-tuple-element.23), channel_id=1, source_target_pairs={{0,24},{8,0},{16,8},{24,16},{1,25},{9,1},{17,9},{25,17},{2,26},{10... | collective-permute-start | bytes 3145736 | tf_op jit(solution)/shard_map/ppermute | solution.py:91
  98.0 89.4 %collective-permute-start.8 = (bf16[128,4096]{1,0:T(8,128)(2,1)S(1)}, bf16[128,4096]{1,0:T(8,128)(2,1)S(1)}, u32[]{:S(2)}, u32[]{:S(2)}) collective-permute-start(bf16[128,4096]{1,0:T(8,128)(2,1)S(1)} %get-tuple-element.24), channel_id=1, source_target_pairs={{0,16},{8,24},{16,0},{24,8},{1,17},{9,25},{17,1},{25,9},{2,18},{10... | collective-permute-start | bytes 3145736 | tf_op jit(solution)/shard_map/ppermute | solution.py:91
  114.7 74.9 %copy-start.2 = (bf16[128,4096]{1,0:T(8,128)(2,1)S(1)}, bf16[128,4096]{1,0:T(8,128)(2,1)}, u32[]{:S(2)}) copy-start(bf16[128,4096]{1,0:T(8,128)(2,1)} %param.9) | copy-start | bytes 3145732
  114.7 74.9 %copy-start.4 = (bf16[128,4096]{1,0:T(8,128)(2,1)S(1)}, bf16[128,4096]{1,0:T(8,128)(2,1)}, u32[]{:S(2)}) copy-start(bf16[128,4096]{1,0:T(8,128)(2,1)} %param.10) | copy-start | bytes 3145732
  195.6 87.1 %collective-permute-start.13 = (bf16[128,4096]{1,0:T(8,128)(2,1)}, bf16[128,4096]{1,0:T(8,128)(2,1)S(1)}, u32[]{:S(2)}, u32[]{:S(2)}) collective-permute-start(bf16[128,4096]{1,0:T(8,128)(2,1)} %get-tuple-element.19), channel_id=1, source_target_pairs={{0,8},{8,16},{16,24},{24,0},{1,9},{9,17},{17,25},{25,1},{2,10},{10... | collective-permute-start | bytes 3145736 | tf_op jit(solution)/shard_map/ppermute | solution.py:36
  197.3 156.8 %collective-permute-start.14 = (bf16[128,4096]{1,0:T(8,128)(2,1)}, bf16[128,4096]{1,0:T(8,128)(2,1)S(1)}, u32[]{:S(2)}, u32[]{:S(2)}) collective-permute-start(bf16[128,4096]{1,0:T(8,128)(2,1)} %get-tuple-element.19), channel_id=1, source_target_pairs={{0,16},{8,24},{16,0},{24,8},{1,17},{9,25},{17,1},{25,9},{2,18},{10... | collective-permute-start | bytes 3145736 | tf_op jit(solution)/shard_map/ppermute | solution.py:36
  201.6 156.3 %collective-permute-start.15 = (bf16[128,4096]{1,0:T(8,128)(2,1)}, bf16[128,4096]{1,0:T(8,128)(2,1)S(1)}, u32[]{:S(2)}, u32[]{:S(2)}) collective-permute-start(bf16[128,4096]{1,0:T(8,128)(2,1)} %get-tuple-element.19), channel_id=1, source_target_pairs={{0,24},{8,0},{16,8},{24,16},{1,25},{9,1},{17,9},{25,17},{2,26},{10... | collective-permute-start | bytes 3145736 | tf_op jit(solution)/shard_map/ppermute | solution.py:36
  359.0 9.8 %collective-permute-start.16 = (bf16[512,4096]{1,0:T(8,128)(2,1)}, bf16[512,4096]{1,0:T(8,128)(2,1)}, u32[]{:S(2)}, u32[]{:S(2)}) collective-permute-start(bf16[512,4096]{1,0:T(8,128)(2,1)} %constant_dynamic-update-slice_fusion), channel_id=1, source_target_pairs={{0,4},{4,0},{1,5},{5,1},{2,6},{6,2},{3,7},{7,3},{8,12},{12,8},{9,1... | collective-permute-start | bytes 12582920 | tf_op jit(solution)/shard_map/ppermute | solution.py:38
  395.5 31.6 %collective-permute-start.17 = (f32[256,1024]{1,0:T(8,128)}, f32[256,1024]{1,0:T(8,128)S(1)}, u32[]{:S(2)}, u32[]{:S(2)}) collective-permute-start(f32[256,1024]{1,0:T(8,128)} %get-tuple-element.28), channel_id=1, source_target_pairs={{0,1},{1,2},{2,3},{3,0},{4,5},{5,6},{6,7},{7,4},{8,9},{9,10},{10,1... | collective-permute-start | bytes 3145736 | tf_op jit(solution)/shard_map/ppermute | solution.py:53
  397.0 48.1 %collective-permute-start.19 = (f32[256,1024]{1,0:T(8,128)}, f32[256,1024]{1,0:T(8,128)S(1)}, u32[]{:S(2)}, u32[]{:S(2)}) collective-permute-start(f32[256,1024]{1,0:T(8,128)} %get-tuple-element.29), channel_id=1, source_target_pairs={{0,3},{1,0},{2,1},{3,2},{4,7},{5,4},{6,5},{7,6},{8,11},{9,8},{10,9... | collective-permute-start | bytes 3145736 | tf_op jit(solution)/shard_map/ppermute | solution.py:53
  397.5 48.1 %collective-permute-start.18 = (f32[256,1024]{1,0:T(8,128)}, f32[256,1024]{1,0:T(8,128)S(1)}, u32[]{:S(2)}, u32[]{:S(2)}) collective-permute-start(f32[256,1024]{1,0:T(8,128)} %get-tuple-element.30), channel_id=1, source_target_pairs={{0,2},{1,3},{2,0},{3,1},{4,6},{5,7},{6,4},{7,5},{8,10},{9,11},{10,... | collective-permute-start | bytes 3145736 | tf_op jit(solution)/shard_map/ppermute | solution.py:53
  425.0 41.7 %collective-permute-start.10 = (f32[256,1024]{1,0:T(8,128)S(1)}, f32[256,1024]{1,0:T(8,128)S(1)}, u32[]{:S(2)}, u32[]{:S(2)}) collective-permute-start(f32[256,1024]{1,0:T(8,128)S(1)} %get-tuple-element.25), channel_id=1, source_target_pairs={{0,1},{1,2},{2,3},{3,0},{4,5},{5,6},{6,7},{7,4},{8,9},{9,10},{10,1... | collective-permute-start | bytes 3145736 | tf_op jit(solution)/shard_map/ppermute | solution.py:53
  426.5 63.3 %collective-permute-start.12 = (f32[256,1024]{1,0:T(8,128)S(1)}, f32[256,1024]{1,0:T(8,128)S(1)}, u32[]{:S(2)}, u32[]{:S(2)}) collective-permute-start(f32[256,1024]{1,0:T(8,128)S(1)} %get-tuple-element.26), channel_id=1, source_target_pairs={{0,3},{1,0},{2,1},{3,2},{4,7},{5,4},{6,5},{7,6},{8,11},{9,8},{10,9... | collective-permute-start | bytes 3145736 | tf_op jit(solution)/shard_map/ppermute | solution.py:53
  427.1 63.1 %collective-permute-start.11 = (f32[256,1024]{1,0:T(8,128)S(1)}, f32[256,1024]{1,0:T(8,128)S(1)}, u32[]{:S(2)}, u32[]{:S(2)}) collective-permute-start(f32[256,1024]{1,0:T(8,128)S(1)} %get-tuple-element.27), channel_id=1, source_target_pairs={{0,2},{1,3},{2,0},{3,1},{4,6},{5,7},{6,4},{7,5},{8,10},{9,11},{10,... | collective-permute-start | bytes 3145736 | tf_op jit(solution)/shard_map/ppermute | solution.py:53
  (7 other events, 77.0 us)
Sparse Core Ops, SparseCore 0:
  10.6 80.7 all-gather.2
  191.6 157.6 all-gather.4

commit v5 on v2

--- a/solution.py
+++ b/solution.py
@@ -45,6 +45,7 @@
     hidden_act = lax.all_gather(hidden_local, ROW, axis=0, tiled=True)
 
     grad_full = gather_col(out_grad)
+    activations, grad_full = lax.optimization_barrier((activations, grad_full))
     act_full = gather_col(activations)
     tokens_all = act_full.shape[0]
 
@@ -65,21 +66,29 @@
         preferred_element_type=jnp.float32,
     )
     chip_sum = (hid_keep + hid_recv).reshape(chips, -1, hid_keep.shape[1])
-    chip_sum, hidden_act = lax.optimization_barrier((chip_sum, hidden_act))
     hid_rows = lax.dynamic_index_in_dim(chip_sum, z, axis=0, keepdims=False)
-    for s in range(1, chips):
-        piece = lax.dynamic_index_in_dim(chip_sum, (z + s) % chips, axis=0, keepdims=False)
-        piece = lax.ppermute(piece.astype(jnp.bfloat16), "z", shift_perm(chips, s))
+    pieces = [
+        lax.dynamic_index_in_dim(chip_sum, (z + s) % chips, axis=0, keepdims=False).astype(
+            jnp.bfloat16
+        )
+        for s in range(1, chips)
+    ]
+    pieces, hid_rows, hidden_act, act_full = lax.optimization_barrier(
+        (pieces, hid_rows, hidden_act, act_full)
+    )
+    for s, piece in enumerate(pieces, start=1):
+        piece = lax.ppermute(piece, "z", shift_perm(chips, s))
         hid_rows = hid_rows + piece.astype(jnp.float32)
+    acc_down = lax.dot_general(
+        hidden_act, grad_full, CONTRACT_FIRST, preferred_element_type=jnp.float32
+    )
+    hid_rows, acc_down = lax.optimization_barrier((hid_rows, acc_down))
 
     gate_local = (
         hid_rows * up_float * sigmoid_gate * (1.0 + gate_float * (1.0 - sigmoid_gate))
     ).astype(jnp.bfloat16)
     up_local = (hid_rows * silu_gate).astype(jnp.bfloat16)
 
-    acc_down = lax.dot_general(
-        hidden_act, grad_full, CONTRACT_FIRST, preferred_element_type=jnp.float32
-    )
     gate_delta = lax.all_gather(gate_local, ROW, axis=0, tiled=True)
     up_delta = lax.all_gather(up_local, ROW, axis=0, tiled=True)
     acc_gate = lax.dot_general(
@@ -88,6 +97,7 @@
     input_gate = reduce_scatter_col(
         lax.dot_general(gate_delta, gate_weight, CONTRACT_LAST, preferred_element_type=jnp.float32)
     )
+    acc_gate, input_gate, up_delta = lax.optimization_barrier((acc_gate, input_gate, up_delta))
     acc_up = lax.dot_general(act_full, up_delta, CONTRACT_FIRST, preferred_element_type=jnp.float32)
     input_up = reduce_scatter_col(
         lax.dot_general(up_delta, up_weight, CONTRACT_LAST, preferred_element_type=jnp.float32)

time: 435 us -> 441 us (1.014)
  local copies, waits for them, and re-layouts: 18.2 us -> 6.26 us
  other arithmetic: 11.6 us -> 21.5 us
  waiting for transfers between devices: 281 us -> 290 us
    ppermute x6, waiting for transfers between devices: 17.1 us -> 73.1 us  [reduce_scatter_col(): total = total + lax.ppermute(piece, 'col', shift_perm(n, s))]
    all_gather x1, waiting for transfers between devices: 63.7 us -> 20.4 us  [body(): up_delta = lax.all_gather(up_local, ROW, axis=0, tiled=True)]
    all_gather x1, waiting for transfers between devices: 35 us -> 70.2 us  [body(): gate_delta = lax.all_gather(gate_local, ROW, axis=0, tiled=True)]
    ppermute x3, waiting for transfers between devices: 90.2 us -> 72.3 us  [body(): piece = lax.ppermute(piece, 'z', shift_perm(chips, s))]
    all_gather x1, waiting for transfers between devices: 21.3 us -> 7.12 us  [body(): hidden_act = lax.all_gather(hidden_local, ROW, axis=0, tiled=True)]
    ppermute x1, waiting for transfers between devices: 13.5 us -> 0.01 us  [body(): hid_recv = lax.ppermute(hid_send, 'core', [(0, 1), (1, 0)])]
    convert_element_type x1 -> x3, other arithmetic: 5.63 us -> 16.2 us  [the longest x1 9.77 us: body(): (acc_down * factor).astype(jnp.bfloat16)]
    ppermute x6, waiting for transfers between devices: 39.1 us -> 45.8 us  [gather_col(): part = lax.ppermute(block, 'col', shift_perm(n, s))]
  transfers between devices with their start and end apart: 19 -> 19, of which waited for: 12 -> 16; matrix products, arithmetic and copies ran while one was open for 23% -> 17% of each run, Pallas kernels for 0% -> 0%
where the time goes in v5:
time: 441 us; the launch traced here: 436 us
  waiting for transfers between devices  290 us (66%)
  matrix products  84.3 us (19%)
  other arithmetic  21.5 us (5%)
  starting transfers between devices  20.4 us (5%)
  between operations  14.1 us (3%)
  local copies, waits for them, and re-layouts  6.26 us (1%)
    ppermute x6, waiting for transfers between devices, reduce_scatter_col(): total = total + lax.ppermute(piece, 'col', shift_perm(n, s))  73.1 us
    ppermute x3, waiting for transfers between devices, body(): piece = lax.ppermute(piece, 'z', shift_perm(chips, s))  72.3 us
    all_gather x1, waiting for transfers between devices, body(): gate_delta = lax.all_gather(gate_local, ROW, axis=0, tiled=True)  70.2 us
    ppermute x6, waiting for transfers between devices, gather_col(): part = lax.ppermute(block, 'col', shift_perm(n, s))  45.8 us
    all_gather x1, waiting for transfers between devices, body(): up_delta = lax.all_gather(up_local, ROW, axis=0, tiled=True)  20.4 us
    dot_general x1, matrix products, body(): lax.dot_general(hidden_act, grad_full, CONTRACT_FIRST, preferred_element_...  16.2 us
    dot_general x1, matrix products, body(): lax.dot_general(act_full, up_delta, CONTRACT_FIRST, preferred_element_typ...  14.8 us
    dot_general x1, matrix products, body(): lax.dot_general(gate_delta, gate_weight, CONTRACT_LAST, preferred_element...  12.8 us
  transfers between devices with their start and end apart: 19, of which 16 were waited for; matrix products, arithmetic and copies ran while one was open for 17% of the time, Pallas kernels for 0%

profile of v5, /device:TPU:10, one launch (start us, length us, event | category | flops | bytes accessed | tf_op | source)
XLA Modules:
  0.0 436.1 jit_solution(18368533199082992916)
XLA Ops:
  7.2 3.2 fusion
  14.4 10.9 %collective-permute-done = bf16[256,1024]{1,0:T(8,128)(2,1)S(1)} collective-permute-done((bf16[256,1024]{1,0:T(8,128)(2,1)S(1)}, bf16[256,1024]{1,0:T(8,128)(2,1)S(1)}, u32[]{:S(2)}, u32[]{:S(2)}) %collective-permute-start) | collective-permute-done | bytes 524320 | tf_op jit(solution)/shard_map/ppermute | solution.py:23
  25.4 11.3 %collective-permute-done.1 = bf16[256,1024]{1,0:T(8,128)(2,1)S(1)} collective-permute-done((bf16[256,1024]{1,0:T(8,128)(2,1)S(1)}, bf16[256,1024]{1,0:T(8,128)(2,1)S(1)}, u32[]{:S(2)}, u32[]{:S(2)}) %collective-permute-start.1) | collective-permute-done | bytes 524320 | tf_op jit(solution)/shard_map/ppermute | solution.py:23
  38.1 6.8 %fusion.17 = f32[512,4096]{1,0:T(8,128)} fusion(bf16[512,1024]{1,0:T(8,128)(2,1)S(1)} %bitcast.66, bf16[4096,1024]{1,0:T(8,128)(2,1)S(1)} %copy-done.7), kind=kOutput, calls=%fused_computation.50 | convolution fusion | flops 4294967296 | bytes 17825792 | tf_op jit(solution)/shard_map/dot_general | solution.py:59
  47.7 11.9 %collective-permute-done.4 = bf16[256,1024]{1,0:T(8,128)(2,1)S(1)} collective-permute-done((bf16[256,1024]{1,0:T(8,128)(2,1)S(1)}, bf16[256,1024]{1,0:T(8,128)(2,1)S(1)}, u32[]{:S(2)}, u32[]{:S(2)}) %collective-permute-start.4) | collective-permute-done | bytes 524320 | tf_op jit(solution)/shard_map/ppermute | solution.py:23
  59.7 11.7 %collective-permute-done.5 = bf16[256,1024]{1,0:T(8,128)(2,1)S(1)} collective-permute-done((bf16[256,1024]{1,0:T(8,128)(2,1)S(1)}, bf16[256,1024]{1,0:T(8,128)(2,1)S(1)}, u32[]{:S(2)}, u32[]{:S(2)}) %collective-permute-start.5) | collective-permute-done | bytes 524320 | tf_op jit(solution)/shard_map/ppermute | solution.py:23
  72.8 9.5 %convolution_add_fusion = f32[512,4096]{1,0:T(8,128)S(1)} fusion(f32[512,4096]{1,0:T(8,128)} %collective-permute-done.3, bf16[512,1024]{1,0:T(8,128)(2,1)S(1)} %bitcast.65, bf16[4096,1024]{1,0:T(8,128)(2,1)} %param.13), kind=kOutput, calls=%fused_computation.3 | convolution fusion | flops 4297064448 | bytes 26214400 | tf_op jit(solution)/shard_map/dot_general | solution.py:64
  84.2 7.1 %all-gather.4.cloned.1.call-done = bf16[1024,4096]{1,0:T(8,128)(2,1)} async-done(((bf16[128,4096]{1,0:T(8,128)(2,1)}), bf16[1024,4096]{1,0:T(8,128)(2,1)}) %all-gather.4.cloned.1.call-update) | async-done | bytes 8388624 | tf_op jit(solution)/shard_map/all_gather | solution.py:45
  96.6 16.2 %fusion.18 = f32[4096,1024]{1,0:T(8,128)} fusion(bf16[1024,4096]{1,0:T(8,128)(2,1)} %all-gather.4.cloned.1.call-done, bf16[1024,1024]{1,0:T(8,128)(2,1)} %copy-done), kind=kOutput, calls=%fused_computation.51 | convolution fusion | flops 8589934592 | bytes 27262976 | tf_op jit(solution)/shard_map/dot_general | solution.py:82
  112.8 5.9 %collective-permute-done.9 = bf16[128,4096]{1,0:T(8,128)(2,1)S(1)} collective-permute-done((bf16[128,4096]{1,0:T(8,128)(2,1)}, bf16[128,4096]{1,0:T(8,128)(2,1)S(1)}, u32[]{:S(2)}, u32[]{:S(2)}) %collective-permute-start.9) | collective-permute-done | bytes 1048608 | tf_op jit(solution)/shard_map/ppermute | solution.py:80
  118.7 44.1 %collective-permute-done.8 = bf16[128,4096]{1,0:T(8,128)(2,1)S(1)} collective-permute-done((bf16[128,4096]{1,0:T(8,128)(2,1)}, bf16[128,4096]{1,0:T(8,128)(2,1)S(1)}, u32[]{:S(2)}, u32[]{:S(2)}) %collective-permute-start.8) | collective-permute-done | bytes 1048608 | tf_op jit(solution)/shard_map/ppermute | solution.py:80
  162.8 22.3 %collective-permute-done.7 = bf16[128,4096]{1,0:T(8,128)(2,1)S(1)} collective-permute-done((bf16[128,4096]{1,0:T(8,128)(2,1)S(1)}, bf16[128,4096]{1,0:T(8,128)(2,1)S(1)}, u32[]{:S(2)}, u32[]{:S(2)}) %collective-permute-start.7) | collective-permute-done | bytes 1048608 | tf_op jit(solution)/shard_map/ppermute | solution.py:80
  188.8 9.8 %multiply_convert_fusion = bf16[4096,1024]{1,0:T(8,128)(2,1)} fusion(f32[4096,1024]{1,0:T(8,128)} %fusion.18), kind=kLoop, calls=%fused_computation | loop fusion | flops 8388608 | bytes 25165824 | tf_op jit(solution)/shard_map/convert_element_type | solution.py:111
  198.6 70.2 %all-gather.6.cloned.1.call-done = bf16[1024,4096]{1,0:T(8,128)(2,1)} async-done(((bf16[128,4096]{1,0:T(8,128)(2,1)}), bf16[1024,4096]{1,0:T(8,128)(2,1)}) %all-gather.6.cloned.1.call-update) | async-done | bytes 8388624 | tf_op jit(solution)/shard_map/all_gather | solution.py:92
  268.8 12.8 %fusion.20 = f32[1024,1024]{1,0:T(8,128)S(1)} fusion(bf16[1024,4096]{1,0:T(8,128)(2,1)} %all-gather.6.cloned.1.call-done, bf16[1024,4096]{1,0:T(8,128)(2,1)} %param.11), kind=kOutput, calls=%fused_computation.53 | convolution fusion | flops 8589934592 | bytes 20971520 | tf_op jit(solution)/shard_map/dot_general | solution.py:98
  286.5 11.5 %fusion.19 = f32[1024,4096]{1,0:T(8,128)} fusion(bf16[1024,1024]{1,0:T(8,128)(2,1)S(1)} %copy-done.4, bf16[1024,4096]{1,0:T(8,128)(2,1)S(1)} %copy-done.8), kind=kOutput, calls=%fused_computation.52 | convolution fusion | flops 8589934592 | bytes 27262976 | tf_op jit(solution)/shard_map/dot_general | solution.py:94
  298.0 11.0 %collective-permute-done.12 = f32[256,1024]{1,0:T(8,128)S(1)} collective-permute-done((f32[256,1024]{1,0:T(8,128)S(1)}, f32[256,1024]{1,0:T(8,128)S(1)}, u32[]{:S(2)}, u32[]{:S(2)}) %collective-permute-start.12) | collective-permute-done | bytes 1048608 | tf_op jit(solution)/shard_map/ppermute | solution.py:35
  309.0 20.9 %collective-permute-done.11 = f32[256,1024]{1,0:T(8,128)S(1)} collective-permute-done((f32[256,1024]{1,0:T(8,128)S(1)}, f32[256,1024]{1,0:T(8,128)S(1)}, u32[]{:S(2)}, u32[]{:S(2)}) %collective-permute-start.11) | collective-permute-done | bytes 1048608 | tf_op jit(solution)/shard_map/ppermute | solution.py:35
  331.2 20.4 %all-gather.8.cloned.1.call-done = bf16[1024,4096]{1,0:T(8,128)(2,1)} async-done(((bf16[128,4096]{1,0:T(8,128)(2,1)}), bf16[1024,4096]{1,0:T(8,128)(2,1)}) %all-gather.8.cloned.1.call-update) | async-done | bytes 8388624 | tf_op jit(solution)/shard_map/all_gather | solution.py:93
  351.6 14.8 %multiply_convert_fusion.1 = bf16[1024,4096]{1,0:T(8,128)(2,1)} fusion(bf16[1024,1024]{1,0:T(8,128)(2,1)S(1)} %copy-done.4, bf16[1024,4096]{1,0:T(8,128)(2,1)} %all-gather.8.cloned.1.call-done), kind=kOutput, calls=%fused_computation.1 | convolution fusion | flops 8598323200 | bytes 18874368 | tf_op jit(solution)/shard_map/dot_general | solution.py:101
  366.4 12.8 %fusion.21 = f32[1024,1024]{1,0:T(8,128)S(1)} fusion(bf16[1024,4096]{1,0:T(8,128)(2,1)} %all-gather.8.cloned.1.call-done, bf16[1024,4096]{1,0:T(8,128)(2,1)} %param.12), kind=kOutput, calls=%fused_computation.54 | convolution fusion | flops 8589934592 | bytes 20971520 | tf_op jit(solution)/shard_map/dot_general | solution.py:103
  384.0 4.0 multiply_convert_fusion.2
  388.1 18.5 %collective-permute-done.15 = f32[256,1024]{1,0:T(8,128)S(1)} collective-permute-done((f32[256,1024]{1,0:T(8,128)S(1)}, f32[256,1024]{1,0:T(8,128)S(1)}, u32[]{:S(2)}, u32[]{:S(2)}) %collective-permute-start.15) | collective-permute-done | bytes 1048608 | tf_op jit(solution)/shard_map/ppermute | solution.py:35
  406.6 20.9 %collective-permute-done.14 = f32[256,1024]{1,0:T(8,128)S(1)} collective-permute-done((f32[256,1024]{1,0:T(8,128)S(1)}, f32[256,1024]{1,0:T(8,128)S(1)}, u32[]{:S(2)}, u32[]{:S(2)}) %collective-permute-start.14) | collective-permute-done | bytes 1048608 | tf_op jit(solution)/shard_map/ppermute | solution.py:35
  (73 shorter events, 33.7 us)
Async XLA Ops:
  7.2 84.2 %all-gather.4.cloned.1.call-start = ((), (), s32[]{:S(2)}) async-start(), calls=%async_computation | async-start | bytes 9437184 | tf_op jit(solution)/shard_map/all_gather | solution.py:45
  10.4 258.4 %all-gather.6.cloned.1.call-start = ((), (), s32[]{:S(2)}) async-start(), calls=%async_computation.1 | async-start | bytes 9437184 | tf_op jit(solution)/shard_map/all_gather | solution.py:92
  10.5 14.9 %collective-permute-start = (bf16[256,1024]{1,0:T(8,128)(2,1)S(1)}, bf16[256,1024]{1,0:T(8,128)(2,1)S(1)}, u32[]{:S(2)}, u32[]{:S(2)}) collective-permute-start(bf16[256,1024]{1,0:T(8,128)(2,1)S(1)} %copy-done.5), channel_id=1, source_target_pairs={{0,1},{1,2},{2,3},{3,0},{4,5},{5,6},{6,7},{7,4},{8,9},{9,10},{10,1... | collective-permute-start | bytes 1572872 | tf_op jit(solution)/shard_map/ppermute | solution.py:23
  12.0 24.6 %collective-permute-start.1 = (bf16[256,1024]{1,0:T(8,128)(2,1)S(1)}, bf16[256,1024]{1,0:T(8,128)(2,1)S(1)}, u32[]{:S(2)}, u32[]{:S(2)}) collective-permute-start(bf16[256,1024]{1,0:T(8,128)(2,1)S(1)} %copy-done.5), channel_id=1, source_target_pairs={{0,2},{1,3},{2,0},{3,1},{4,6},{5,7},{6,4},{7,5},{8,10},{9,11},{10,... | collective-permute-start | bytes 1572872 | tf_op jit(solution)/shard_map/ppermute | solution.py:23
  12.5 24.2 %collective-permute-start.2 = (bf16[256,1024]{1,0:T(8,128)(2,1)S(1)}, bf16[256,1024]{1,0:T(8,128)(2,1)S(1)}, u32[]{:S(2)}, u32[]{:S(2)}) collective-permute-start(bf16[256,1024]{1,0:T(8,128)(2,1)S(1)} %copy-done.5), channel_id=1, source_target_pairs={{0,3},{1,0},{2,1},{3,2},{4,7},{5,4},{6,5},{7,6},{8,11},{9,8},{10,9... | collective-permute-start | bytes 1572872 | tf_op jit(solution)/shard_map/ppermute | solution.py:23
  14.4 23.7 %copy-start.7 = (bf16[4096,1024]{1,0:T(8,128)(2,1)S(1)}, bf16[4096,1024]{1,0:T(8,128)(2,1)}, u32[]{:S(2)}) copy-start(bf16[4096,1024]{1,0:T(8,128)(2,1)} %param.13) | copy-start | bytes 25165828
  44.9 26.6 %collective-permute-start.3 = (f32[512,4096]{1,0:T(8,128)}, f32[512,4096]{1,0:T(8,128)}, u32[]{:S(2)}, u32[]{:S(2)}) collective-permute-start(f32[512,4096]{1,0:T(8,128)} %fusion.17), channel_id=1, source_target_pairs={{0,4},{4,0},{1,5},{5,1},{2,6},{6,2},{3,7},{7,3},{8,12},{12,8},{9,1... | collective-permute-start | bytes 25165832 | tf_op jit(solution)/shard_map/ppermute | solution.py:63
  44.9 14.7 %collective-permute-start.4 = (bf16[256,1024]{1,0:T(8,128)(2,1)S(1)}, bf16[256,1024]{1,0:T(8,128)(2,1)S(1)}, u32[]{:S(2)}, u32[]{:S(2)}) collective-permute-start(bf16[256,1024]{1,0:T(8,128)(2,1)S(1)} %copy-done.6), channel_id=1, source_target_pairs={{0,1},{1,2},{2,3},{3,0},{4,5},{5,6},{6,7},{7,4},{8,9},{9,10},{10,1... | collective-permute-start | bytes 1572872 | tf_op jit(solution)/shard_map/ppermute | solution.py:23
  46.2 25.1 %collective-permute-start.5 = (bf16[256,1024]{1,0:T(8,128)(2,1)S(1)}, bf16[256,1024]{1,0:T(8,128)(2,1)S(1)}, u32[]{:S(2)}, u32[]{:S(2)}) collective-permute-start(bf16[256,1024]{1,0:T(8,128)(2,1)S(1)} %copy-done.6), channel_id=1, source_target_pairs={{0,2},{1,3},{2,0},{3,1},{4,6},{5,7},{6,4},{7,5},{8,10},{9,11},{10,... | collective-permute-start | bytes 1572872 | tf_op jit(solution)/shard_map/ppermute | solution.py:23
  46.7 24.7 %collective-permute-start.6 = (bf16[256,1024]{1,0:T(8,128)(2,1)S(1)}, bf16[256,1024]{1,0:T(8,128)(2,1)S(1)}, u32[]{:S(2)}, u32[]{:S(2)}) collective-permute-start(bf16[256,1024]{1,0:T(8,128)(2,1)S(1)} %copy-done.6), channel_id=1, source_target_pairs={{0,3},{1,0},{2,1},{3,2},{4,7},{5,4},{6,5},{7,6},{8,11},{9,8},{10,9... | collective-permute-start | bytes 1572872 | tf_op jit(solution)/shard_map/ppermute | solution.py:23
  91.3 27.4 %collective-permute-start.9 = (bf16[128,4096]{1,0:T(8,128)(2,1)}, bf16[128,4096]{1,0:T(8,128)(2,1)S(1)}, u32[]{:S(2)}, u32[]{:S(2)}) collective-permute-start(bf16[128,4096]{1,0:T(8,128)(2,1)} %get-tuple-element.23), channel_id=1, source_target_pairs={{0,24},{8,0},{16,8},{24,16},{1,25},{9,1},{17,9},{25,17},{2,26},{10... | collective-permute-start | bytes 3145736 | tf_op jit(solution)/shard_map/ppermute | solution.py:80
  94.4 68.5 %collective-permute-start.8 = (bf16[128,4096]{1,0:T(8,128)(2,1)}, bf16[128,4096]{1,0:T(8,128)(2,1)S(1)}, u32[]{:S(2)}, u32[]{:S(2)}) collective-permute-start(bf16[128,4096]{1,0:T(8,128)(2,1)} %get-tuple-element.22), channel_id=1, source_target_pairs={{0,16},{8,24},{16,0},{24,8},{1,17},{9,25},{17,1},{25,9},{2,18},{10... | collective-permute-start | bytes 3145736 | tf_op jit(solution)/shard_map/ppermute | solution.py:80
  95.3 89.8 %collective-permute-start.7 = (bf16[128,4096]{1,0:T(8,128)(2,1)S(1)}, bf16[128,4096]{1,0:T(8,128)(2,1)S(1)}, u32[]{:S(2)}, u32[]{:S(2)}) collective-permute-start(bf16[128,4096]{1,0:T(8,128)(2,1)S(1)} %get-tuple-element.21), channel_id=1, source_target_pairs={{0,8},{8,16},{16,24},{24,0},{1,9},{9,17},{17,25},{25,1},{2,10},{10... | collective-permute-start | bytes 3145736 | tf_op jit(solution)/shard_map/ppermute | solution.py:80
  112.8 72.8 %copy-start.1 = (bf16[128,4096]{1,0:T(8,128)(2,1)S(1)}, bf16[128,4096]{1,0:T(8,128)(2,1)}, u32[]{:S(2)}) copy-start(bf16[128,4096]{1,0:T(8,128)(2,1)} %param.10) | copy-start | bytes 3145732
  112.8 72.8 %copy-start.2 = (bf16[128,4096]{1,0:T(8,128)(2,1)S(1)}, bf16[128,4096]{1,0:T(8,128)(2,1)}, u32[]{:S(2)}) copy-start(bf16[128,4096]{1,0:T(8,128)(2,1)} %param.9) | copy-start | bytes 3145732
  188.0 163.6 %all-gather.8.cloned.1.call-start = ((), (), s32[]{:S(2)}) async-start(), calls=%async_computation.2 | async-start | bytes 9437184 | tf_op jit(solution)/shard_map/all_gather | solution.py:93
  282.0 27.0 %collective-permute-start.12 = (f32[256,1024]{1,0:T(8,128)S(1)}, f32[256,1024]{1,0:T(8,128)S(1)}, u32[]{:S(2)}, u32[]{:S(2)}) collective-permute-start(f32[256,1024]{1,0:T(8,128)S(1)} %get-tuple-element.37), channel_id=1, source_target_pairs={{0,3},{1,0},{2,1},{3,2},{4,7},{5,4},{6,5},{7,6},{8,11},{9,8},{10,9... | collective-permute-start | bytes 3145736 | tf_op jit(solution)/shard_map/ppermute | solution.py:35
  282.4 47.5 %collective-permute-start.11 = (f32[256,1024]{1,0:T(8,128)S(1)}, f32[256,1024]{1,0:T(8,128)S(1)}, u32[]{:S(2)}, u32[]{:S(2)}) collective-permute-start(f32[256,1024]{1,0:T(8,128)S(1)} %get-tuple-element.38), channel_id=1, source_target_pairs={{0,2},{1,3},{2,0},{3,1},{4,6},{5,7},{6,4},{7,5},{8,10},{9,11},{10,... | collective-permute-start | bytes 3145736 | tf_op jit(solution)/shard_map/ppermute | solution.py:35
  284.1 46.7 %collective-permute-start.10 = (f32[256,1024]{1,0:T(8,128)S(1)}, f32[256,1024]{1,0:T(8,128)S(1)}, u32[]{:S(2)}, u32[]{:S(2)}) collective-permute-start(f32[256,1024]{1,0:T(8,128)S(1)} %get-tuple-element.36), channel_id=1, source_target_pairs={{0,1},{1,2},{2,3},{3,0},{4,5},{5,6},{6,7},{7,4},{8,9},{9,10},{10,1... | collective-permute-start | bytes 3145736 | tf_op jit(solution)/shard_map/ppermute | solution.py:35
  351.6 32.4 %slice-start = ((s8[16777216]{0:T(1024)(128)(4,1)}), s8[4194304]{0:T(1024)(128)(4,1)S(1)}, s32[]{:S(2)}) async-start(s8[16777216]{0:T(1024)(128)(4,1)} %bitcast.56), calls=%async_computation.3 | async-start | bytes 8388608
  351.6 32.4 %slice-start.1 = ((s8[16777216]{0:T(1024)(128)(4,1)}), s8[4194304]{0:T(1024)(128)(4,1)S(1)}, s32[]{:S(2)}) async-start(s8[16777216]{0:T(1024)(128)(4,1)} %bitcast.56), calls=%async_computation.4 | async-start | bytes 8388608
  379.6 27.0 %collective-permute-start.15 = (f32[256,1024]{1,0:T(8,128)S(1)}, f32[256,1024]{1,0:T(8,128)S(1)}, u32[]{:S(2)}, u32[]{:S(2)}) collective-permute-start(f32[256,1024]{1,0:T(8,128)S(1)} %get-tuple-element.34), channel_id=1, source_target_pairs={{0,3},{1,0},{2,1},{3,2},{4,7},{5,4},{6,5},{7,6},{8,11},{9,8},{10,9... | collective-permute-start | bytes 3145736 | tf_op jit(solution)/shard_map/ppermute | solution.py:35
  380.0 47.5 %collective-permute-start.14 = (f32[256,1024]{1,0:T(8,128)S(1)}, f32[256,1024]{1,0:T(8,128)S(1)}, u32[]{:S(2)}, u32[]{:S(2)}) collective-permute-start(f32[256,1024]{1,0:T(8,128)S(1)} %get-tuple-element.35), channel_id=1, source_target_pairs={{0,2},{1,3},{2,0},{3,1},{4,6},{5,7},{6,4},{7,5},{8,10},{9,11},{10,... | collective-permute-start | bytes 3145736 | tf_op jit(solution)/shard_map/ppermute | solution.py:35
  381.6 46.7 %collective-permute-start.13 = (f32[256,1024]{1,0:T(8,128)S(1)}, f32[256,1024]{1,0:T(8,128)S(1)}, u32[]{:S(2)}, u32[]{:S(2)}) collective-permute-start(f32[256,1024]{1,0:T(8,128)S(1)} %get-tuple-element.33), channel_id=1, source_target_pairs={{0,1},{1,2},{2,3},{3,0},{4,5},{5,6},{6,7},{7,4},{8,9},{9,10},{10,1... | collective-permute-start | bytes 3145736 | tf_op jit(solution)/shard_map/ppermute | solution.py:35
  (8 other events, 70.7 us)
Sparse Core Ops, SparseCore 0:
  10.6 80.7 all-gather.3
  188.2 80.5 all-gather.5
  271.0 80.5 all-gather.7

commit v6 on v2

--- a/solution.py
+++ b/solution.py
@@ -45,6 +45,7 @@
     hidden_act = lax.all_gather(hidden_local, ROW, axis=0, tiled=True)
 
     grad_full = gather_col(out_grad)
+    activations, grad_full = lax.optimization_barrier((activations, grad_full))
     act_full = gather_col(activations)
     tokens_all = act_full.shape[0]
 
@@ -65,21 +66,22 @@
         preferred_element_type=jnp.float32,
     )
     chip_sum = (hid_keep + hid_recv).reshape(chips, -1, hid_keep.shape[1])
-    chip_sum, hidden_act = lax.optimization_barrier((chip_sum, hidden_act))
+    chip_sum, hidden_act, act_full = lax.optimization_barrier((chip_sum, hidden_act, act_full))
     hid_rows = lax.dynamic_index_in_dim(chip_sum, z, axis=0, keepdims=False)
     for s in range(1, chips):
         piece = lax.dynamic_index_in_dim(chip_sum, (z + s) % chips, axis=0, keepdims=False)
         piece = lax.ppermute(piece.astype(jnp.bfloat16), "z", shift_perm(chips, s))
         hid_rows = hid_rows + piece.astype(jnp.float32)
+    acc_down = lax.dot_general(
+        hidden_act, grad_full, CONTRACT_FIRST, preferred_element_type=jnp.float32
+    )
+    hid_rows, acc_down = lax.optimization_barrier((hid_rows, acc_down))
 
     gate_local = (
         hid_rows * up_float * sigmoid_gate * (1.0 + gate_float * (1.0 - sigmoid_gate))
     ).astype(jnp.bfloat16)
     up_local = (hid_rows * silu_gate).astype(jnp.bfloat16)
 
-    acc_down = lax.dot_general(
-        hidden_act, grad_full, CONTRACT_FIRST, preferred_element_type=jnp.float32
-    )
     gate_delta = lax.all_gather(gate_local, ROW, axis=0, tiled=True)
     up_delta = lax.all_gather(up_local, ROW, axis=0, tiled=True)
     acc_gate = lax.dot_general(
@@ -88,10 +90,13 @@
     input_gate = reduce_scatter_col(
         lax.dot_general(gate_delta, gate_weight, CONTRACT_LAST, preferred_element_type=jnp.float32)
     )
+    acc_gate, input_gate, up_delta = lax.optimization_barrier((acc_gate, input_gate, up_delta))
+    input_up = lax.dot_general(
+        up_delta, up_weight, CONTRACT_LAST, preferred_element_type=jnp.float32
+    )
+    up_delta, input_up = lax.optimization_barrier((up_delta, input_up))
+    input_up = reduce_scatter_col(input_up)
     acc_up = lax.dot_general(act_full, up_delta, CONTRACT_FIRST, preferred_element_type=jnp.float32)
-    input_up = reduce_scatter_col(
-        lax.dot_general(up_delta, up_weight, CONTRACT_LAST, preferred_element_type=jnp.float32)
-    )
     input_rows = (input_gate + input_up).astype(jnp.bfloat16)
     factor = float(tokens_all) ** (-0.5)
     return (

time: 435 us -> 433 us (level)
  waiting for transfers between devices: 281 us -> 267 us
  other arithmetic: 11.6 us -> 24.2 us
    all_gather x1, waiting for transfers between devices: 63.7 us -> 19.9 us  [body(): up_delta = lax.all_gather(up_local, ROW, axis=0, tiled=True)]
    ppermute x6, waiting for transfers between devices: 17.1 us -> 58.3 us  [reduce_scatter_col(): total = total + lax.ppermute(piece, 'col', shift_perm(n, s))]
    all_gather x1, waiting for transfers between devices: 35 us -> 71.3 us  [body(): gate_delta = lax.all_gather(gate_local, ROW, axis=0, tiled=True)]
    ppermute x3, waiting for transfers between devices: 90.2 us -> 72.7 us  [body(): piece = lax.ppermute(piece.astype(jnp.bfloat16), 'z', shift_perm(chips, s))]
    all_gather x1, waiting for transfers between devices: 21.3 us -> 4.36 us  [body(): hidden_act = lax.all_gather(hidden_local, ROW, axis=0, tiled=True)]
    ppermute x1, waiting for transfers between devices: 13.5 us -> 0.01 us  [body(): hid_recv = lax.ppermute(hid_send, 'core', [(0, 1), (1, 0)])]
    convert_element_type x1 -> x3, other arithmetic: 5.63 us -> 16 us  [the longest x1 9.6 us: body(): (acc_down * factor).astype(jnp.bfloat16)]
  transfers between devices with their start and end apart: 19 -> 19, of which waited for: 12 -> 16; matrix products, arithmetic and copies ran while one was open for 23% -> 24% of each run, Pallas kernels for 0% -> 0%
where the time goes in v6:
time: 433 us; the launch traced here: 429 us
  waiting for transfers between devices  267 us (62%)
  matrix products  87.5 us (20%)
  other arithmetic  24.2 us (6%)
  starting transfers between devices  18.7 us (4%)
  local copies, waits for them, and re-layouts  16.8 us (4%)
  between operations  14 us (3%)
    ppermute x3, waiting for transfers between devices, body(): piece = lax.ppermute(piece.astype(jnp.bfloat16), 'z', shift_perm(chips, s))  72.7 us
    all_gather x1, waiting for transfers between devices, body(): gate_delta = lax.all_gather(gate_local, ROW, axis=0, tiled=True)  71.3 us
    ppermute x6, waiting for transfers between devices, reduce_scatter_col(): total = total + lax.ppermute(piece, 'col', shift_perm(n, s))  58.3 us
    ppermute x6, waiting for transfers between devices, gather_col(): part = lax.ppermute(block, 'col', shift_perm(n, s))  40.2 us
    all_gather x1, waiting for transfers between devices, body(): up_delta = lax.all_gather(up_local, ROW, axis=0, tiled=True)  19.9 us
    dot_general x1, matrix products, body(): lax.dot_general(act_full, up_delta, CONTRACT_FIRST, preferred_element_typ...  15.6 us
    dot_general x1, matrix products, body(): lax.dot_general(hidden_act, grad_full, CONTRACT_FIRST, preferred_element_...  14.6 us
    dot_general x1, matrix products, body(): lax.dot_general(act_full, gate_delta, CONTRACT_FIRST, preferred_element_t...  13.7 us
  transfers between devices with their start and end apart: 19, of which 16 were waited for; matrix products, arithmetic and copies ran while one was open for 24% of the time, Pallas kernels for 0%

profile of v6, /device:TPU:10, one launch (start us, length us, event | category | flops | bytes accessed | tf_op | source)
XLA Modules:
  0.0 428.7 jit_solution(13403951689311367380)
XLA Ops:
  7.2 3.2 fusion
  14.4 11.0 %collective-permute-done = bf16[256,1024]{1,0:T(8,128)(2,1)} collective-permute-done((bf16[256,1024]{1,0:T(8,128)(2,1)S(1)}, bf16[256,1024]{1,0:T(8,128)(2,1)}, u32[]{:S(2)}, u32[]{:S(2)}) %collective-permute-start) | collective-permute-done | bytes 524320 | tf_op jit(solution)/shard_map/ppermute | solution.py:23
  26.5 10.2 %collective-permute-done.1 = bf16[256,1024]{1,0:T(8,128)(2,1)} collective-permute-done((bf16[256,1024]{1,0:T(8,128)(2,1)S(1)}, bf16[256,1024]{1,0:T(8,128)(2,1)}, u32[]{:S(2)}, u32[]{:S(2)}) %collective-permute-start.1) | collective-permute-done | bytes 524320 | tf_op jit(solution)/shard_map/ppermute | solution.py:23
  38.1 6.8 %fusion.19 = f32[512,4096]{1,0:T(8,128)} fusion(bf16[512,1024]{1,0:T(8,128)(2,1)S(1)} %bitcast.70, bf16[4096,1024]{1,0:T(8,128)(2,1)S(1)} %copy-done.3), kind=kOutput, calls=%fused_computation.51 | convolution fusion | flops 4294967296 | bytes 17825792 | tf_op jit(solution)/shard_map/dot_general | solution.py:59
  50.9 9.1 %collective-permute-done.4 = bf16[256,1024]{1,0:T(8,128)(2,1)} collective-permute-done((bf16[256,1024]{1,0:T(8,128)(2,1)}, bf16[256,1024]{1,0:T(8,128)(2,1)}, u32[]{:S(2)}, u32[]{:S(2)}) %collective-permute-start.4) | collective-permute-done | bytes 524320 | tf_op jit(solution)/shard_map/ppermute | solution.py:23
  61.8 9.9 %collective-permute-done.5 = bf16[256,1024]{1,0:T(8,128)(2,1)} collective-permute-done((bf16[256,1024]{1,0:T(8,128)(2,1)}, bf16[256,1024]{1,0:T(8,128)(2,1)}, u32[]{:S(2)}, u32[]{:S(2)}) %collective-permute-start.5) | collective-permute-done | bytes 524320 | tf_op jit(solution)/shard_map/ppermute | solution.py:23
  75.5 11.5 %convolution_add_fusion = f32[512,4096]{1,0:T(8,128)} fusion(f32[512,4096]{1,0:T(8,128)} %collective-permute-done.3, bf16[512,1024]{1,0:T(8,128)(2,1)S(1)} %bitcast.69, bf16[4096,1024]{1,0:T(8,128)(2,1)} %param.13), kind=kOutput, calls=%fused_computation.3 | convolution fusion | flops 4297064448 | bytes 26214400 | tf_op jit(solution)/shard_map/dot_general | solution.py:64
  87.0 4.4 %all-gather.4.cloned.1.call-done = bf16[1024,4096]{1,0:T(8,128)(2,1)} async-done(((bf16[128,4096]{1,0:T(8,128)(2,1)}), bf16[1024,4096]{1,0:T(8,128)(2,1)}) %all-gather.4.cloned.1.call-update) | async-done | bytes 8388624 | tf_op jit(solution)/shard_map/all_gather | solution.py:45
  91.3 3.3 fusion.10
  100.1 14.6 %fusion.20 = f32[4096,1024]{1,0:T(8,128)} fusion(bf16[1024,4096]{1,0:T(8,128)(2,1)} %all-gather.4.cloned.1.call-done, bf16[1024,1024]{1,0:T(8,128)(2,1)S(1)} %constant_dynamic-update-slice_fusion.4), kind=kOutput, calls=%fused_computation.52 | convolution fusion | flops 8589934592 | bytes 27262976 | tf_op jit(solution)/shard_map/dot_general | solution.py:75
  114.7 7.0 %collective-permute-done.7 = bf16[128,4096]{1,0:T(8,128)(2,1)S(1)} collective-permute-done((bf16[128,4096]{1,0:T(8,128)(2,1)S(1)}, bf16[128,4096]{1,0:T(8,128)(2,1)S(1)}, u32[]{:S(2)}, u32[]{:S(2)}) %collective-permute-start.7) | collective-permute-done | bytes 1048608 | tf_op jit(solution)/shard_map/ppermute | solution.py:73
  121.7 24.5 %collective-permute-done.9 = bf16[128,4096]{1,0:T(8,128)(2,1)S(1)} collective-permute-done((bf16[128,4096]{1,0:T(8,128)(2,1)S(1)}, bf16[128,4096]{1,0:T(8,128)(2,1)S(1)}, u32[]{:S(2)}, u32[]{:S(2)}) %collective-permute-start.9) | collective-permute-done | bytes 1048608 | tf_op jit(solution)/shard_map/ppermute | solution.py:73
  146.1 41.3 %collective-permute-done.8 = bf16[128,4096]{1,0:T(8,128)(2,1)S(1)} collective-permute-done((bf16[128,4096]{1,0:T(8,128)(2,1)S(1)}, bf16[128,4096]{1,0:T(8,128)(2,1)S(1)}, u32[]{:S(2)}, u32[]{:S(2)}) %collective-permute-start.8) | collective-permute-done | bytes 1048608 | tf_op jit(solution)/shard_map/ppermute | solution.py:73
  192.8 9.6 %multiply_convert_fusion = bf16[4096,1024]{1,0:T(8,128)(2,1)} fusion(f32[4096,1024]{1,0:T(8,128)} %fusion.20), kind=kLoop, calls=%fused_computation | loop fusion | flops 8388608 | bytes 25165824 | tf_op jit(solution)/shard_map/convert_element_type | solution.py:106
  202.4 71.3 %all-gather.6.cloned.1.call-done = bf16[1024,4096]{1,0:T(8,128)(2,1)} async-done(((bf16[128,4096]{1,0:T(8,128)(2,1)}), bf16[1024,4096]{1,0:T(8,128)(2,1)}) %all-gather.6.cloned.1.call-update) | async-done | bytes 8388624 | tf_op jit(solution)/shard_map/all_gather | solution.py:85
  273.6 12.8 %fusion.22 = f32[1024,1024]{1,0:T(8,128)S(1)} fusion(bf16[1024,4096]{1,0:T(8,128)(2,1)} %all-gather.6.cloned.1.call-done, bf16[1024,4096]{1,0:T(8,128)(2,1)} %param.11), kind=kOutput, calls=%fused_computation.54 | convolution fusion | flops 8589934592 | bytes 20971520 | tf_op jit(solution)/shard_map/dot_general | solution.py:91
  290.4 13.7 %fusion.21 = f32[1024,4096]{1,0:T(8,128)} fusion(bf16[1024,1024]{1,0:T(8,128)(2,1)} %constant_dynamic-update-slice_fusion, bf16[1024,4096]{1,0:T(8,128)(2,1)S(1)} %copy-done.4), kind=kOutput, calls=%fused_computation.53 | convolution fusion | flops 8589934592 | bytes 27262976 | tf_op jit(solution)/shard_map/dot_general | solution.py:87
  304.1 8.8 %collective-permute-done.10 = f32[256,1024]{1,0:T(8,128)S(1)} collective-permute-done((f32[256,1024]{1,0:T(8,128)S(1)}, f32[256,1024]{1,0:T(8,128)S(1)}, u32[]{:S(2)}, u32[]{:S(2)}) %collective-permute-start.10) | collective-permute-done | bytes 1048608 | tf_op jit(solution)/shard_map/ppermute | solution.py:35
  312.9 22.8 %collective-permute-done.12 = f32[256,1024]{1,0:T(8,128)S(1)} collective-permute-done((f32[256,1024]{1,0:T(8,128)S(1)}, f32[256,1024]{1,0:T(8,128)S(1)}, u32[]{:S(2)}, u32[]{:S(2)}) %collective-permute-start.12) | collective-permute-done | bytes 1048608 | tf_op jit(solution)/shard_map/ppermute | solution.py:35
  336.6 19.9 %all-gather.8.cloned.1.call-done = bf16[1024,4096]{1,0:T(8,128)(2,1)} async-done(((bf16[128,4096]{1,0:T(8,128)(2,1)}), bf16[1024,4096]{1,0:T(8,128)(2,1)}) %all-gather.8.cloned.1.call-update) | async-done | bytes 8388624 | tf_op jit(solution)/shard_map/all_gather | solution.py:86
  356.4 12.6 %fusion.23 = f32[1024,1024]{1,0:T(8,128)S(1)} fusion(bf16[1024,4096]{1,0:T(8,128)(2,1)} %all-gather.8.cloned.1.call-done, bf16[1024,4096]{1,0:T(8,128)(2,1)} %param.12), kind=kOutput, calls=%fused_computation.55 | convolution fusion | flops 8589934592 | bytes 20971520 | tf_op jit(solution)/shard_map/dot_general | solution.py:94
  373.9 15.6 %multiply_convert_fusion.1 = bf16[1024,4096]{1,0:T(8,128)(2,1)} fusion(bf16[1024,1024]{1,0:T(8,128)(2,1)} %constant_dynamic-update-slice_fusion, bf16[1024,4096]{1,0:T(8,128)(2,1)} %all-gather.8.cloned.1.call-done), kind=kOutput, calls=%fused_computation.1 | convolution fusion | flops 8598323200 | bytes 18874368 | tf_op jit(solution)/shard_map/dot_general | solution.py:99
  389.5 4.0 multiply_convert_fusion.2
  396.6 22.8 %collective-permute-done.15 = f32[256,1024]{1,0:T(8,128)S(1)} collective-permute-done((f32[256,1024]{1,0:T(8,128)S(1)}, f32[256,1024]{1,0:T(8,128)S(1)}, u32[]{:S(2)}, u32[]{:S(2)}) %collective-permute-start.15) | collective-permute-done | bytes 1048608 | tf_op jit(solution)/shard_map/ppermute | solution.py:35
  (64 shorter events, 44.2 us)
Async XLA Ops:
  7.2 84.2 %all-gather.4.cloned.1.call-start = ((), (), s32[]{:S(2)}) async-start(), calls=%async_computation | async-start | bytes 9437184 | tf_op jit(solution)/shard_map/all_gather | solution.py:45
  10.4 263.2 %all-gather.6.cloned.1.call-start = ((), (), s32[]{:S(2)}) async-start(), calls=%async_computation.1 | async-start | bytes 9437184 | tf_op jit(solution)/shard_map/all_gather | solution.py:85
  10.5 15.0 %collective-permute-start = (bf16[256,1024]{1,0:T(8,128)(2,1)S(1)}, bf16[256,1024]{1,0:T(8,128)(2,1)}, u32[]{:S(2)}, u32[]{:S(2)}) collective-permute-start(bf16[256,1024]{1,0:T(8,128)(2,1)S(1)} %copy-done.2), channel_id=1, source_target_pairs={{0,1},{1,2},{2,3},{3,0},{4,5},{5,6},{6,7},{7,4},{8,9},{9,10},{10,1... | collective-permute-start | bytes 1572872 | tf_op jit(solution)/shard_map/ppermute | solution.py:23
  12.0 24.7 %collective-permute-start.1 = (bf16[256,1024]{1,0:T(8,128)(2,1)S(1)}, bf16[256,1024]{1,0:T(8,128)(2,1)}, u32[]{:S(2)}, u32[]{:S(2)}) collective-permute-start(bf16[256,1024]{1,0:T(8,128)(2,1)S(1)} %copy-done.2), channel_id=1, source_target_pairs={{0,2},{1,3},{2,0},{3,1},{4,6},{5,7},{6,4},{7,5},{8,10},{9,11},{10,... | collective-permute-start | bytes 1572872 | tf_op jit(solution)/shard_map/ppermute | solution.py:23
  12.5 25.3 %collective-permute-start.2 = (bf16[256,1024]{1,0:T(8,128)(2,1)S(1)}, bf16[256,1024]{1,0:T(8,128)(2,1)S(1)}, u32[]{:S(2)}, u32[]{:S(2)}) collective-permute-start(bf16[256,1024]{1,0:T(8,128)(2,1)S(1)} %copy-done.2), channel_id=1, source_target_pairs={{0,3},{1,0},{2,1},{3,2},{4,7},{5,4},{6,5},{7,6},{8,11},{9,8},{10,9... | collective-permute-start | bytes 1572872 | tf_op jit(solution)/shard_map/ppermute | solution.py:23
  14.4 23.8 %copy-start.3 = (bf16[4096,1024]{1,0:T(8,128)(2,1)S(1)}, bf16[4096,1024]{1,0:T(8,128)(2,1)}, u32[]{:S(2)}) copy-start(bf16[4096,1024]{1,0:T(8,128)(2,1)} %param.13) | copy-start | bytes 25165828
  44.9 30.5 %collective-permute-start.3 = (f32[512,4096]{1,0:T(8,128)}, f32[512,4096]{1,0:T(8,128)}, u32[]{:S(2)}, u32[]{:S(2)}) collective-permute-start(f32[512,4096]{1,0:T(8,128)} %fusion.19), channel_id=1, source_target_pairs={{0,4},{4,0},{1,5},{5,1},{2,6},{6,2},{3,7},{7,3},{8,12},{12,8},{9,1... | collective-permute-start | bytes 25165832 | tf_op jit(solution)/shard_map/ppermute | solution.py:63
  44.9 15.0 %collective-permute-start.4 = (bf16[256,1024]{1,0:T(8,128)(2,1)}, bf16[256,1024]{1,0:T(8,128)(2,1)}, u32[]{:S(2)}, u32[]{:S(2)}) collective-permute-start(bf16[256,1024]{1,0:T(8,128)(2,1)} %param.7), channel_id=1, source_target_pairs={{0,1},{1,2},{2,3},{3,0},{4,5},{5,6},{6,7},{7,4},{8,9},{9,10},{10,1... | collective-permute-start | bytes 1572872 | tf_op jit(solution)/shard_map/ppermute | solution.py:23
  46.1 25.6 %collective-permute-start.5 = (bf16[256,1024]{1,0:T(8,128)(2,1)}, bf16[256,1024]{1,0:T(8,128)(2,1)}, u32[]{:S(2)}, u32[]{:S(2)}) collective-permute-start(bf16[256,1024]{1,0:T(8,128)(2,1)} %param.7), channel_id=1, source_target_pairs={{0,2},{1,3},{2,0},{3,1},{4,6},{5,7},{6,4},{7,5},{8,10},{9,11},{10,... | collective-permute-start | bytes 1572872 | tf_op jit(solution)/shard_map/ppermute | solution.py:23
  46.6 27.0 %collective-permute-start.6 = (bf16[256,1024]{1,0:T(8,128)(2,1)}, bf16[256,1024]{1,0:T(8,128)(2,1)}, u32[]{:S(2)}, u32[]{:S(2)}) collective-permute-start(bf16[256,1024]{1,0:T(8,128)(2,1)} %param.7), channel_id=1, source_target_pairs={{0,3},{1,0},{2,1},{3,2},{4,7},{5,4},{6,5},{7,6},{8,11},{9,8},{10,9... | collective-permute-start | bytes 1572872 | tf_op jit(solution)/shard_map/ppermute | solution.py:23
  94.6 27.0 %collective-permute-start.7 = (bf16[128,4096]{1,0:T(8,128)(2,1)S(1)}, bf16[128,4096]{1,0:T(8,128)(2,1)S(1)}, u32[]{:S(2)}, u32[]{:S(2)}) collective-permute-start(bf16[128,4096]{1,0:T(8,128)(2,1)S(1)} %get-tuple-element.28), channel_id=1, source_target_pairs={{0,8},{8,16},{16,24},{24,0},{1,9},{9,17},{17,25},{25,1},{2,10},{10... | collective-permute-start | bytes 3145736 | tf_op jit(solution)/shard_map/ppermute | solution.py:73
  97.2 49.0 %collective-permute-start.9 = (bf16[128,4096]{1,0:T(8,128)(2,1)S(1)}, bf16[128,4096]{1,0:T(8,128)(2,1)S(1)}, u32[]{:S(2)}, u32[]{:S(2)}) collective-permute-start(bf16[128,4096]{1,0:T(8,128)(2,1)S(1)} %get-tuple-element.29), channel_id=1, source_target_pairs={{0,24},{8,0},{16,8},{24,16},{1,25},{9,1},{17,9},{25,17},{2,26},{10... | collective-permute-start | bytes 3145736 | tf_op jit(solution)/shard_map/ppermute | solution.py:73
  98.0 89.4 %collective-permute-start.8 = (bf16[128,4096]{1,0:T(8,128)(2,1)S(1)}, bf16[128,4096]{1,0:T(8,128)(2,1)S(1)}, u32[]{:S(2)}, u32[]{:S(2)}) collective-permute-start(bf16[128,4096]{1,0:T(8,128)(2,1)S(1)} %get-tuple-element.30), channel_id=1, source_target_pairs={{0,16},{8,24},{16,0},{24,8},{1,17},{9,25},{17,1},{25,9},{2,18},{10... | collective-permute-start | bytes 3145736 | tf_op jit(solution)/shard_map/ppermute | solution.py:73
  114.7 74.9 %copy-start = (bf16[128,4096]{1,0:T(8,128)(2,1)S(1)}, bf16[128,4096]{1,0:T(8,128)(2,1)}, u32[]{:S(2)}) copy-start(bf16[128,4096]{1,0:T(8,128)(2,1)} %param.10) | copy-start | bytes 3145732
  114.7 74.9 %copy-start.1 = (bf16[128,4096]{1,0:T(8,128)(2,1)S(1)}, bf16[128,4096]{1,0:T(8,128)(2,1)}, u32[]{:S(2)}) copy-start(bf16[128,4096]{1,0:T(8,128)(2,1)} %param.9) | copy-start | bytes 3145732
  192.0 164.5 %all-gather.8.cloned.1.call-start = ((), (), s32[]{:S(2)}) async-start(), calls=%async_computation.2 | async-start | bytes 9437184 | tf_op jit(solution)/shard_map/all_gather | solution.py:86
  286.8 26.0 %collective-permute-start.10 = (f32[256,1024]{1,0:T(8,128)S(1)}, f32[256,1024]{1,0:T(8,128)S(1)}, u32[]{:S(2)}, u32[]{:S(2)}) collective-permute-start(f32[256,1024]{1,0:T(8,128)S(1)} %get-tuple-element.34), channel_id=1, source_target_pairs={{0,1},{1,2},{2,3},{3,0},{4,5},{5,6},{6,7},{7,4},{8,9},{9,10},{10,1... | collective-permute-start | bytes 3145736 | tf_op jit(solution)/shard_map/ppermute | solution.py:35
  288.4 47.3 %collective-permute-start.12 = (f32[256,1024]{1,0:T(8,128)S(1)}, f32[256,1024]{1,0:T(8,128)S(1)}, u32[]{:S(2)}, u32[]{:S(2)}) collective-permute-start(f32[256,1024]{1,0:T(8,128)S(1)} %get-tuple-element.35), channel_id=1, source_target_pairs={{0,3},{1,0},{2,1},{3,2},{4,7},{5,4},{6,5},{7,6},{8,11},{9,8},{10,9... | collective-permute-start | bytes 3145736 | tf_op jit(solution)/shard_map/ppermute | solution.py:35
  288.9 47.2 %collective-permute-start.11 = (f32[256,1024]{1,0:T(8,128)S(1)}, f32[256,1024]{1,0:T(8,128)S(1)}, u32[]{:S(2)}, u32[]{:S(2)}) collective-permute-start(f32[256,1024]{1,0:T(8,128)S(1)} %get-tuple-element.36), channel_id=1, source_target_pairs={{0,2},{1,3},{2,0},{3,1},{4,6},{5,7},{6,4},{7,5},{8,10},{9,11},{10,... | collective-permute-start | bytes 3145736 | tf_op jit(solution)/shard_map/ppermute | solution.py:35
  369.1 20.4 %slice-start = ((s8[16777216]{0:T(1024)(128)(4,1)}), s8[4194304]{0:T(1024)(128)(4,1)S(1)}, s32[]{:S(2)}) async-start(s8[16777216]{0:T(1024)(128)(4,1)} %bitcast.60), calls=%async_computation.3 | async-start | bytes 8388608
  370.4 26.2 %collective-permute-start.13 = (f32[256,1024]{1,0:T(8,128)}, f32[256,1024]{1,0:T(8,128)S(1)}, u32[]{:S(2)}, u32[]{:S(2)}) collective-permute-start(f32[256,1024]{1,0:T(8,128)} %get-tuple-element.31), channel_id=1, source_target_pairs={{0,1},{1,2},{2,3},{3,0},{4,5},{5,6},{6,7},{7,4},{8,9},{9,10},{10,1... | collective-permute-start | bytes 3145736 | tf_op jit(solution)/shard_map/ppermute | solution.py:35
  371.8 47.6 %collective-permute-start.15 = (f32[256,1024]{1,0:T(8,128)S(1)}, f32[256,1024]{1,0:T(8,128)S(1)}, u32[]{:S(2)}, u32[]{:S(2)}) collective-permute-start(f32[256,1024]{1,0:T(8,128)S(1)} %get-tuple-element.32), channel_id=1, source_target_pairs={{0,3},{1,0},{2,1},{3,2},{4,7},{5,4},{6,5},{7,6},{8,11},{9,8},{10,9... | collective-permute-start | bytes 3145736 | tf_op jit(solution)/shard_map/ppermute | solution.py:35
  372.4 17.1 %slice-start.3 = ((s8[16777216]{0:T(1024)(128)(4,1)}), s8[4194304]{0:T(1024)(128)(4,1)S(1)}, s32[]{:S(2)}) async-start(s8[16777216]{0:T(1024)(128)(4,1)} %bitcast.60), calls=%async_computation.6 | async-start | bytes 8388608
  372.4 47.3 %collective-permute-start.14 = (f32[256,1024]{1,0:T(8,128)S(1)}, f32[256,1024]{1,0:T(8,128)}, u32[]{:S(2)}, u32[]{:S(2)}) collective-permute-start(f32[256,1024]{1,0:T(8,128)S(1)} %get-tuple-element.33), channel_id=1, source_target_pairs={{0,2},{1,3},{2,0},{3,1},{4,6},{5,7},{6,4},{7,5},{8,10},{9,11},{10,... | collective-permute-start | bytes 3145736 | tf_op jit(solution)/shard_map/ppermute | solution.py:35
  (4 other events, 54.2 us)
Sparse Core Ops, SparseCore 0:
  10.6 80.7 all-gather.3
  192.1 81.4 all-gather.5
  275.8 80.5 all-gather.7

commit v7 on v6

--- a/solution.py
+++ b/solution.py
@@ -72,16 +72,15 @@
         piece = lax.dynamic_index_in_dim(chip_sum, (z + s) % chips, axis=0, keepdims=False)
         piece = lax.ppermute(piece.astype(jnp.bfloat16), "z", shift_perm(chips, s))
         hid_rows = hid_rows + piece.astype(jnp.float32)
-    acc_down = lax.dot_general(
-        hidden_act, grad_full, CONTRACT_FIRST, preferred_element_type=jnp.float32
-    )
-    hid_rows, acc_down = lax.optimization_barrier((hid_rows, acc_down))
 
     gate_local = (
         hid_rows * up_float * sigmoid_gate * (1.0 + gate_float * (1.0 - sigmoid_gate))
     ).astype(jnp.bfloat16)
     up_local = (hid_rows * silu_gate).astype(jnp.bfloat16)
 
+    acc_down = lax.dot_general(
+        hidden_act, grad_full, CONTRACT_FIRST, preferred_element_type=jnp.float32
+    )
     gate_delta = lax.all_gather(gate_local, ROW, axis=0, tiled=True)
     up_delta = lax.all_gather(up_local, ROW, axis=0, tiled=True)
     acc_gate = lax.dot_general(

time: 433 us -> 436 us (level)
  waiting for transfers between devices: 267 us -> 277 us
  other arithmetic: 24.2 us -> 15.7 us
    ppermute x3, waiting for transfers between devices: 72.7 us -> 87.6 us  [body(): piece = lax.ppermute(piece.astype(jnp.bfloat16), 'z', shift_perm(chips, s))]
    convert_element_type x1 -> x0, other arithmetic: 9.6 us -> none  [body(): (acc_down * factor).astype(jnp.bfloat16)]
    all_gather x1, waiting for transfers between devices: 71.3 us -> 66.3 us  [body(): gate_delta = lax.all_gather(gate_local, ROW, axis=0, tiled=True)]
  transfers between devices with their start and end apart: 19 -> 19, of which waited for: 16 -> 16; matrix products, arithmetic and copies ran while one was open for 24% -> 21% of each run, Pallas kernels for 0% -> 0%
where the time goes in v7:
time: 436 us; the launch traced here: 431 us
  waiting for transfers between devices  277 us (64%)
  matrix products  87.6 us (20%)
  starting transfers between devices  18.9 us (4%)
  local copies, waits for them, and re-layouts  18 us (4%)
  other arithmetic  15.7 us (4%)
  between operations  13.9 us (3%)
    ppermute x3, waiting for transfers between devices, body(): piece = lax.ppermute(piece.astype(jnp.bfloat16), 'z', shift_perm(chips, s))  87.6 us
    all_gather x1, waiting for transfers between devices, body(): gate_delta = lax.all_gather(gate_local, ROW, axis=0, tiled=True)  66.3 us
    ppermute x6, waiting for transfers between devices, reduce_scatter_col(): total = total + lax.ppermute(piece, 'col', shift_perm(n, s))  58.3 us
    ppermute x6, waiting for transfers between devices, gather_col(): part = lax.ppermute(block, 'col', shift_perm(n, s))  40.2 us
    all_gather x1, waiting for transfers between devices, body(): up_delta = lax.all_gather(up_local, ROW, axis=0, tiled=True)  20 us
    dot_general x1, matrix products, body(): lax.dot_general(act_full, up_delta, CONTRACT_FIRST, preferred_element_typ...  15.6 us
    dot_general x1, matrix products, body(): lax.dot_general(hidden_act, grad_full, CONTRACT_FIRST, preferred_element_...  14.6 us
    dot_general x1, matrix products, body(): lax.dot_general(act_full, gate_delta, CONTRACT_FIRST, preferred_element_t...  13.7 us
  transfers between devices with their start and end apart: 19, of which 16 were waited for; matrix products, arithmetic and copies ran while one was open for 21% of the time, Pallas kernels for 0%

profile of v7, /device:TPU:10, one launch (start us, length us, event | category | flops | bytes accessed | tf_op | source)
XLA Modules:
  0.0 431.4 jit_solution(5525726142895538213)
XLA Ops:
  7.2 3.2 fusion
  14.4 11.0 %collective-permute-done = bf16[256,1024]{1,0:T(8,128)(2,1)} collective-permute-done((bf16[256,1024]{1,0:T(8,128)(2,1)S(1)}, bf16[256,1024]{1,0:T(8,128)(2,1)}, u32[]{:S(2)}, u32[]{:S(2)}) %collective-permute-start) | collective-permute-done | bytes 524320 | tf_op jit(solution)/shard_map/ppermute | solution.py:23
  26.5 10.2 %collective-permute-done.1 = bf16[256,1024]{1,0:T(8,128)(2,1)} collective-permute-done((bf16[256,1024]{1,0:T(8,128)(2,1)S(1)}, bf16[256,1024]{1,0:T(8,128)(2,1)}, u32[]{:S(2)}, u32[]{:S(2)}) %collective-permute-start.1) | collective-permute-done | bytes 524320 | tf_op jit(solution)/shard_map/ppermute | solution.py:23
  38.2 6.8 %fusion.19 = f32[512,4096]{1,0:T(8,128)} fusion(bf16[512,1024]{1,0:T(8,128)(2,1)S(1)} %bitcast.74, bf16[4096,1024]{1,0:T(8,128)(2,1)S(1)} %copy-done.2), kind=kOutput, calls=%fused_computation.51 | convolution fusion | flops 4294967296 | bytes 17825792 | tf_op jit(solution)/shard_map/dot_general | solution.py:59
  50.9 9.0 %collective-permute-done.4 = bf16[256,1024]{1,0:T(8,128)(2,1)} collective-permute-done((bf16[256,1024]{1,0:T(8,128)(2,1)}, bf16[256,1024]{1,0:T(8,128)(2,1)}, u32[]{:S(2)}, u32[]{:S(2)}) %collective-permute-start.4) | collective-permute-done | bytes 524320 | tf_op jit(solution)/shard_map/ppermute | solution.py:23
  61.9 9.9 %collective-permute-done.5 = bf16[256,1024]{1,0:T(8,128)(2,1)} collective-permute-done((bf16[256,1024]{1,0:T(8,128)(2,1)}, bf16[256,1024]{1,0:T(8,128)(2,1)}, u32[]{:S(2)}, u32[]{:S(2)}) %collective-permute-start.5) | collective-permute-done | bytes 524320 | tf_op jit(solution)/shard_map/ppermute | solution.py:23
  75.5 11.5 %convolution_add_fusion = f32[512,4096]{1,0:T(8,128)} fusion(f32[512,4096]{1,0:T(8,128)} %collective-permute-done.3, bf16[512,1024]{1,0:T(8,128)(2,1)S(1)} %bitcast.73, bf16[4096,1024]{1,0:T(8,128)(2,1)} %param.13), kind=kOutput, calls=%fused_computation.3 | convolution fusion | flops 4297064448 | bytes 26214400 | tf_op jit(solution)/shard_map/dot_general | solution.py:64
  87.0 4.3 %all-gather.4.cloned.1.call-done = bf16[1024,4096]{1,0:T(8,128)(2,1)} async-done(((bf16[128,4096]{1,0:T(8,128)(2,1)}), bf16[1024,4096]{1,0:T(8,128)(2,1)}) %all-gather.4.cloned.1.call-update) | async-done | bytes 8388624 | tf_op jit(solution)/shard_map/all_gather | solution.py:45
  91.3 4.6 %fusion.10 = (bf16[128,4096]{1,0:T(8,128)(2,1)}, bf16[128,4096]{1,0:T(8,128)(2,1)}, bf16[128,4096]{1,0:T(8,128)(2,1)}) fusion(f32[4,128,4096]{2,1,0:T(8,128)} %bitcast.71, s32[]{:T(128)S(6)} %select_n.115, s32[]{:T(128)S(6)} %select_n.119, s32[]{:T(128)S(6)} %select_n.117), kind=kLoop, calls=%fused_computation.24 | loop fusion | bytes 6291468 | tf_op jit(solution)/shard_map/convert_element_type | solution.py:73
  101.4 21.9 %collective-permute-done.7 = bf16[128,4096]{1,0:T(8,128)(2,1)} collective-permute-done((bf16[128,4096]{1,0:T(8,128)(2,1)}, bf16[128,4096]{1,0:T(8,128)(2,1)}, u32[]{:S(2)}, u32[]{:S(2)}) %collective-permute-start.7) | collective-permute-done | bytes 1048608 | tf_op jit(solution)/shard_map/ppermute | solution.py:73
  123.2 24.5 %collective-permute-done.9 = bf16[128,4096]{1,0:T(8,128)(2,1)} collective-permute-done((bf16[128,4096]{1,0:T(8,128)(2,1)}, bf16[128,4096]{1,0:T(8,128)(2,1)}, u32[]{:S(2)}, u32[]{:S(2)}) %collective-permute-start.9) | collective-permute-done | bytes 1048608 | tf_op jit(solution)/shard_map/ppermute | solution.py:73
  147.7 41.3 %collective-permute-done.8 = bf16[128,4096]{1,0:T(8,128)(2,1)} collective-permute-done((bf16[128,4096]{1,0:T(8,128)(2,1)}, bf16[128,4096]{1,0:T(8,128)(2,1)}, u32[]{:S(2)}, u32[]{:S(2)}) %collective-permute-start.8) | collective-permute-done | bytes 1048608 | tf_op jit(solution)/shard_map/ppermute | solution.py:73
  189.0 5.6 %multiply_convert_fusion.3 = (bf16[128,4096]{1,0:T(8,128)(2,1)}, bf16[128,4096]{1,0:T(8,128)(2,1)}) fusion(bf16[128,4096]{1,0:T(8,128)(2,1)} %param.9, bf16[128,4096]{1,0:T(8,128)(2,1)} %collective-permute-done.9, bf16[128,4096]{1,0:T(8,128)(2,1)} %collective-permute-done.8, bf16[128,4096]{1,0:T(8,128)(2,1)} %collective-permute-done.7, ...), kind=kLoop, calls=%fused_computation.20 | loop fusion | flops 11010048 | bytes 9437188 | tf_op jit(solution)/shard_map/convert_element_type | solution.py:79
  195.5 14.6 %multiply_convert_fusion = bf16[4096,1024]{1,0:T(8,128)(2,1)} fusion(bf16[1024,4096]{1,0:T(8,128)(2,1)} %all-gather.4.cloned.1.call-done, bf16[1024,1024]{1,0:T(8,128)(2,1)S(1)} %constant_dynamic-update-slice_fusion.4), kind=kOutput, calls=%fused_computation | convolution fusion | flops 8598323200 | bytes 18874368 | tf_op jit(solution)/shard_map/dot_general | solution.py:81
  210.0 66.3 %all-gather.6.cloned.1.call-done = bf16[1024,4096]{1,0:T(8,128)(2,1)} async-done(((bf16[128,4096]{1,0:T(8,128)(2,1)}), bf16[1024,4096]{1,0:T(8,128)(2,1)}) %all-gather.6.cloned.1.call-update) | async-done | bytes 8388624 | tf_op jit(solution)/shard_map/all_gather | solution.py:84
  276.3 12.8 %fusion.21 = f32[1024,1024]{1,0:T(8,128)S(1)} fusion(bf16[1024,4096]{1,0:T(8,128)(2,1)} %all-gather.6.cloned.1.call-done, bf16[1024,4096]{1,0:T(8,128)(2,1)} %param.11), kind=kOutput, calls=%fused_computation.53 | convolution fusion | flops 8589934592 | bytes 20971520 | tf_op jit(solution)/shard_map/dot_general | solution.py:90
  293.0 13.7 %fusion.20 = f32[1024,4096]{1,0:T(8,128)} fusion(bf16[1024,1024]{1,0:T(8,128)(2,1)} %constant_dynamic-update-slice_fusion, bf16[1024,4096]{1,0:T(8,128)(2,1)S(1)} %copy-done.3), kind=kOutput, calls=%fused_computation.52 | convolution fusion | flops 8589934592 | bytes 27262976 | tf_op jit(solution)/shard_map/dot_general | solution.py:86
  306.6 8.8 %collective-permute-done.10 = f32[256,1024]{1,0:T(8,128)S(1)} collective-permute-done((f32[256,1024]{1,0:T(8,128)S(1)}, f32[256,1024]{1,0:T(8,128)S(1)}, u32[]{:S(2)}, u32[]{:S(2)}) %collective-permute-start.10) | collective-permute-done | bytes 1048608 | tf_op jit(solution)/shard_map/ppermute | solution.py:35
  315.5 22.8 %collective-permute-done.12 = f32[256,1024]{1,0:T(8,128)S(1)} collective-permute-done((f32[256,1024]{1,0:T(8,128)S(1)}, f32[256,1024]{1,0:T(8,128)S(1)}, u32[]{:S(2)}, u32[]{:S(2)}) %collective-permute-start.12) | collective-permute-done | bytes 1048608 | tf_op jit(solution)/shard_map/ppermute | solution.py:35
  339.1 20.0 %all-gather.8.cloned.1.call-done = bf16[1024,4096]{1,0:T(8,128)(2,1)} async-done(((bf16[128,4096]{1,0:T(8,128)(2,1)}), bf16[1024,4096]{1,0:T(8,128)(2,1)}) %all-gather.8.cloned.1.call-update) | async-done | bytes 8388624 | tf_op jit(solution)/shard_map/all_gather | solution.py:85
  359.1 12.6 %fusion.22 = f32[1024,1024]{1,0:T(8,128)S(1)} fusion(bf16[1024,4096]{1,0:T(8,128)(2,1)} %all-gather.8.cloned.1.call-done, bf16[1024,4096]{1,0:T(8,128)(2,1)} %param.12), kind=kOutput, calls=%fused_computation.54 | convolution fusion | flops 8589934592 | bytes 20971520 | tf_op jit(solution)/shard_map/dot_general | solution.py:93
  376.6 15.6 %multiply_convert_fusion.1 = bf16[1024,4096]{1,0:T(8,128)(2,1)} fusion(bf16[1024,1024]{1,0:T(8,128)(2,1)} %constant_dynamic-update-slice_fusion, bf16[1024,4096]{1,0:T(8,128)(2,1)} %all-gather.8.cloned.1.call-done), kind=kOutput, calls=%fused_computation.1 | convolution fusion | flops 8598323200 | bytes 18874368 | tf_op jit(solution)/shard_map/dot_general | solution.py:98
  392.2 4.0 multiply_convert_fusion.2
  399.3 22.8 %collective-permute-done.15 = f32[256,1024]{1,0:T(8,128)S(1)} collective-permute-done((f32[256,1024]{1,0:T(8,128)S(1)}, f32[256,1024]{1,0:T(8,128)S(1)}, u32[]{:S(2)}, u32[]{:S(2)}) %collective-permute-start.15) | collective-permute-done | bytes 1048608 | tf_op jit(solution)/shard_map/ppermute | solution.py:35
  (60 shorter events, 39.6 us)
Async XLA Ops:
  7.2 84.2 %all-gather.4.cloned.1.call-start = ((), (), s32[]{:S(2)}) async-start(), calls=%async_computation | async-start | bytes 9437184 | tf_op jit(solution)/shard_map/all_gather | solution.py:45
  10.4 265.9 %all-gather.6.cloned.1.call-start = ((), (), s32[]{:S(2)}) async-start(), calls=%async_computation.1 | async-start | bytes 9437184 | tf_op jit(solution)/shard_map/all_gather | solution.py:84
  10.5 15.0 %collective-permute-start = (bf16[256,1024]{1,0:T(8,128)(2,1)S(1)}, bf16[256,1024]{1,0:T(8,128)(2,1)}, u32[]{:S(2)}, u32[]{:S(2)}) collective-permute-start(bf16[256,1024]{1,0:T(8,128)(2,1)S(1)} %copy-done.1), channel_id=1, source_target_pairs={{0,1},{1,2},{2,3},{3,0},{4,5},{5,6},{6,7},{7,4},{8,9},{9,10},{10,1... | collective-permute-start | bytes 1572872 | tf_op jit(solution)/shard_map/ppermute | solution.py:23
  12.0 24.7 %collective-permute-start.1 = (bf16[256,1024]{1,0:T(8,128)(2,1)S(1)}, bf16[256,1024]{1,0:T(8,128)(2,1)}, u32[]{:S(2)}, u32[]{:S(2)}) collective-permute-start(bf16[256,1024]{1,0:T(8,128)(2,1)S(1)} %copy-done.1), channel_id=1, source_target_pairs={{0,2},{1,3},{2,0},{3,1},{4,6},{5,7},{6,4},{7,5},{8,10},{9,11},{10,... | collective-permute-start | bytes 1572872 | tf_op jit(solution)/shard_map/ppermute | solution.py:23
  12.5 25.3 %collective-permute-start.2 = (bf16[256,1024]{1,0:T(8,128)(2,1)S(1)}, bf16[256,1024]{1,0:T(8,128)(2,1)S(1)}, u32[]{:S(2)}, u32[]{:S(2)}) collective-permute-start(bf16[256,1024]{1,0:T(8,128)(2,1)S(1)} %copy-done.1), channel_id=1, source_target_pairs={{0,3},{1,0},{2,1},{3,2},{4,7},{5,4},{6,5},{7,6},{8,11},{9,8},{10,9... | collective-permute-start | bytes 1572872 | tf_op jit(solution)/shard_map/ppermute | solution.py:23
  14.4 23.8 %copy-start.2 = (bf16[4096,1024]{1,0:T(8,128)(2,1)S(1)}, bf16[4096,1024]{1,0:T(8,128)(2,1)}, u32[]{:S(2)}) copy-start(bf16[4096,1024]{1,0:T(8,128)(2,1)} %param.13) | copy-start | bytes 25165828
  45.0 30.5 %collective-permute-start.3 = (f32[512,4096]{1,0:T(8,128)}, f32[512,4096]{1,0:T(8,128)}, u32[]{:S(2)}, u32[]{:S(2)}) collective-permute-start(f32[512,4096]{1,0:T(8,128)} %fusion.19), channel_id=1, source_target_pairs={{0,4},{4,0},{1,5},{5,1},{2,6},{6,2},{3,7},{7,3},{8,12},{12,8},{9,1... | collective-permute-start | bytes 25165832 | tf_op jit(solution)/shard_map/ppermute | solution.py:63
  45.0 15.0 %collective-permute-start.4 = (bf16[256,1024]{1,0:T(8,128)(2,1)}, bf16[256,1024]{1,0:T(8,128)(2,1)}, u32[]{:S(2)}, u32[]{:S(2)}) collective-permute-start(bf16[256,1024]{1,0:T(8,128)(2,1)} %param.7), channel_id=1, source_target_pairs={{0,1},{1,2},{2,3},{3,0},{4,5},{5,6},{6,7},{7,4},{8,9},{9,10},{10,1... | collective-permute-start | bytes 1572872 | tf_op jit(solution)/shard_map/ppermute | solution.py:23
  46.2 25.6 %collective-permute-start.5 = (bf16[256,1024]{1,0:T(8,128)(2,1)}, bf16[256,1024]{1,0:T(8,128)(2,1)}, u32[]{:S(2)}, u32[]{:S(2)}) collective-permute-start(bf16[256,1024]{1,0:T(8,128)(2,1)} %param.7), channel_id=1, source_target_pairs={{0,2},{1,3},{2,0},{3,1},{4,6},{5,7},{6,4},{7,5},{8,10},{9,11},{10,... | collective-permute-start | bytes 1572872 | tf_op jit(solution)/shard_map/ppermute | solution.py:23
  46.7 27.0 %collective-permute-start.6 = (bf16[256,1024]{1,0:T(8,128)(2,1)}, bf16[256,1024]{1,0:T(8,128)(2,1)}, u32[]{:S(2)}, u32[]{:S(2)}) collective-permute-start(bf16[256,1024]{1,0:T(8,128)(2,1)} %param.7), channel_id=1, source_target_pairs={{0,3},{1,0},{2,1},{3,2},{4,7},{5,4},{6,5},{7,6},{8,11},{9,8},{10,9... | collective-permute-start | bytes 1572872 | tf_op jit(solution)/shard_map/ppermute | solution.py:23
  87.0 102.0 %copy-start = (bf16[128,4096]{1,0:T(8,128)(2,1)S(1)}, bf16[128,4096]{1,0:T(8,128)(2,1)}, u32[]{:S(2)}) copy-start(bf16[128,4096]{1,0:T(8,128)(2,1)} %param.10) | copy-start | bytes 3145732
  96.0 27.3 %collective-permute-start.7 = (bf16[128,4096]{1,0:T(8,128)(2,1)}, bf16[128,4096]{1,0:T(8,128)(2,1)}, u32[]{:S(2)}, u32[]{:S(2)}) collective-permute-start(bf16[128,4096]{1,0:T(8,128)(2,1)} %get-tuple-element.26), channel_id=1, source_target_pairs={{0,8},{8,16},{16,24},{24,0},{1,9},{9,17},{17,25},{25,1},{2,10},{10... | collective-permute-start | bytes 3145736 | tf_op jit(solution)/shard_map/ppermute | solution.py:73
  98.5 49.3 %collective-permute-start.9 = (bf16[128,4096]{1,0:T(8,128)(2,1)}, bf16[128,4096]{1,0:T(8,128)(2,1)}, u32[]{:S(2)}, u32[]{:S(2)}) collective-permute-start(bf16[128,4096]{1,0:T(8,128)(2,1)} %get-tuple-element.27), channel_id=1, source_target_pairs={{0,24},{8,0},{16,8},{24,16},{1,25},{9,1},{17,9},{25,17},{2,26},{10... | collective-permute-start | bytes 3145736 | tf_op jit(solution)/shard_map/ppermute | solution.py:73
  99.0 90.0 %collective-permute-start.8 = (bf16[128,4096]{1,0:T(8,128)(2,1)}, bf16[128,4096]{1,0:T(8,128)(2,1)}, u32[]{:S(2)}, u32[]{:S(2)}) collective-permute-start(bf16[128,4096]{1,0:T(8,128)(2,1)} %get-tuple-element.28), channel_id=1, source_target_pairs={{0,16},{8,24},{16,0},{24,8},{1,17},{9,25},{17,1},{25,9},{2,18},{10... | collective-permute-start | bytes 3145736 | tf_op jit(solution)/shard_map/ppermute | solution.py:73
  194.7 164.5 %all-gather.8.cloned.1.call-start = ((), (), s32[]{:S(2)}) async-start(), calls=%async_computation.2 | async-start | bytes 9437184 | tf_op jit(solution)/shard_map/all_gather | solution.py:85
  289.4 26.0 %collective-permute-start.10 = (f32[256,1024]{1,0:T(8,128)S(1)}, f32[256,1024]{1,0:T(8,128)S(1)}, u32[]{:S(2)}, u32[]{:S(2)}) collective-permute-start(f32[256,1024]{1,0:T(8,128)S(1)} %get-tuple-element.32), channel_id=1, source_target_pairs={{0,1},{1,2},{2,3},{3,0},{4,5},{5,6},{6,7},{7,4},{8,9},{9,10},{10,1... | collective-permute-start | bytes 3145736 | tf_op jit(solution)/shard_map/ppermute | solution.py:35
  290.9 47.3 %collective-permute-start.12 = (f32[256,1024]{1,0:T(8,128)S(1)}, f32[256,1024]{1,0:T(8,128)S(1)}, u32[]{:S(2)}, u32[]{:S(2)}) collective-permute-start(f32[256,1024]{1,0:T(8,128)S(1)} %get-tuple-element.33), channel_id=1, source_target_pairs={{0,3},{1,0},{2,1},{3,2},{4,7},{5,4},{6,5},{7,6},{8,11},{9,8},{10,9... | collective-permute-start | bytes 3145736 | tf_op jit(solution)/shard_map/ppermute | solution.py:35
  291.5 47.2 %collective-permute-start.11 = (f32[256,1024]{1,0:T(8,128)S(1)}, f32[256,1024]{1,0:T(8,128)S(1)}, u32[]{:S(2)}, u32[]{:S(2)}) collective-permute-start(f32[256,1024]{1,0:T(8,128)S(1)} %get-tuple-element.34), channel_id=1, source_target_pairs={{0,2},{1,3},{2,0},{3,1},{4,6},{5,7},{6,4},{7,5},{8,10},{9,11},{10,... | collective-permute-start | bytes 3145736 | tf_op jit(solution)/shard_map/ppermute | solution.py:35
  371.8 20.4 %slice-start = ((s8[16777216]{0:T(1024)(128)(4,1)}), s8[4194304]{0:T(1024)(128)(4,1)S(1)}, s32[]{:S(2)}) async-start(s8[16777216]{0:T(1024)(128)(4,1)} %bitcast.64), calls=%async_computation.3 | async-start | bytes 8388608
  373.1 26.2 %collective-permute-start.13 = (f32[256,1024]{1,0:T(8,128)}, f32[256,1024]{1,0:T(8,128)S(1)}, u32[]{:S(2)}, u32[]{:S(2)}) collective-permute-start(f32[256,1024]{1,0:T(8,128)} %get-tuple-element.29), channel_id=1, source_target_pairs={{0,1},{1,2},{2,3},{3,0},{4,5},{5,6},{6,7},{7,4},{8,9},{9,10},{10,1... | collective-permute-start | bytes 3145736 | tf_op jit(solution)/shard_map/ppermute | solution.py:35
  374.5 47.5 %collective-permute-start.15 = (f32[256,1024]{1,0:T(8,128)S(1)}, f32[256,1024]{1,0:T(8,128)S(1)}, u32[]{:S(2)}, u32[]{:S(2)}) collective-permute-start(f32[256,1024]{1,0:T(8,128)S(1)} %get-tuple-element.30), channel_id=1, source_target_pairs={{0,3},{1,0},{2,1},{3,2},{4,7},{5,4},{6,5},{7,6},{8,11},{9,8},{10,9... | collective-permute-start | bytes 3145736 | tf_op jit(solution)/shard_map/ppermute | solution.py:35
  375.1 17.0 %slice-start.2 = ((s8[16777216]{0:T(1024)(128)(4,1)}), s8[4194304]{0:T(1024)(128)(4,1)S(1)}, s32[]{:S(2)}) async-start(s8[16777216]{0:T(1024)(128)(4,1)} %bitcast.64), calls=%async_computation.5 | async-start | bytes 8388608
  375.1 17.0 %slice-start.3 = ((s8[16777216]{0:T(1024)(128)(4,1)}), s8[4194304]{0:T(1024)(128)(4,1)S(1)}, s32[]{:S(2)}) async-start(s8[16777216]{0:T(1024)(128)(4,1)} %bitcast.64), calls=%async_computation.6 | async-start | bytes 8388608
  375.1 47.3 %collective-permute-start.14 = (f32[256,1024]{1,0:T(8,128)S(1)}, f32[256,1024]{1,0:T(8,128)}, u32[]{:S(2)}, u32[]{:S(2)}) collective-permute-start(f32[256,1024]{1,0:T(8,128)S(1)} %get-tuple-element.31), channel_id=1, source_target_pairs={{0,2},{1,3},{2,0},{3,1},{4,6},{5,7},{6,4},{7,5},{8,10},{9,11},{10,... | collective-permute-start | bytes 3145736 | tf_op jit(solution)/shard_map/ppermute | solution.py:35
  (3 other events, 37.0 us)
Sparse Core Ops, SparseCore 0:
  10.6 80.7 all-gather.3
  194.8 81.4 all-gather.5
  278.5 80.5 all-gather.7

commit v8 on v7

--- a/solution.py
+++ b/solution.py
@@ -25,14 +25,15 @@
     return full
 
 
-def reduce_scatter_col(partial):
+def reduce_scatter_col(partial, send_dtype=jnp.float32):
     n = lax.axis_size("col")
     c = lax.axis_index("col")
     blocks = partial.reshape((n, -1) + partial.shape[1:])
     total = lax.dynamic_index_in_dim(blocks, c, axis=0, keepdims=False)
     for s in range(1, n):
         piece = lax.dynamic_index_in_dim(blocks, (c + s) % n, axis=0, keepdims=False)
-        total = total + lax.ppermute(piece, "col", shift_perm(n, s))
+        piece = lax.ppermute(piece.astype(send_dtype), "col", shift_perm(n, s))
+        total = total + piece.astype(jnp.float32)
     return total
 
 
@@ -94,7 +95,7 @@
         up_delta, up_weight, CONTRACT_LAST, preferred_element_type=jnp.float32
     )
     up_delta, input_up = lax.optimization_barrier((up_delta, input_up))
-    input_up = reduce_scatter_col(input_up)
+    input_up = reduce_scatter_col(input_up, jnp.bfloat16)
     acc_up = lax.dot_general(act_full, up_delta, CONTRACT_FIRST, preferred_element_type=jnp.float32)
     input_rows = (input_gate + input_up).astype(jnp.bfloat16)
     factor = float(tokens_all) ** (-0.5)

time: 436 us -> 411 us (0.943)
  waiting for transfers between devices: 277 us -> 255 us
    ppermute x6, waiting for transfers between devices: 58.3 us -> 35.7 us  [reduce_scatter_col(): piece = lax.ppermute(piece.astype(send_dtype), 'col', shift_perm(n, s))]
  transfers between devices with their start and end apart: 19 -> 19, of which waited for: 16 -> 15; matrix products, arithmetic and copies ran while one was open for 21% -> 22% of each run, Pallas kernels for 0% -> 0%
where the time goes in v8:
time: 411 us; the launch traced here: 407 us
  waiting for transfers between devices  255 us (62%)
  matrix products  87.6 us (21%)
  starting transfers between devices  18.9 us (5%)
  local copies, waits for them, and re-layouts  17 us (4%)
  other arithmetic  14.4 us (4%)
  between operations  14 us (3%)
    ppermute x3, waiting for transfers between devices, body(): piece = lax.ppermute(piece.astype(jnp.bfloat16), 'z', shift_perm(chips, s))  87.6 us
    all_gather x1, waiting for transfers between devices, body(): gate_delta = lax.all_gather(gate_local, ROW, axis=0, tiled=True)  66.3 us
    ppermute x6, waiting for transfers between devices, gather_col(): part = lax.ppermute(block, 'col', shift_perm(n, s))  40.2 us
    ppermute x6, waiting for transfers between devices, reduce_scatter_col(): piece = lax.ppermute(piece.astype(send_dtype), 'col', shift_perm(n, s))  35.7 us
    all_gather x1, waiting for transfers between devices, body(): up_delta = lax.all_gather(up_local, ROW, axis=0, tiled=True)  20 us
    dot_general x1, matrix products, body(): lax.dot_general(act_full, up_delta, CONTRACT_FIRST, preferred_element_typ...  15.6 us
    dot_general x1, matrix products, body(): lax.dot_general(hidden_act, grad_full, CONTRACT_FIRST, preferred_element_...  14.6 us
    dot_general x1, matrix products, body(): lax.dot_general(act_full, gate_delta, CONTRACT_FIRST, preferred_element_t...  13.7 us
  transfers between devices with their start and end apart: 19, of which 15 were waited for; matrix products, arithmetic and copies ran while one was open for 22% of the time, Pallas kernels for 0%

profile of v8, /device:TPU:10, one launch (start us, length us, event | category | flops | bytes accessed | tf_op | source)
XLA Modules:
  0.0 406.6 jit_solution(13675910228461109038)
XLA Ops:
  7.2 3.2 fusion
  14.4 11.0 %collective-permute-done = bf16[256,1024]{1,0:T(8,128)(2,1)} collective-permute-done((bf16[256,1024]{1,0:T(8,128)(2,1)S(1)}, bf16[256,1024]{1,0:T(8,128)(2,1)}, u32[]{:S(2)}, u32[]{:S(2)}) %collective-permute-start) | collective-permute-done | bytes 524320 | tf_op jit(solution)/shard_map/ppermute | solution.py:23
  26.5 10.2 %collective-permute-done.1 = bf16[256,1024]{1,0:T(8,128)(2,1)} collective-permute-done((bf16[256,1024]{1,0:T(8,128)(2,1)S(1)}, bf16[256,1024]{1,0:T(8,128)(2,1)}, u32[]{:S(2)}, u32[]{:S(2)}) %collective-permute-start.1) | collective-permute-done | bytes 524320 | tf_op jit(solution)/shard_map/ppermute | solution.py:23
  38.2 6.8 %fusion.22 = f32[512,4096]{1,0:T(8,128)} fusion(bf16[512,1024]{1,0:T(8,128)(2,1)S(1)} %bitcast.74, bf16[4096,1024]{1,0:T(8,128)(2,1)S(1)} %copy-done.2), kind=kOutput, calls=%fused_computation.54 | convolution fusion | flops 4294967296 | bytes 17825792 | tf_op jit(solution)/shard_map/dot_general | solution.py:60
  50.9 9.0 %collective-permute-done.4 = bf16[256,1024]{1,0:T(8,128)(2,1)} collective-permute-done((bf16[256,1024]{1,0:T(8,128)(2,1)}, bf16[256,1024]{1,0:T(8,128)(2,1)}, u32[]{:S(2)}, u32[]{:S(2)}) %collective-permute-start.4) | collective-permute-done | bytes 524320 | tf_op jit(solution)/shard_map/ppermute | solution.py:23
  61.9 9.9 %collective-permute-done.5 = bf16[256,1024]{1,0:T(8,128)(2,1)} collective-permute-done((bf16[256,1024]{1,0:T(8,128)(2,1)}, bf16[256,1024]{1,0:T(8,128)(2,1)}, u32[]{:S(2)}, u32[]{:S(2)}) %collective-permute-start.5) | collective-permute-done | bytes 524320 | tf_op jit(solution)/shard_map/ppermute | solution.py:23
  75.5 11.5 %convolution_add_fusion = f32[512,4096]{1,0:T(8,128)} fusion(f32[512,4096]{1,0:T(8,128)} %collective-permute-done.3, bf16[512,1024]{1,0:T(8,128)(2,1)S(1)} %bitcast.73, bf16[4096,1024]{1,0:T(8,128)(2,1)} %param.13), kind=kOutput, calls=%fused_computation.3 | convolution fusion | flops 4297064448 | bytes 26214400 | tf_op jit(solution)/shard_map/dot_general | solution.py:65
  87.0 4.3 %all-gather.4.cloned.1.call-done = bf16[1024,4096]{1,0:T(8,128)(2,1)} async-done(((bf16[128,4096]{1,0:T(8,128)(2,1)}), bf16[1024,4096]{1,0:T(8,128)(2,1)}) %all-gather.4.cloned.1.call-update) | async-done | bytes 8388624 | tf_op jit(solution)/shard_map/all_gather | solution.py:46
  91.3 4.6 %fusion.10 = (bf16[128,4096]{1,0:T(8,128)(2,1)}, bf16[128,4096]{1,0:T(8,128)(2,1)}, bf16[128,4096]{1,0:T(8,128)(2,1)}) fusion(f32[4,128,4096]{2,1,0:T(8,128)} %bitcast.69, s32[]{:T(128)S(6)} %select_n.115, s32[]{:T(128)S(6)} %select_n.119, s32[]{:T(128)S(6)} %select_n.117), kind=kLoop, calls=%fused_computation.24 | loop fusion | bytes 6291468 | tf_op jit(solution)/shard_map/convert_element_type | solution.py:74
  101.4 21.9 %collective-permute-done.7 = bf16[128,4096]{1,0:T(8,128)(2,1)} collective-permute-done((bf16[128,4096]{1,0:T(8,128)(2,1)}, bf16[128,4096]{1,0:T(8,128)(2,1)}, u32[]{:S(2)}, u32[]{:S(2)}) %collective-permute-start.7) | collective-permute-done | bytes 1048608 | tf_op jit(solution)/shard_map/ppermute | solution.py:74
  123.2 24.5 %collective-permute-done.9 = bf16[128,4096]{1,0:T(8,128)(2,1)} collective-permute-done((bf16[128,4096]{1,0:T(8,128)(2,1)}, bf16[128,4096]{1,0:T(8,128)(2,1)}, u32[]{:S(2)}, u32[]{:S(2)}) %collective-permute-start.9) | collective-permute-done | bytes 1048608 | tf_op jit(solution)/shard_map/ppermute | solution.py:74
  147.7 41.3 %collective-permute-done.8 = bf16[128,4096]{1,0:T(8,128)(2,1)} collective-permute-done((bf16[128,4096]{1,0:T(8,128)(2,1)}, bf16[128,4096]{1,0:T(8,128)(2,1)}, u32[]{:S(2)}, u32[]{:S(2)}) %collective-permute-start.8) | collective-permute-done | bytes 1048608 | tf_op jit(solution)/shard_map/ppermute | solution.py:74
  189.0 5.6 %multiply_convert_fusion.3 = (bf16[128,4096]{1,0:T(8,128)(2,1)}, bf16[128,4096]{1,0:T(8,128)(2,1)}) fusion(bf16[128,4096]{1,0:T(8,128)(2,1)} %param.9, bf16[128,4096]{1,0:T(8,128)(2,1)} %collective-permute-done.9, bf16[128,4096]{1,0:T(8,128)(2,1)} %collective-permute-done.8, bf16[128,4096]{1,0:T(8,128)(2,1)} %collective-permute-done.7, ...), kind=kLoop, calls=%fused_computation.20 | loop fusion | flops 11010048 | bytes 9437188 | tf_op jit(solution)/shard_map/convert_element_type | solution.py:80
  195.5 14.6 %multiply_convert_fusion = bf16[4096,1024]{1,0:T(8,128)(2,1)} fusion(bf16[1024,4096]{1,0:T(8,128)(2,1)} %all-gather.4.cloned.1.call-done, bf16[1024,1024]{1,0:T(8,128)(2,1)S(1)} %constant_dynamic-update-slice_fusion.4), kind=kOutput, calls=%fused_computation | convolution fusion | flops 8598323200 | bytes 18874368 | tf_op jit(solution)/shard_map/dot_general | solution.py:82
  210.0 66.3 %all-gather.6.cloned.1.call-done = bf16[1024,4096]{1,0:T(8,128)(2,1)} async-done(((bf16[128,4096]{1,0:T(8,128)(2,1)}), bf16[1024,4096]{1,0:T(8,128)(2,1)}) %all-gather.6.cloned.1.call-update) | async-done | bytes 8388624 | tf_op jit(solution)/shard_map/all_gather | solution.py:85
  276.3 12.8 %fusion.24 = f32[1024,1024]{1,0:T(8,128)S(1)} fusion(bf16[1024,4096]{1,0:T(8,128)(2,1)} %all-gather.6.cloned.1.call-done, bf16[1024,4096]{1,0:T(8,128)(2,1)} %param.11), kind=kOutput, calls=%fused_computation.56 | convolution fusion | flops 8589934592 | bytes 20971520 | tf_op jit(solution)/shard_map/dot_general | solution.py:91
  293.0 13.7 %fusion.23 = f32[1024,4096]{1,0:T(8,128)} fusion(bf16[1024,1024]{1,0:T(8,128)(2,1)} %constant_dynamic-update-slice_fusion, bf16[1024,4096]{1,0:T(8,128)(2,1)S(1)} %copy-done.3), kind=kOutput, calls=%fused_computation.55 | convolution fusion | flops 8589934592 | bytes 27262976 | tf_op jit(solution)/shard_map/dot_general | solution.py:87
  306.6 8.8 %collective-permute-done.10 = f32[256,1024]{1,0:T(8,128)S(1)} collective-permute-done((f32[256,1024]{1,0:T(8,128)S(1)}, f32[256,1024]{1,0:T(8,128)S(1)}, u32[]{:S(2)}, u32[]{:S(2)}) %collective-permute-start.10) | collective-permute-done | bytes 1048608 | tf_op jit(solution)/shard_map/ppermute | solution.py:35
  315.5 22.8 %collective-permute-done.12 = f32[256,1024]{1,0:T(8,128)S(1)} collective-permute-done((f32[256,1024]{1,0:T(8,128)S(1)}, f32[256,1024]{1,0:T(8,128)S(1)}, u32[]{:S(2)}, u32[]{:S(2)}) %collective-permute-start.12) | collective-permute-done | bytes 1048608 | tf_op jit(solution)/shard_map/ppermute | solution.py:35
  339.1 20.0 %all-gather.8.cloned.1.call-done = bf16[1024,4096]{1,0:T(8,128)(2,1)} async-done(((bf16[128,4096]{1,0:T(8,128)(2,1)}), bf16[1024,4096]{1,0:T(8,128)(2,1)}) %all-gather.8.cloned.1.call-update) | async-done | bytes 8388624 | tf_op jit(solution)/shard_map/all_gather | solution.py:86
  359.1 12.6 %fusion.25 = f32[1024,1024]{1,0:T(8,128)S(1)} fusion(bf16[1024,4096]{1,0:T(8,128)(2,1)} %all-gather.8.cloned.1.call-done, bf16[1024,4096]{1,0:T(8,128)(2,1)} %param.12), kind=kOutput, calls=%fused_computation.57 | convolution fusion | flops 8589934592 | bytes 20971520 | tf_op jit(solution)/shard_map/dot_general | solution.py:94
  375.6 15.6 %multiply_convert_fusion.1 = bf16[1024,4096]{1,0:T(8,128)(2,1)} fusion(bf16[1024,1024]{1,0:T(8,128)(2,1)} %constant_dynamic-update-slice_fusion, bf16[1024,4096]{1,0:T(8,128)(2,1)} %all-gather.8.cloned.1.call-done), kind=kOutput, calls=%fused_computation.1 | convolution fusion | flops 8598323200 | bytes 18874368 | tf_op jit(solution)/shard_map/dot_general | solution.py:99
  391.2 4.0 multiply_convert_fusion.2
  395.2 3.2 collective-permute-done.15
  (60 shorter events, 34.3 us)
Async XLA Ops:
  7.2 84.2 %all-gather.4.cloned.1.call-start = ((), (), s32[]{:S(2)}) async-start(), calls=%async_computation | async-start | bytes 9437184 | tf_op jit(solution)/shard_map/all_gather | solution.py:46
  10.4 265.9 %all-gather.6.cloned.1.call-start = ((), (), s32[]{:S(2)}) async-start(), calls=%async_computation.1 | async-start | bytes 9437184 | tf_op jit(solution)/shard_map/all_gather | solution.py:85
  10.5 15.0 %collective-permute-start = (bf16[256,1024]{1,0:T(8,128)(2,1)S(1)}, bf16[256,1024]{1,0:T(8,128)(2,1)}, u32[]{:S(2)}, u32[]{:S(2)}) collective-permute-start(bf16[256,1024]{1,0:T(8,128)(2,1)S(1)} %copy-done.1), channel_id=1, source_target_pairs={{0,1},{1,2},{2,3},{3,0},{4,5},{5,6},{6,7},{7,4},{8,9},{9,10},{10,1... | collective-permute-start | bytes 1572872 | tf_op jit(solution)/shard_map/ppermute | solution.py:23
  12.0 24.7 %collective-permute-start.1 = (bf16[256,1024]{1,0:T(8,128)(2,1)S(1)}, bf16[256,1024]{1,0:T(8,128)(2,1)}, u32[]{:S(2)}, u32[]{:S(2)}) collective-permute-start(bf16[256,1024]{1,0:T(8,128)(2,1)S(1)} %copy-done.1), channel_id=1, source_target_pairs={{0,2},{1,3},{2,0},{3,1},{4,6},{5,7},{6,4},{7,5},{8,10},{9,11},{10,... | collective-permute-start | bytes 1572872 | tf_op jit(solution)/shard_map/ppermute | solution.py:23
  12.5 25.3 %collective-permute-start.2 = (bf16[256,1024]{1,0:T(8,128)(2,1)S(1)}, bf16[256,1024]{1,0:T(8,128)(2,1)S(1)}, u32[]{:S(2)}, u32[]{:S(2)}) collective-permute-start(bf16[256,1024]{1,0:T(8,128)(2,1)S(1)} %copy-done.1), channel_id=1, source_target_pairs={{0,3},{1,0},{2,1},{3,2},{4,7},{5,4},{6,5},{7,6},{8,11},{9,8},{10,9... | collective-permute-start | bytes 1572872 | tf_op jit(solution)/shard_map/ppermute | solution.py:23
  14.4 23.8 %copy-start.2 = (bf16[4096,1024]{1,0:T(8,128)(2,1)S(1)}, bf16[4096,1024]{1,0:T(8,128)(2,1)}, u32[]{:S(2)}) copy-start(bf16[4096,1024]{1,0:T(8,128)(2,1)} %param.13) | copy-start | bytes 25165828
  45.0 30.5 %collective-permute-start.3 = (f32[512,4096]{1,0:T(8,128)}, f32[512,4096]{1,0:T(8,128)}, u32[]{:S(2)}, u32[]{:S(2)}) collective-permute-start(f32[512,4096]{1,0:T(8,128)} %fusion.22), channel_id=1, source_target_pairs={{0,4},{4,0},{1,5},{5,1},{2,6},{6,2},{3,7},{7,3},{8,12},{12,8},{9,1... | collective-permute-start | bytes 25165832 | tf_op jit(solution)/shard_map/ppermute | solution.py:64
  45.0 15.0 %collective-permute-start.4 = (bf16[256,1024]{1,0:T(8,128)(2,1)}, bf16[256,1024]{1,0:T(8,128)(2,1)}, u32[]{:S(2)}, u32[]{:S(2)}) collective-permute-start(bf16[256,1024]{1,0:T(8,128)(2,1)} %param.7), channel_id=1, source_target_pairs={{0,1},{1,2},{2,3},{3,0},{4,5},{5,6},{6,7},{7,4},{8,9},{9,10},{10,1... | collective-permute-start | bytes 1572872 | tf_op jit(solution)/shard_map/ppermute | solution.py:23
  46.2 25.6 %collective-permute-start.5 = (bf16[256,1024]{1,0:T(8,128)(2,1)}, bf16[256,1024]{1,0:T(8,128)(2,1)}, u32[]{:S(2)}, u32[]{:S(2)}) collective-permute-start(bf16[256,1024]{1,0:T(8,128)(2,1)} %param.7), channel_id=1, source_target_pairs={{0,2},{1,3},{2,0},{3,1},{4,6},{5,7},{6,4},{7,5},{8,10},{9,11},{10,... | collective-permute-start | bytes 1572872 | tf_op jit(solution)/shard_map/ppermute | solution.py:23
  46.7 27.0 %collective-permute-start.6 = (bf16[256,1024]{1,0:T(8,128)(2,1)}, bf16[256,1024]{1,0:T(8,128)(2,1)}, u32[]{:S(2)}, u32[]{:S(2)}) collective-permute-start(bf16[256,1024]{1,0:T(8,128)(2,1)} %param.7), channel_id=1, source_target_pairs={{0,3},{1,0},{2,1},{3,2},{4,7},{5,4},{6,5},{7,6},{8,11},{9,8},{10,9... | collective-permute-start | bytes 1572872 | tf_op jit(solution)/shard_map/ppermute | solution.py:23
  87.0 102.0 %copy-start = (bf16[128,4096]{1,0:T(8,128)(2,1)S(1)}, bf16[128,4096]{1,0:T(8,128)(2,1)}, u32[]{:S(2)}) copy-start(bf16[128,4096]{1,0:T(8,128)(2,1)} %param.10) | copy-start | bytes 3145732
  96.0 27.3 %collective-permute-start.7 = (bf16[128,4096]{1,0:T(8,128)(2,1)}, bf16[128,4096]{1,0:T(8,128)(2,1)}, u32[]{:S(2)}, u32[]{:S(2)}) collective-permute-start(bf16[128,4096]{1,0:T(8,128)(2,1)} %get-tuple-element.26), channel_id=1, source_target_pairs={{0,8},{8,16},{16,24},{24,0},{1,9},{9,17},{17,25},{25,1},{2,10},{10... | collective-permute-start | bytes 3145736 | tf_op jit(solution)/shard_map/ppermute | solution.py:74
  98.5 49.3 %collective-permute-start.9 = (bf16[128,4096]{1,0:T(8,128)(2,1)}, bf16[128,4096]{1,0:T(8,128)(2,1)}, u32[]{:S(2)}, u32[]{:S(2)}) collective-permute-start(bf16[128,4096]{1,0:T(8,128)(2,1)} %get-tuple-element.27), channel_id=1, source_target_pairs={{0,24},{8,0},{16,8},{24,16},{1,25},{9,1},{17,9},{25,17},{2,26},{10... | collective-permute-start | bytes 3145736 | tf_op jit(solution)/shard_map/ppermute | solution.py:74
  99.0 90.0 %collective-permute-start.8 = (bf16[128,4096]{1,0:T(8,128)(2,1)}, bf16[128,4096]{1,0:T(8,128)(2,1)}, u32[]{:S(2)}, u32[]{:S(2)}) collective-permute-start(bf16[128,4096]{1,0:T(8,128)(2,1)} %get-tuple-element.28), channel_id=1, source_target_pairs={{0,16},{8,24},{16,0},{24,8},{1,17},{9,25},{17,1},{25,9},{2,18},{10... | collective-permute-start | bytes 3145736 | tf_op jit(solution)/shard_map/ppermute | solution.py:74
  194.7 164.5 %all-gather.8.cloned.1.call-start = ((), (), s32[]{:S(2)}) async-start(), calls=%async_computation.2 | async-start | bytes 9437184 | tf_op jit(solution)/shard_map/all_gather | solution.py:86
  289.4 26.0 %collective-permute-start.10 = (f32[256,1024]{1,0:T(8,128)S(1)}, f32[256,1024]{1,0:T(8,128)S(1)}, u32[]{:S(2)}, u32[]{:S(2)}) collective-permute-start(f32[256,1024]{1,0:T(8,128)S(1)} %get-tuple-element.32), channel_id=1, source_target_pairs={{0,1},{1,2},{2,3},{3,0},{4,5},{5,6},{6,7},{7,4},{8,9},{9,10},{10,1... | collective-permute-start | bytes 3145736 | tf_op jit(solution)/shard_map/ppermute | solution.py:35
  290.9 47.3 %collective-permute-start.12 = (f32[256,1024]{1,0:T(8,128)S(1)}, f32[256,1024]{1,0:T(8,128)S(1)}, u32[]{:S(2)}, u32[]{:S(2)}) collective-permute-start(f32[256,1024]{1,0:T(8,128)S(1)} %get-tuple-element.33), channel_id=1, source_target_pairs={{0,3},{1,0},{2,1},{3,2},{4,7},{5,4},{6,5},{7,6},{8,11},{9,8},{10,9... | collective-permute-start | bytes 3145736 | tf_op jit(solution)/shard_map/ppermute | solution.py:35
  291.5 47.2 %collective-permute-start.11 = (f32[256,1024]{1,0:T(8,128)S(1)}, f32[256,1024]{1,0:T(8,128)S(1)}, u32[]{:S(2)}, u32[]{:S(2)}) collective-permute-start(f32[256,1024]{1,0:T(8,128)S(1)} %get-tuple-element.34), channel_id=1, source_target_pairs={{0,2},{1,3},{2,0},{3,1},{4,6},{5,7},{6,4},{7,5},{8,10},{9,11},{10,... | collective-permute-start | bytes 3145736 | tf_op jit(solution)/shard_map/ppermute | solution.py:35
  371.8 19.4 %slice-start = ((s8[16777216]{0:T(1024)(128)(4,1)}), s8[4194304]{0:T(1024)(128)(4,1)S(1)}, s32[]{:S(2)}) async-start(s8[16777216]{0:T(1024)(128)(4,1)} %bitcast.64), calls=%async_computation.3 | async-start | bytes 8388608
  372.0 23.2 %collective-permute-start.13 = (bf16[256,1024]{1,0:T(8,128)(2,1)S(1)}, bf16[256,1024]{1,0:T(8,128)(2,1)S(1)}, u32[]{:S(2)}, u32[]{:S(2)}) collective-permute-start(bf16[256,1024]{1,0:T(8,128)(2,1)S(1)} %get-tuple-element.29), channel_id=1, source_target_pairs={{0,1},{1,2},{2,3},{3,0},{4,5},{5,6},{6,7},{7,4},{8,9},{9,10},{10,1... | collective-permute-start | bytes 1572872 | tf_op jit(solution)/shard_map/ppermute | solution.py:35
  373.6 24.9 %collective-permute-start.15 = (bf16[256,1024]{1,0:T(8,128)(2,1)S(1)}, bf16[256,1024]{1,0:T(8,128)(2,1)S(1)}, u32[]{:S(2)}, u32[]{:S(2)}) collective-permute-start(bf16[256,1024]{1,0:T(8,128)(2,1)S(1)} %get-tuple-element.30), channel_id=1, source_target_pairs={{0,3},{1,0},{2,1},{3,2},{4,7},{5,4},{6,5},{7,6},{8,11},{9,8},{10,9... | collective-permute-start | bytes 1572872 | tf_op jit(solution)/shard_map/ppermute | solution.py:35
  374.1 17.0 %slice-start.2 = ((s8[16777216]{0:T(1024)(128)(4,1)}), s8[4194304]{0:T(1024)(128)(4,1)S(1)}, s32[]{:S(2)}) async-start(s8[16777216]{0:T(1024)(128)(4,1)} %bitcast.64), calls=%async_computation.5 | async-start | bytes 8388608
  374.1 17.0 %slice-start.3 = ((s8[16777216]{0:T(1024)(128)(4,1)}), s8[4194304]{0:T(1024)(128)(4,1)S(1)}, s32[]{:S(2)}) async-start(s8[16777216]{0:T(1024)(128)(4,1)} %bitcast.64), calls=%async_computation.6 | async-start | bytes 8388608
  374.1 24.7 %collective-permute-start.14 = (bf16[256,1024]{1,0:T(8,128)(2,1)S(1)}, bf16[256,1024]{1,0:T(8,128)(2,1)S(1)}, u32[]{:S(2)}, u32[]{:S(2)}) collective-permute-start(bf16[256,1024]{1,0:T(8,128)(2,1)S(1)} %get-tuple-element.31), channel_id=1, source_target_pairs={{0,2},{1,3},{2,0},{3,1},{4,6},{5,7},{6,4},{7,5},{8,10},{9,11},{10,... | collective-permute-start | bytes 1572872 | tf_op jit(solution)/shard_map/ppermute | solution.py:35
  (3 other events, 37.0 us)
Sparse Core Ops, SparseCore 0:
  10.6 80.7 all-gather.3
  194.8 81.4 all-gather.5
  278.5 80.5 all-gather.7

commit v9 on v8

--- a/solution.py
+++ b/solution.py
@@ -69,7 +69,7 @@
     chip_sum = (hid_keep + hid_recv).reshape(chips, -1, hid_keep.shape[1])
     chip_sum, hidden_act, act_full = lax.optimization_barrier((chip_sum, hidden_act, act_full))
     hid_rows = lax.dynamic_index_in_dim(chip_sum, z, axis=0, keepdims=False)
-    for s in range(1, chips):
+    for s in [1] + list(range(chips - 1, 1, -1)):
         piece = lax.dynamic_index_in_dim(chip_sum, (z + s) % chips, axis=0, keepdims=False)
         piece = lax.ppermute(piece.astype(jnp.bfloat16), "z", shift_perm(chips, s))
         hid_rows = hid_rows + piece.astype(jnp.float32)

time: 411 us -> 411 us (level)
  no operation moved by 1% of the time
where the time goes in v9:
time: 411 us; the launch traced here: 407 us
  waiting for transfers between devices  255 us (62%)
  matrix products  87.6 us (21%)
  starting transfers between devices  18.9 us (5%)
  local copies, waits for them, and re-layouts  17 us (4%)
  other arithmetic  14.4 us (4%)
  between operations  14 us (3%)
    ppermute x3, waiting for transfers between devices, body(): piece = lax.ppermute(piece.astype(jnp.bfloat16), 'z', shift_perm(chips, s))  90.2 us
    all_gather x1, waiting for transfers between devices, body(): gate_delta = lax.all_gather(gate_local, ROW, axis=0, tiled=True)  63.8 us
    ppermute x6, waiting for transfers between devices, gather_col(): part = lax.ppermute(block, 'col', shift_perm(n, s))  40.2 us
    ppermute x6, waiting for transfers between devices, reduce_scatter_col(): piece = lax.ppermute(piece.astype(send_dtype), 'col', shift_perm(n, s))  35.7 us
    all_gather x1, waiting for transfers between devices, body(): up_delta = lax.all_gather(up_local, ROW, axis=0, tiled=True)  20 us
    dot_general x1, matrix products, body(): lax.dot_general(act_full, up_delta, CONTRACT_FIRST, preferred_element_typ...  15.6 us
    dot_general x1, matrix products, body(): lax.dot_general(hidden_act, grad_full, CONTRACT_FIRST, preferred_element_...  14.6 us
    dot_general x1, matrix products, body(): lax.dot_general(act_full, gate_delta, CONTRACT_FIRST, preferred_element_t...  13.7 us
  transfers between devices with their start and end apart: 19, of which 15 were waited for; matrix products, arithmetic and copies ran while one was open for 22% of the time, Pallas kernels for 0%

profile of v9, /device:TPU:10, one launch (start us, length us, event | category | flops | bytes accessed | tf_op | source)
XLA Modules:
  0.0 406.6 jit_solution(8132090471871800116)
XLA Ops:
  7.2 3.2 fusion
  14.4 11.0 %collective-permute-done = bf16[256,1024]{1,0:T(8,128)(2,1)} collective-permute-done((bf16[256,1024]{1,0:T(8,128)(2,1)S(1)}, bf16[256,1024]{1,0:T(8,128)(2,1)}, u32[]{:S(2)}, u32[]{:S(2)}) %collective-permute-start) | collective-permute-done | bytes 524320 | tf_op jit(solution)/shard_map/ppermute | solution.py:23
  26.5 10.2 %collective-permute-done.1 = bf16[256,1024]{1,0:T(8,128)(2,1)} collective-permute-done((bf16[256,1024]{1,0:T(8,128)(2,1)S(1)}, bf16[256,1024]{1,0:T(8,128)(2,1)}, u32[]{:S(2)}, u32[]{:S(2)}) %collective-permute-start.1) | collective-permute-done | bytes 524320 | tf_op jit(solution)/shard_map/ppermute | solution.py:23
  38.2 6.8 %fusion.22 = f32[512,4096]{1,0:T(8,128)} fusion(bf16[512,1024]{1,0:T(8,128)(2,1)S(1)} %bitcast.74, bf16[4096,1024]{1,0:T(8,128)(2,1)S(1)} %copy-done.2), kind=kOutput, calls=%fused_computation.54 | convolution fusion | flops 4294967296 | bytes 17825792 | tf_op jit(solution)/shard_map/dot_general | solution.py:60
  50.9 9.0 %collective-permute-done.4 = bf16[256,1024]{1,0:T(8,128)(2,1)} collective-permute-done((bf16[256,1024]{1,0:T(8,128)(2,1)}, bf16[256,1024]{1,0:T(8,128)(2,1)}, u32[]{:S(2)}, u32[]{:S(2)}) %collective-permute-start.4) | collective-permute-done | bytes 524320 | tf_op jit(solution)/shard_map/ppermute | solution.py:23
  61.9 9.9 %collective-permute-done.5 = bf16[256,1024]{1,0:T(8,128)(2,1)} collective-permute-done((bf16[256,1024]{1,0:T(8,128)(2,1)}, bf16[256,1024]{1,0:T(8,128)(2,1)}, u32[]{:S(2)}, u32[]{:S(2)}) %collective-permute-start.5) | collective-permute-done | bytes 524320 | tf_op jit(solution)/shard_map/ppermute | solution.py:23
  75.5 11.5 %convolution_add_fusion = f32[512,4096]{1,0:T(8,128)} fusion(f32[512,4096]{1,0:T(8,128)} %collective-permute-done.3, bf16[512,1024]{1,0:T(8,128)(2,1)S(1)} %bitcast.73, bf16[4096,1024]{1,0:T(8,128)(2,1)} %param.13), kind=kOutput, calls=%fused_computation.3 | convolution fusion | flops 4297064448 | bytes 26214400 | tf_op jit(solution)/shard_map/dot_general | solution.py:65
  87.0 4.3 %all-gather.4.cloned.1.call-done = bf16[1024,4096]{1,0:T(8,128)(2,1)} async-done(((bf16[128,4096]{1,0:T(8,128)(2,1)}), bf16[1024,4096]{1,0:T(8,128)(2,1)}) %all-gather.4.cloned.1.call-update) | async-done | bytes 8388624 | tf_op jit(solution)/shard_map/all_gather | solution.py:46
  91.3 4.6 %fusion.10 = (bf16[128,4096]{1,0:T(8,128)(2,1)}, bf16[128,4096]{1,0:T(8,128)(2,1)}, bf16[128,4096]{1,0:T(8,128)(2,1)}) fusion(f32[4,128,4096]{2,1,0:T(8,128)} %bitcast.69, s32[]{:T(128)S(6)} %select_n.115, s32[]{:T(128)S(6)} %select_n.119, s32[]{:T(128)S(6)} %select_n.117), kind=kLoop, calls=%fused_computation.24 | loop fusion | bytes 6291468 | tf_op jit(solution)/shard_map/convert_element_type | solution.py:74
  98.5 2.9 collective-permute-start.9
  101.4 21.9 %collective-permute-done.7 = bf16[128,4096]{1,0:T(8,128)(2,1)} collective-permute-done((bf16[128,4096]{1,0:T(8,128)(2,1)}, bf16[128,4096]{1,0:T(8,128)(2,1)}, u32[]{:S(2)}, u32[]{:S(2)}) %collective-permute-start.7) | collective-permute-done | bytes 1048608 | tf_op jit(solution)/shard_map/ppermute | solution.py:74
  123.2 65.8 %collective-permute-done.9 = bf16[128,4096]{1,0:T(8,128)(2,1)} collective-permute-done((bf16[128,4096]{1,0:T(8,128)(2,1)}, bf16[128,4096]{1,0:T(8,128)(2,1)}, u32[]{:S(2)}, u32[]{:S(2)}) %collective-permute-start.9) | collective-permute-done | bytes 1048608 | tf_op jit(solution)/shard_map/ppermute | solution.py:74
  191.5 5.6 %multiply_convert_fusion.3 = (bf16[128,4096]{1,0:T(8,128)(2,1)}, bf16[128,4096]{1,0:T(8,128)(2,1)}) fusion(bf16[128,4096]{1,0:T(8,128)(2,1)} %param.9, bf16[128,4096]{1,0:T(8,128)(2,1)} %collective-permute-done.9, bf16[128,4096]{1,0:T(8,128)(2,1)} %collective-permute-done.8, bf16[128,4096]{1,0:T(8,128)(2,1)} %collective-permute-done.7, ...), kind=kLoop, calls=%fused_computation.20 | loop fusion | flops 11010048 | bytes 9437188 | tf_op jit(solution)/shard_map/convert_element_type | solution.py:80
  198.0 14.6 %multiply_convert_fusion = bf16[4096,1024]{1,0:T(8,128)(2,1)} fusion(bf16[1024,4096]{1,0:T(8,128)(2,1)} %all-gather.4.cloned.1.call-done, bf16[1024,1024]{1,0:T(8,128)(2,1)S(1)} %constant_dynamic-update-slice_fusion.4), kind=kOutput, calls=%fused_computation | convolution fusion | flops 8598323200 | bytes 18874368 | tf_op jit(solution)/shard_map/dot_general | solution.py:82
  212.6 63.8 %all-gather.6.cloned.1.call-done = bf16[1024,4096]{1,0:T(8,128)(2,1)} async-done(((bf16[128,4096]{1,0:T(8,128)(2,1)}), bf16[1024,4096]{1,0:T(8,128)(2,1)}) %all-gather.6.cloned.1.call-update) | async-done | bytes 8388624 | tf_op jit(solution)/shard_map/all_gather | solution.py:85
  276.3 12.8 %fusion.24 = f32[1024,1024]{1,0:T(8,128)S(1)} fusion(bf16[1024,4096]{1,0:T(8,128)(2,1)} %all-gather.6.cloned.1.call-done, bf16[1024,4096]{1,0:T(8,128)(2,1)} %param.11), kind=kOutput, calls=%fused_computation.56 | convolution fusion | flops 8589934592 | bytes 20971520 | tf_op jit(solution)/shard_map/dot_general | solution.py:91
  293.0 13.7 %fusion.23 = f32[1024,4096]{1,0:T(8,128)} fusion(bf16[1024,1024]{1,0:T(8,128)(2,1)} %constant_dynamic-update-slice_fusion, bf16[1024,4096]{1,0:T(8,128)(2,1)S(1)} %copy-done.3), kind=kOutput, calls=%fused_computation.55 | convolution fusion | flops 8589934592 | bytes 27262976 | tf_op jit(solution)/shard_map/dot_general | solution.py:87
  306.7 8.8 %collective-permute-done.10 = f32[256,1024]{1,0:T(8,128)S(1)} collective-permute-done((f32[256,1024]{1,0:T(8,128)S(1)}, f32[256,1024]{1,0:T(8,128)S(1)}, u32[]{:S(2)}, u32[]{:S(2)}) %collective-permute-start.10) | collective-permute-done | bytes 1048608 | tf_op jit(solution)/shard_map/ppermute | solution.py:35
  315.5 22.8 %collective-permute-done.12 = f32[256,1024]{1,0:T(8,128)S(1)} collective-permute-done((f32[256,1024]{1,0:T(8,128)S(1)}, f32[256,1024]{1,0:T(8,128)S(1)}, u32[]{:S(2)}, u32[]{:S(2)}) %collective-permute-start.12) | collective-permute-done | bytes 1048608 | tf_op jit(solution)/shard_map/ppermute | solution.py:35
  339.1 20.0 %all-gather.8.cloned.1.call-done = bf16[1024,4096]{1,0:T(8,128)(2,1)} async-done(((bf16[128,4096]{1,0:T(8,128)(2,1)}), bf16[1024,4096]{1,0:T(8,128)(2,1)}) %all-gather.8.cloned.1.call-update) | async-done | bytes 8388624 | tf_op jit(solution)/shard_map/all_gather | solution.py:86
  359.1 12.6 %fusion.25 = f32[1024,1024]{1,0:T(8,128)S(1)} fusion(bf16[1024,4096]{1,0:T(8,128)(2,1)} %all-gather.8.cloned.1.call-done, bf16[1024,4096]{1,0:T(8,128)(2,1)} %param.12), kind=kOutput, calls=%fused_computation.57 | convolution fusion | flops 8589934592 | bytes 20971520 | tf_op jit(solution)/shard_map/dot_general | solution.py:94
  375.6 15.6 %multiply_convert_fusion.1 = bf16[1024,4096]{1,0:T(8,128)(2,1)} fusion(bf16[1024,1024]{1,0:T(8,128)(2,1)} %constant_dynamic-update-slice_fusion, bf16[1024,4096]{1,0:T(8,128)(2,1)} %all-gather.8.cloned.1.call-done), kind=kOutput, calls=%fused_computation.1 | convolution fusion | flops 8598323200 | bytes 18874368 | tf_op jit(solution)/shard_map/dot_general | solution.py:99
  391.2 4.0 multiply_convert_fusion.2
  395.2 3.2 collective-permute-done.15
  (60 shorter events, 33.9 us)
Async XLA Ops:
  7.2 84.2 %all-gather.4.cloned.1.call-start = ((), (), s32[]{:S(2)}) async-start(), calls=%async_computation | async-start | bytes 9437184 | tf_op jit(solution)/shard_map/all_gather | solution.py:46
  10.4 265.9 %all-gather.6.cloned.1.call-start = ((), (), s32[]{:S(2)}) async-start(), calls=%async_computation.1 | async-start | bytes 9437184 | tf_op jit(solution)/shard_map/all_gather | solution.py:85
  10.5 15.0 %collective-permute-start = (bf16[256,1024]{1,0:T(8,128)(2,1)S(1)}, bf16[256,1024]{1,0:T(8,128)(2,1)}, u32[]{:S(2)}, u32[]{:S(2)}) collective-permute-start(bf16[256,1024]{1,0:T(8,128)(2,1)S(1)} %copy-done.1), channel_id=1, source_target_pairs={{0,1},{1,2},{2,3},{3,0},{4,5},{5,6},{6,7},{7,4},{8,9},{9,10},{10,1... | collective-permute-start | bytes 1572872 | tf_op jit(solution)/shard_map/ppermute | solution.py:23
  12.0 24.7 %collective-permute-start.1 = (bf16[256,1024]{1,0:T(8,128)(2,1)S(1)}, bf16[256,1024]{1,0:T(8,128)(2,1)}, u32[]{:S(2)}, u32[]{:S(2)}) collective-permute-start(bf16[256,1024]{1,0:T(8,128)(2,1)S(1)} %copy-done.1), channel_id=1, source_target_pairs={{0,2},{1,3},{2,0},{3,1},{4,6},{5,7},{6,4},{7,5},{8,10},{9,11},{10,... | collective-permute-start | bytes 1572872 | tf_op jit(solution)/shard_map/ppermute | solution.py:23
  12.5 25.3 %collective-permute-start.2 = (bf16[256,1024]{1,0:T(8,128)(2,1)S(1)}, bf16[256,1024]{1,0:T(8,128)(2,1)S(1)}, u32[]{:S(2)}, u32[]{:S(2)}) collective-permute-start(bf16[256,1024]{1,0:T(8,128)(2,1)S(1)} %copy-done.1), channel_id=1, source_target_pairs={{0,3},{1,0},{2,1},{3,2},{4,7},{5,4},{6,5},{7,6},{8,11},{9,8},{10,9... | collective-permute-start | bytes 1572872 | tf_op jit(solution)/shard_map/ppermute | solution.py:23
  14.4 23.8 %copy-start.2 = (bf16[4096,1024]{1,0:T(8,128)(2,1)S(1)}, bf16[4096,1024]{1,0:T(8,128)(2,1)}, u32[]{:S(2)}) copy-start(bf16[4096,1024]{1,0:T(8,128)(2,1)} %param.13) | copy-start | bytes 25165828
  45.0 30.5 %collective-permute-start.3 = (f32[512,4096]{1,0:T(8,128)}, f32[512,4096]{1,0:T(8,128)}, u32[]{:S(2)}, u32[]{:S(2)}) collective-permute-start(f32[512,4096]{1,0:T(8,128)} %fusion.22), channel_id=1, source_target_pairs={{0,4},{4,0},{1,5},{5,1},{2,6},{6,2},{3,7},{7,3},{8,12},{12,8},{9,1... | collective-permute-start | bytes 25165832 | tf_op jit(solution)/shard_map/ppermute | solution.py:64
  45.0 15.0 %collective-permute-start.4 = (bf16[256,1024]{1,0:T(8,128)(2,1)}, bf16[256,1024]{1,0:T(8,128)(2,1)}, u32[]{:S(2)}, u32[]{:S(2)}) collective-permute-start(bf16[256,1024]{1,0:T(8,128)(2,1)} %param.7), channel_id=1, source_target_pairs={{0,1},{1,2},{2,3},{3,0},{4,5},{5,6},{6,7},{7,4},{8,9},{9,10},{10,1... | collective-permute-start | bytes 1572872 | tf_op jit(solution)/shard_map/ppermute | solution.py:23
  46.2 25.6 %collective-permute-start.5 = (bf16[256,1024]{1,0:T(8,128)(2,1)}, bf16[256,1024]{1,0:T(8,128)(2,1)}, u32[]{:S(2)}, u32[]{:S(2)}) collective-permute-start(bf16[256,1024]{1,0:T(8,128)(2,1)} %param.7), channel_id=1, source_target_pairs={{0,2},{1,3},{2,0},{3,1},{4,6},{5,7},{6,4},{7,5},{8,10},{9,11},{10,... | collective-permute-start | bytes 1572872 | tf_op jit(solution)/shard_map/ppermute | solution.py:23
  46.7 27.0 %collective-permute-start.6 = (bf16[256,1024]{1,0:T(8,128)(2,1)}, bf16[256,1024]{1,0:T(8,128)(2,1)}, u32[]{:S(2)}, u32[]{:S(2)}) collective-permute-start(bf16[256,1024]{1,0:T(8,128)(2,1)} %param.7), channel_id=1, source_target_pairs={{0,3},{1,0},{2,1},{3,2},{4,7},{5,4},{6,5},{7,6},{8,11},{9,8},{10,9... | collective-permute-start | bytes 1572872 | tf_op jit(solution)/shard_map/ppermute | solution.py:23
  87.0 104.5 %copy-start = (bf16[128,4096]{1,0:T(8,128)(2,1)S(1)}, bf16[128,4096]{1,0:T(8,128)(2,1)}, u32[]{:S(2)}) copy-start(bf16[128,4096]{1,0:T(8,128)(2,1)} %param.10) | copy-start | bytes 3145732
  96.0 27.3 %collective-permute-start.7 = (bf16[128,4096]{1,0:T(8,128)(2,1)}, bf16[128,4096]{1,0:T(8,128)(2,1)}, u32[]{:S(2)}, u32[]{:S(2)}) collective-permute-start(bf16[128,4096]{1,0:T(8,128)(2,1)} %get-tuple-element.26), channel_id=1, source_target_pairs={{0,8},{8,16},{16,24},{24,0},{1,9},{9,17},{17,25},{25,1},{2,10},{10... | collective-permute-start | bytes 3145736 | tf_op jit(solution)/shard_map/ppermute | solution.py:74
  98.5 90.6 %collective-permute-start.9 = (bf16[128,4096]{1,0:T(8,128)(2,1)}, bf16[128,4096]{1,0:T(8,128)(2,1)}, u32[]{:S(2)}, u32[]{:S(2)}) collective-permute-start(bf16[128,4096]{1,0:T(8,128)(2,1)} %get-tuple-element.27), channel_id=1, source_target_pairs={{0,16},{8,24},{16,0},{24,8},{1,17},{9,25},{17,1},{25,9},{2,18},{10... | collective-permute-start | bytes 3145736 | tf_op jit(solution)/shard_map/ppermute | solution.py:74
  101.4 90.2 %collective-permute-start.8 = (bf16[128,4096]{1,0:T(8,128)(2,1)}, bf16[128,4096]{1,0:T(8,128)(2,1)}, u32[]{:S(2)}, u32[]{:S(2)}) collective-permute-start(bf16[128,4096]{1,0:T(8,128)(2,1)} %get-tuple-element.28), channel_id=1, source_target_pairs={{0,24},{8,0},{16,8},{24,16},{1,25},{9,1},{17,9},{25,17},{2,26},{10... | collective-permute-start | bytes 3145736 | tf_op jit(solution)/shard_map/ppermute | solution.py:74
  197.2 161.9 %all-gather.8.cloned.1.call-start = ((), (), s32[]{:S(2)}) async-start(), calls=%async_computation.2 | async-start | bytes 9437184 | tf_op jit(solution)/shard_map/all_gather | solution.py:86
  289.4 26.0 %collective-permute-start.10 = (f32[256,1024]{1,0:T(8,128)S(1)}, f32[256,1024]{1,0:T(8,128)S(1)}, u32[]{:S(2)}, u32[]{:S(2)}) collective-permute-start(f32[256,1024]{1,0:T(8,128)S(1)} %get-tuple-element.32), channel_id=1, source_target_pairs={{0,1},{1,2},{2,3},{3,0},{4,5},{5,6},{6,7},{7,4},{8,9},{9,10},{10,1... | collective-permute-start | bytes 3145736 | tf_op jit(solution)/shard_map/ppermute | solution.py:35
  290.9 47.3 %collective-permute-start.12 = (f32[256,1024]{1,0:T(8,128)S(1)}, f32[256,1024]{1,0:T(8,128)S(1)}, u32[]{:S(2)}, u32[]{:S(2)}) collective-permute-start(f32[256,1024]{1,0:T(8,128)S(1)} %get-tuple-element.33), channel_id=1, source_target_pairs={{0,3},{1,0},{2,1},{3,2},{4,7},{5,4},{6,5},{7,6},{8,11},{9,8},{10,9... | collective-permute-start | bytes 3145736 | tf_op jit(solution)/shard_map/ppermute | solution.py:35
  291.5 47.2 %collective-permute-start.11 = (f32[256,1024]{1,0:T(8,128)S(1)}, f32[256,1024]{1,0:T(8,128)S(1)}, u32[]{:S(2)}, u32[]{:S(2)}) collective-permute-start(f32[256,1024]{1,0:T(8,128)S(1)} %get-tuple-element.34), channel_id=1, source_target_pairs={{0,2},{1,3},{2,0},{3,1},{4,6},{5,7},{6,4},{7,5},{8,10},{9,11},{10,... | collective-permute-start | bytes 3145736 | tf_op jit(solution)/shard_map/ppermute | solution.py:35
  371.8 19.4 %slice-start = ((s8[16777216]{0:T(1024)(128)(4,1)}), s8[4194304]{0:T(1024)(128)(4,1)S(1)}, s32[]{:S(2)}) async-start(s8[16777216]{0:T(1024)(128)(4,1)} %bitcast.64), calls=%async_computation.3 | async-start | bytes 8388608
  372.0 23.2 %collective-permute-start.13 = (bf16[256,1024]{1,0:T(8,128)(2,1)S(1)}, bf16[256,1024]{1,0:T(8,128)(2,1)S(1)}, u32[]{:S(2)}, u32[]{:S(2)}) collective-permute-start(bf16[256,1024]{1,0:T(8,128)(2,1)S(1)} %get-tuple-element.29), channel_id=1, source_target_pairs={{0,1},{1,2},{2,3},{3,0},{4,5},{5,6},{6,7},{7,4},{8,9},{9,10},{10,1... | collective-permute-start | bytes 1572872 | tf_op jit(solution)/shard_map/ppermute | solution.py:35
  373.6 24.8 %collective-permute-start.15 = (bf16[256,1024]{1,0:T(8,128)(2,1)S(1)}, bf16[256,1024]{1,0:T(8,128)(2,1)S(1)}, u32[]{:S(2)}, u32[]{:S(2)}) collective-permute-start(bf16[256,1024]{1,0:T(8,128)(2,1)S(1)} %get-tuple-element.30), channel_id=1, source_target_pairs={{0,3},{1,0},{2,1},{3,2},{4,7},{5,4},{6,5},{7,6},{8,11},{9,8},{10,9... | collective-permute-start | bytes 1572872 | tf_op jit(solution)/shard_map/ppermute | solution.py:35
  374.1 17.1 %slice-start.2 = ((s8[16777216]{0:T(1024)(128)(4,1)}), s8[4194304]{0:T(1024)(128)(4,1)S(1)}, s32[]{:S(2)}) async-start(s8[16777216]{0:T(1024)(128)(4,1)} %bitcast.64), calls=%async_computation.5 | async-start | bytes 8388608
  374.1 17.1 %slice-start.3 = ((s8[16777216]{0:T(1024)(128)(4,1)}), s8[4194304]{0:T(1024)(128)(4,1)S(1)}, s32[]{:S(2)}) async-start(s8[16777216]{0:T(1024)(128)(4,1)} %bitcast.64), calls=%async_computation.6 | async-start | bytes 8388608
  374.1 24.8 %collective-permute-start.14 = (bf16[256,1024]{1,0:T(8,128)(2,1)S(1)}, bf16[256,1024]{1,0:T(8,128)(2,1)S(1)}, u32[]{:S(2)}, u32[]{:S(2)}) collective-permute-start(bf16[256,1024]{1,0:T(8,128)(2,1)S(1)} %get-tuple-element.31), channel_id=1, source_target_pairs={{0,2},{1,3},{2,0},{3,1},{4,6},{5,7},{6,4},{7,5},{8,10},{9,11},{10,... | collective-permute-start | bytes 1572872 | tf_op jit(solution)/shard_map/ppermute | solution.py:35
  (3 other events, 37.0 us)
Sparse Core Ops, SparseCore 0:
  10.6 80.7 all-gather.3
  197.3 78.9 all-gather.5
  278.5 80.5 all-gather.7

commit v10 on v9

--- a/solution.py
+++ b/solution.py
@@ -90,7 +90,9 @@
     input_gate = reduce_scatter_col(
         lax.dot_general(gate_delta, gate_weight, CONTRACT_LAST, preferred_element_type=jnp.float32)
     )
-    acc_gate, input_gate, up_delta = lax.optimization_barrier((acc_gate, input_gate, up_delta))
+    factor = float(tokens_all) ** (-0.5)
+    gate_grad = (acc_gate * factor).astype(jnp.bfloat16)
+    gate_grad, input_gate, up_delta = lax.optimization_barrier((gate_grad, input_gate, up_delta))
     input_up = lax.dot_general(
         up_delta, up_weight, CONTRACT_LAST, preferred_element_type=jnp.float32
     )
@@ -98,10 +100,9 @@
     input_up = reduce_scatter_col(input_up, jnp.bfloat16)
     acc_up = lax.dot_general(act_full, up_delta, CONTRACT_FIRST, preferred_element_type=jnp.float32)
     input_rows = (input_gate + input_up).astype(jnp.bfloat16)
-    factor = float(tokens_all) ** (-0.5)
     return (
         input_rows,
-        (acc_gate * factor).astype(jnp.bfloat16),
+        gate_grad,
         (acc_up * factor).astype(jnp.bfloat16),
         (acc_down * factor).astype(jnp.bfloat16),
     )

time: 411 us -> 411 us (level)
  waiting for transfers between devices: 255 us -> 260 us
    ppermute x6, waiting for transfers between devices: 35.7 us -> 40.7 us  [reduce_scatter_col(): piece = lax.ppermute(piece.astype(send_dtype), 'col', shift_perm(n, s))]
  transfers between devices with their start and end apart: 19 -> 19, of which waited for: 15 -> 14; matrix products, arithmetic and copies ran while one was open for 22% -> 21% of each run, Pallas kernels for 0% -> 0%
where the time goes in v10:
time: 411 us; the launch traced here: 405 us
  waiting for transfers between devices  260 us (63%)
  matrix products  84 us (20%)
  starting transfers between devices  19.8 us (5%)
  local copies, waits for them, and re-layouts  17.2 us (4%)
  between operations  13.9 us (3%)
  other arithmetic  10.4 us (3%)
    ppermute x3, waiting for transfers between devices, body(): piece = lax.ppermute(piece.astype(jnp.bfloat16), 'z', shift_perm(chips, s))  89.5 us
    all_gather x1, waiting for transfers between devices, body(): gate_delta = lax.all_gather(gate_local, ROW, axis=0, tiled=True)  64.4 us
    ppermute x6, waiting for transfers between devices, reduce_scatter_col(): piece = lax.ppermute(piece.astype(send_dtype), 'col', shift_perm(n, s))  40.7 us
    ppermute x6, waiting for transfers between devices, gather_col(): part = lax.ppermute(block, 'col', shift_perm(n, s))  40.1 us
    all_gather x1, waiting for transfers between devices, body(): up_delta = lax.all_gather(up_local, ROW, axis=0, tiled=True)  20.5 us
    dot_general x1, matrix products, body(): lax.dot_general(hidden_act, grad_full, CONTRACT_FIRST, preferred_element_...  14.6 us
    dot_general x1, matrix products, body(): lax.dot_general(up_delta, up_weight, CONTRACT_LAST, preferred_element_typ...  12.8 us
    dot_general x1, matrix products, body(): lax.dot_general(gate_delta, gate_weight, CONTRACT_LAST, preferred_element...  12.8 us
  transfers between devices with their start and end apart: 19, of which 14 were waited for; matrix products, arithmetic and copies ran while one was open for 21% of the time, Pallas kernels for 0%

profile of v10, /device:TPU:10, one launch (start us, length us, event | category | flops | bytes accessed | tf_op | source)
XLA Modules:
  0.0 405.4 jit_solution(11458039251214388354)
XLA Ops:
  7.2 3.2 fusion
  14.4 11.0 %collective-permute-done = bf16[256,1024]{1,0:T(8,128)(2,1)} collective-permute-done((bf16[256,1024]{1,0:T(8,128)(2,1)S(1)}, bf16[256,1024]{1,0:T(8,128)(2,1)}, u32[]{:S(2)}, u32[]{:S(2)}) %collective-permute-start) | collective-permute-done | bytes 524320 | tf_op jit(solution)/shard_map/ppermute | solution.py:23
  26.5 10.2 %collective-permute-done.1 = bf16[256,1024]{1,0:T(8,128)(2,1)} collective-permute-done((bf16[256,1024]{1,0:T(8,128)(2,1)S(1)}, bf16[256,1024]{1,0:T(8,128)(2,1)}, u32[]{:S(2)}, u32[]{:S(2)}) %collective-permute-start.1) | collective-permute-done | bytes 524320 | tf_op jit(solution)/shard_map/ppermute | solution.py:23
  38.2 6.8 %fusion.22 = f32[512,4096]{1,0:T(8,128)} fusion(bf16[512,1024]{1,0:T(8,128)(2,1)S(1)} %bitcast.72, bf16[4096,1024]{1,0:T(8,128)(2,1)S(1)} %copy-done.2), kind=kOutput, calls=%fused_computation.54 | convolution fusion | flops 4294967296 | bytes 17825792 | tf_op jit(solution)/shard_map/dot_general | solution.py:60
  51.0 9.0 %collective-permute-done.4 = bf16[256,1024]{1,0:T(8,128)(2,1)} collective-permute-done((bf16[256,1024]{1,0:T(8,128)(2,1)}, bf16[256,1024]{1,0:T(8,128)(2,1)}, u32[]{:S(2)}, u32[]{:S(2)}) %collective-permute-start.4) | collective-permute-done | bytes 524320 | tf_op jit(solution)/shard_map/ppermute | solution.py:23
  61.9 9.8 %collective-permute-done.5 = bf16[256,1024]{1,0:T(8,128)(2,1)} collective-permute-done((bf16[256,1024]{1,0:T(8,128)(2,1)}, bf16[256,1024]{1,0:T(8,128)(2,1)}, u32[]{:S(2)}, u32[]{:S(2)}) %collective-permute-start.5) | collective-permute-done | bytes 524320 | tf_op jit(solution)/shard_map/ppermute | solution.py:23
  75.5 11.5 %convolution_add_fusion = f32[512,4096]{1,0:T(8,128)} fusion(f32[512,4096]{1,0:T(8,128)} %collective-permute-done.3, bf16[512,1024]{1,0:T(8,128)(2,1)S(1)} %bitcast.71, bf16[4096,1024]{1,0:T(8,128)(2,1)} %param.13), kind=kOutput, calls=%fused_computation.3 | convolution fusion | flops 4297064448 | bytes 26214400 | tf_op jit(solution)/shard_map/dot_general | solution.py:65
  87.0 4.3 %all-gather.4.cloned.1.call-done = bf16[1024,4096]{1,0:T(8,128)(2,1)} async-done(((bf16[128,4096]{1,0:T(8,128)(2,1)}), bf16[1024,4096]{1,0:T(8,128)(2,1)}) %all-gather.4.cloned.1.call-update) | async-done | bytes 8388624 | tf_op jit(solution)/shard_map/all_gather | solution.py:46
  91.3 4.8 %fusion.10 = (bf16[128,4096]{1,0:T(8,128)(2,1)}, bf16[128,4096]{1,0:T(8,128)(2,1)}, bf16[128,4096]{1,0:T(8,128)(2,1)}) fusion(f32[4,128,4096]{2,1,0:T(8,128)} %bitcast.67, s32[]{:T(128)S(6)} %select_n.115, s32[]{:T(128)S(6)} %select_n.119, s32[]{:T(128)S(6)} %select_n.117), kind=kLoop, calls=%fused_computation.24 | loop fusion | bytes 6291468 | tf_op jit(solution)/shard_map/convert_element_type | solution.py:74
  96.1 2.4 collective-permute-start.9
  100.6 66.7 %collective-permute-done.9 = bf16[128,4096]{1,0:T(8,128)(2,1)} collective-permute-done((bf16[128,4096]{1,0:T(8,128)(2,1)}, bf16[128,4096]{1,0:T(8,128)(2,1)}, u32[]{:S(2)}, u32[]{:S(2)}) %collective-permute-start.9) | collective-permute-done | bytes 1048608 | tf_op jit(solution)/shard_map/ppermute | solution.py:74
  167.3 22.8 %collective-permute-done.8 = bf16[128,4096]{1,0:T(8,128)(2,1)} collective-permute-done((bf16[128,4096]{1,0:T(8,128)(2,1)}, bf16[128,4096]{1,0:T(8,128)(2,1)}, u32[]{:S(2)}, u32[]{:S(2)}) %collective-permute-start.8) | collective-permute-done | bytes 1048608 | tf_op jit(solution)/shard_map/ppermute | solution.py:74
  190.1 5.6 %multiply_convert_fusion.3 = (bf16[128,4096]{1,0:T(8,128)(2,1)}, bf16[128,4096]{1,0:T(8,128)(2,1)}) fusion(bf16[128,4096]{1,0:T(8,128)(2,1)} %param.9, bf16[128,4096]{1,0:T(8,128)(2,1)} %collective-permute-done.9, bf16[128,4096]{1,0:T(8,128)(2,1)} %collective-permute-done.8, bf16[128,4096]{1,0:T(8,128)(2,1)} %collective-permute-done.7, ...), kind=kLoop, calls=%fused_computation.20 | loop fusion | flops 11010048 | bytes 9437188 | tf_op jit(solution)/shard_map/convert_element_type | solution.py:80
  196.6 14.6 %multiply_convert_fusion = bf16[4096,1024]{1,0:T(8,128)(2,1)} fusion(bf16[1024,4096]{1,0:T(8,128)(2,1)} %all-gather.4.cloned.1.call-done, bf16[1024,1024]{1,0:T(8,128)(2,1)S(1)} %constant_dynamic-update-slice_fusion.4), kind=kOutput, calls=%fused_computation | convolution fusion | flops 8598323200 | bytes 18874368 | tf_op jit(solution)/shard_map/dot_general | solution.py:82
  211.1 64.4 %all-gather.6.cloned.1.call-done = bf16[1024,4096]{1,0:T(8,128)(2,1)} async-done(((bf16[128,4096]{1,0:T(8,128)(2,1)}), bf16[1024,4096]{1,0:T(8,128)(2,1)}) %all-gather.6.cloned.1.call-update) | async-done | bytes 8388624 | tf_op jit(solution)/shard_map/all_gather | solution.py:85
  275.5 12.8 %fusion.23 = f32[1024,1024]{1,0:T(8,128)S(1)} fusion(bf16[1024,4096]{1,0:T(8,128)(2,1)} %all-gather.6.cloned.1.call-done, bf16[1024,4096]{1,0:T(8,128)(2,1)} %param.11), kind=kOutput, calls=%fused_computation.55 | convolution fusion | flops 8589934592 | bytes 20971520 | tf_op jit(solution)/shard_map/dot_general | solution.py:91
  293.0 12.8 %multiply_convert_fusion.2 = bf16[1024,4096]{1,0:T(8,128)(2,1)} fusion(bf16[1024,1024]{1,0:T(8,128)(2,1)} %constant_dynamic-update-slice_fusion, bf16[1024,4096]{1,0:T(8,128)(2,1)S(1)} %copy-done.4), kind=kOutput, calls=%fused_computation.2 | convolution fusion | flops 8598323200 | bytes 18874368 | tf_op jit(solution)/shard_map/dot_general | solution.py:87
  305.8 9.8 %collective-permute-done.12 = f32[256,1024]{1,0:T(8,128)S(1)} collective-permute-done((f32[256,1024]{1,0:T(8,128)S(1)}, f32[256,1024]{1,0:T(8,128)S(1)}, u32[]{:S(2)}, u32[]{:S(2)}) %collective-permute-start.12) | collective-permute-done | bytes 1048608 | tf_op jit(solution)/shard_map/ppermute | solution.py:35
  315.6 20.9 %collective-permute-done.11 = f32[256,1024]{1,0:T(8,128)S(1)} collective-permute-done((f32[256,1024]{1,0:T(8,128)S(1)}, f32[256,1024]{1,0:T(8,128)S(1)}, u32[]{:S(2)}, u32[]{:S(2)}) %collective-permute-start.11) | collective-permute-done | bytes 1048608 | tf_op jit(solution)/shard_map/ppermute | solution.py:35
  337.8 20.5 %all-gather.8.cloned.1.call-done = bf16[1024,4096]{1,0:T(8,128)(2,1)} async-done(((bf16[128,4096]{1,0:T(8,128)(2,1)}), bf16[1024,4096]{1,0:T(8,128)(2,1)}) %all-gather.8.cloned.1.call-update) | async-done | bytes 8388624 | tf_op jit(solution)/shard_map/all_gather | solution.py:86
  358.3 12.8 %fusion.24 = f32[1024,1024]{1,0:T(8,128)S(1)} fusion(bf16[1024,4096]{1,0:T(8,128)(2,1)} %all-gather.8.cloned.1.call-done, bf16[1024,4096]{1,0:T(8,128)(2,1)} %param.12), kind=kOutput, calls=%fused_computation.56 | convolution fusion | flops 8589934592 | bytes 20971520 | tf_op jit(solution)/shard_map/dot_general | solution.py:96
  373.4 2.4 collective-permute-start.13
  375.8 12.8 %multiply_convert_fusion.1 = bf16[1024,4096]{1,0:T(8,128)(2,1)} fusion(bf16[1024,1024]{1,0:T(8,128)(2,1)} %constant_dynamic-update-slice_fusion, bf16[1024,4096]{1,0:T(8,128)(2,1)S(1)} %copy-done.3), kind=kOutput, calls=%fused_computation.1 | convolution fusion | flops 8598323200 | bytes 18874368 | tf_op jit(solution)/shard_map/dot_general | solution.py:101
  388.6 8.2 %collective-permute-done.14 = bf16[256,1024]{1,0:T(8,128)(2,1)S(1)} collective-permute-done((bf16[256,1024]{1,0:T(8,128)(2,1)S(1)}, bf16[256,1024]{1,0:T(8,128)(2,1)S(1)}, u32[]{:S(2)}, u32[]{:S(2)}) %collective-permute-start.14) | collective-permute-done | bytes 524320 | tf_op jit(solution)/shard_map/ppermute | solution.py:35
  (52 shorter events, 31.4 us)
Async XLA Ops:
  7.2 3.3 copy-start.1
  7.2 84.2 %all-gather.4.cloned.1.call-start = ((), (), s32[]{:S(2)}) async-start(), calls=%async_computation | async-start | bytes 9437184 | tf_op jit(solution)/shard_map/all_gather | solution.py:46
  10.4 265.1 %all-gather.6.cloned.1.call-start = ((), (), s32[]{:S(2)}) async-start(), calls=%async_computation.1 | async-start | bytes 9437184 | tf_op jit(solution)/shard_map/all_gather | solution.py:85
  10.5 15.0 %collective-permute-start = (bf16[256,1024]{1,0:T(8,128)(2,1)S(1)}, bf16[256,1024]{1,0:T(8,128)(2,1)}, u32[]{:S(2)}, u32[]{:S(2)}) collective-permute-start(bf16[256,1024]{1,0:T(8,128)(2,1)S(1)} %copy-done.1), channel_id=1, source_target_pairs={{0,1},{1,2},{2,3},{3,0},{4,5},{5,6},{6,7},{7,4},{8,9},{9,10},{10,1... | collective-permute-start | bytes 1572872 | tf_op jit(solution)/shard_map/ppermute | solution.py:23
  12.0 24.7 %collective-permute-start.1 = (bf16[256,1024]{1,0:T(8,128)(2,1)S(1)}, bf16[256,1024]{1,0:T(8,128)(2,1)}, u32[]{:S(2)}, u32[]{:S(2)}) collective-permute-start(bf16[256,1024]{1,0:T(8,128)(2,1)S(1)} %copy-done.1), channel_id=1, source_target_pairs={{0,2},{1,3},{2,0},{3,1},{4,6},{5,7},{6,4},{7,5},{8,10},{9,11},{10,... | collective-permute-start | bytes 1572872 | tf_op jit(solution)/shard_map/ppermute | solution.py:23
  12.5 25.3 %collective-permute-start.2 = (bf16[256,1024]{1,0:T(8,128)(2,1)S(1)}, bf16[256,1024]{1,0:T(8,128)(2,1)S(1)}, u32[]{:S(2)}, u32[]{:S(2)}) collective-permute-start(bf16[256,1024]{1,0:T(8,128)(2,1)S(1)} %copy-done.1), channel_id=1, source_target_pairs={{0,3},{1,0},{2,1},{3,2},{4,7},{5,4},{6,5},{7,6},{8,11},{9,8},{10,9... | collective-permute-start | bytes 1572872 | tf_op jit(solution)/shard_map/ppermute | solution.py:23
  14.4 23.8 %copy-start.2 = (bf16[4096,1024]{1,0:T(8,128)(2,1)S(1)}, bf16[4096,1024]{1,0:T(8,128)(2,1)}, u32[]{:S(2)}) copy-start(bf16[4096,1024]{1,0:T(8,128)(2,1)} %param.13) | copy-start | bytes 25165828
  45.0 30.5 %collective-permute-start.3 = (f32[512,4096]{1,0:T(8,128)}, f32[512,4096]{1,0:T(8,128)}, u32[]{:S(2)}, u32[]{:S(2)}) collective-permute-start(f32[512,4096]{1,0:T(8,128)} %fusion.22), channel_id=1, source_target_pairs={{0,4},{4,0},{1,5},{5,1},{2,6},{6,2},{3,7},{7,3},{8,12},{12,8},{9,1... | collective-permute-start | bytes 25165832 | tf_op jit(solution)/shard_map/ppermute | solution.py:64
  45.0 15.0 %collective-permute-start.4 = (bf16[256,1024]{1,0:T(8,128)(2,1)}, bf16[256,1024]{1,0:T(8,128)(2,1)}, u32[]{:S(2)}, u32[]{:S(2)}) collective-permute-start(bf16[256,1024]{1,0:T(8,128)(2,1)} %param.7), channel_id=1, source_target_pairs={{0,1},{1,2},{2,3},{3,0},{4,5},{5,6},{6,7},{7,4},{8,9},{9,10},{10,1... | collective-permute-start | bytes 1572872 | tf_op jit(solution)/shard_map/ppermute | solution.py:23
  46.2 25.6 %collective-permute-start.5 = (bf16[256,1024]{1,0:T(8,128)(2,1)}, bf16[256,1024]{1,0:T(8,128)(2,1)}, u32[]{:S(2)}, u32[]{:S(2)}) collective-permute-start(bf16[256,1024]{1,0:T(8,128)(2,1)} %param.7), channel_id=1, source_target_pairs={{0,2},{1,3},{2,0},{3,1},{4,6},{5,7},{6,4},{7,5},{8,10},{9,11},{10,... | collective-permute-start | bytes 1572872 | tf_op jit(solution)/shard_map/ppermute | solution.py:23
  46.7 27.0 %collective-permute-start.6 = (bf16[256,1024]{1,0:T(8,128)(2,1)}, bf16[256,1024]{1,0:T(8,128)(2,1)}, u32[]{:S(2)}, u32[]{:S(2)}) collective-permute-start(bf16[256,1024]{1,0:T(8,128)(2,1)} %param.7), channel_id=1, source_target_pairs={{0,3},{1,0},{2,1},{3,2},{4,7},{5,4},{6,5},{7,6},{8,11},{9,8},{10,9... | collective-permute-start | bytes 1572872 | tf_op jit(solution)/shard_map/ppermute | solution.py:23
  91.3 98.8 %copy-start = (bf16[128,4096]{1,0:T(8,128)(2,1)S(1)}, bf16[128,4096]{1,0:T(8,128)(2,1)}, u32[]{:S(2)}) copy-start(bf16[128,4096]{1,0:T(8,128)(2,1)} %param.10) | copy-start | bytes 3145732
  96.1 71.2 %collective-permute-start.9 = (bf16[128,4096]{1,0:T(8,128)(2,1)}, bf16[128,4096]{1,0:T(8,128)(2,1)}, u32[]{:S(2)}, u32[]{:S(2)}) collective-permute-start(bf16[128,4096]{1,0:T(8,128)(2,1)} %get-tuple-element.27), channel_id=1, source_target_pairs={{0,16},{8,24},{16,0},{24,8},{1,17},{9,25},{17,1},{25,9},{2,18},{10... | collective-permute-start | bytes 3145736 | tf_op jit(solution)/shard_map/ppermute | solution.py:74
  98.5 91.6 %collective-permute-start.8 = (bf16[128,4096]{1,0:T(8,128)(2,1)}, bf16[128,4096]{1,0:T(8,128)(2,1)}, u32[]{:S(2)}, u32[]{:S(2)}) collective-permute-start(bf16[128,4096]{1,0:T(8,128)(2,1)} %get-tuple-element.28), channel_id=1, source_target_pairs={{0,24},{8,0},{16,8},{24,16},{1,25},{9,1},{17,9},{25,17},{2,26},{10... | collective-permute-start | bytes 3145736 | tf_op jit(solution)/shard_map/ppermute | solution.py:74
  100.1 90.0 %collective-permute-start.7 = (bf16[128,4096]{1,0:T(8,128)(2,1)}, bf16[128,4096]{1,0:T(8,128)(2,1)}, u32[]{:S(2)}, u32[]{:S(2)}) collective-permute-start(bf16[128,4096]{1,0:T(8,128)(2,1)} %get-tuple-element.26), channel_id=1, source_target_pairs={{0,8},{8,16},{16,24},{24,0},{1,9},{9,17},{17,25},{25,1},{2,10},{10... | collective-permute-start | bytes 3145736 | tf_op jit(solution)/shard_map/ppermute | solution.py:74
  195.8 162.5 %all-gather.8.cloned.1.call-start = ((), (), s32[]{:S(2)}) async-start(), calls=%async_computation.2 | async-start | bytes 9437184 | tf_op jit(solution)/shard_map/all_gather | solution.py:86
  275.5 17.5 %copy-start.4 = (bf16[1024,4096]{1,0:T(8,128)(2,1)S(1)}, bf16[1024,4096]{1,0:T(8,128)(2,1)}, u32[]{:S(2)}) copy-start(bf16[1024,4096]{1,0:T(8,128)(2,1)} %all-gather.6.cloned.1.call-done) | copy-start | bytes 25165828
  288.6 27.0 %collective-permute-start.12 = (f32[256,1024]{1,0:T(8,128)S(1)}, f32[256,1024]{1,0:T(8,128)S(1)}, u32[]{:S(2)}, u32[]{:S(2)}) collective-permute-start(f32[256,1024]{1,0:T(8,128)S(1)} %get-tuple-element.33), channel_id=1, source_target_pairs={{0,3},{1,0},{2,1},{3,2},{4,7},{5,4},{6,5},{7,6},{8,11},{9,8},{10,9... | collective-permute-start | bytes 3145736 | tf_op jit(solution)/shard_map/ppermute | solution.py:35
  289.0 47.5 %collective-permute-start.11 = (f32[256,1024]{1,0:T(8,128)S(1)}, f32[256,1024]{1,0:T(8,128)S(1)}, u32[]{:S(2)}, u32[]{:S(2)}) collective-permute-start(f32[256,1024]{1,0:T(8,128)S(1)} %get-tuple-element.34), channel_id=1, source_target_pairs={{0,2},{1,3},{2,0},{3,1},{4,6},{5,7},{6,4},{7,5},{8,10},{9,11},{10,... | collective-permute-start | bytes 3145736 | tf_op jit(solution)/shard_map/ppermute | solution.py:35
  290.7 46.7 %collective-permute-start.10 = (f32[256,1024]{1,0:T(8,128)S(1)}, f32[256,1024]{1,0:T(8,128)S(1)}, u32[]{:S(2)}, u32[]{:S(2)}) collective-permute-start(f32[256,1024]{1,0:T(8,128)S(1)} %get-tuple-element.32), channel_id=1, source_target_pairs={{0,1},{1,2},{2,3},{3,0},{4,5},{5,6},{6,7},{7,4},{8,9},{9,10},{10,1... | collective-permute-start | bytes 3145736 | tf_op jit(solution)/shard_map/ppermute | solution.py:35
  358.3 17.5 %copy-start.3 = (bf16[1024,4096]{1,0:T(8,128)(2,1)S(1)}, bf16[1024,4096]{1,0:T(8,128)(2,1)}, u32[]{:S(2)}) copy-start(bf16[1024,4096]{1,0:T(8,128)(2,1)} %all-gather.8.cloned.1.call-done) | copy-start | bytes 25165828
  371.3 17.2 %collective-permute-start.15 = (bf16[256,1024]{1,0:T(8,128)(2,1)S(1)}, bf16[256,1024]{1,0:T(8,128)(2,1)S(1)}, u32[]{:S(2)}, u32[]{:S(2)}) collective-permute-start(bf16[256,1024]{1,0:T(8,128)(2,1)S(1)} %get-tuple-element.30), channel_id=1, source_target_pairs={{0,3},{1,0},{2,1},{3,2},{4,7},{5,4},{6,5},{7,6},{8,11},{9,8},{10,9... | collective-permute-start | bytes 1572872 | tf_op jit(solution)/shard_map/ppermute | solution.py:35
  371.7 25.0 %collective-permute-start.14 = (bf16[256,1024]{1,0:T(8,128)(2,1)S(1)}, bf16[256,1024]{1,0:T(8,128)(2,1)S(1)}, u32[]{:S(2)}, u32[]{:S(2)}) collective-permute-start(bf16[256,1024]{1,0:T(8,128)(2,1)S(1)} %get-tuple-element.31), channel_id=1, source_target_pairs={{0,2},{1,3},{2,0},{3,1},{4,6},{5,7},{6,4},{7,5},{8,10},{9,11},{10,... | collective-permute-start | bytes 1572872 | tf_op jit(solution)/shard_map/ppermute | solution.py:35
  373.4 24.2 %collective-permute-start.13 = (bf16[256,1024]{1,0:T(8,128)(2,1)S(1)}, bf16[256,1024]{1,0:T(8,128)(2,1)S(1)}, u32[]{:S(2)}, u32[]{:S(2)}) collective-permute-start(bf16[256,1024]{1,0:T(8,128)(2,1)S(1)} %get-tuple-element.29), channel_id=1, source_target_pairs={{0,1},{1,2},{2,3},{3,0},{4,5},{5,6},{6,7},{7,4},{8,9},{9,10},{10,1... | collective-permute-start | bytes 1572872 | tf_op jit(solution)/shard_map/ppermute | solution.py:35
Sparse Core Ops, SparseCore 0:
  10.6 80.7 all-gather.3
  195.9 79.5 all-gather.5
  277.7 80.5 all-gather.7

commit v11 on v9

--- a/solution.py
+++ b/solution.py
@@ -77,6 +77,7 @@
     gate_local = (
         hid_rows * up_float * sigmoid_gate * (1.0 + gate_float * (1.0 - sigmoid_gate))
     ).astype(jnp.bfloat16)
+    gate_local, hid_rows = lax.optimization_barrier((gate_local, hid_rows))
     up_local = (hid_rows * silu_gate).astype(jnp.bfloat16)
 
     acc_down = lax.dot_general(

time: 411 us -> 410 us (level)
    convert_element_type x0 -> x1, other arithmetic: none -> 5.83 us  [body(): gate_local = (hid_rows * up_float * sigmoid_gate * (1.0 + gate_float * (1...]
  transfers between devices with their start and end apart: 19 -> 19, of which waited for: 15 -> 15; matrix products, arithmetic and copies ran while one was open for 22% -> 23% of each run, Pallas kernels for 0% -> 0%
where the time goes in v11:
time: 410 us; the launch traced here: 406 us
  waiting for transfers between devices  251 us (61%)
  matrix products  87.7 us (21%)
  starting transfers between devices  18.9 us (5%)
  other arithmetic  17.8 us (4%)
  local copies, waits for them, and re-layouts  17.1 us (4%)
  between operations  14 us (3%)
    ppermute x3, waiting for transfers between devices, body(): piece = lax.ppermute(piece.astype(jnp.bfloat16), 'z', shift_perm(chips, s))  90.2 us
    all_gather x1, waiting for transfers between devices, body(): gate_delta = lax.all_gather(gate_local, ROW, axis=0, tiled=True)  60.9 us
    ppermute x6, waiting for transfers between devices, gather_col(): part = lax.ppermute(block, 'col', shift_perm(n, s))  40.2 us
    ppermute x6, waiting for transfers between devices, reduce_scatter_col(): piece = lax.ppermute(piece.astype(send_dtype), 'col', shift_perm(n, s))  35.7 us
    all_gather x1, waiting for transfers between devices, body(): up_delta = lax.all_gather(up_local, ROW, axis=0, tiled=True)  19.4 us
    dot_general x1, matrix products, body(): lax.dot_general(act_full, up_delta, CONTRACT_FIRST, preferred_element_typ...  15.6 us
    dot_general x1, matrix products, body(): lax.dot_general(hidden_act, grad_full, CONTRACT_FIRST, preferred_element_...  14.8 us
    dot_general x1, matrix products, body(): lax.dot_general(act_full, gate_delta, CONTRACT_FIRST, preferred_element_t...  13.7 us
  transfers between devices with their start and end apart: 19, of which 15 were waited for; matrix products, arithmetic and copies ran while one was open for 23% of the time, Pallas kernels for 0%

profile of v11, /device:TPU:10, one launch (start us, length us, event | category | flops | bytes accessed | tf_op | source)
XLA Modules:
  0.0 406.3 jit_solution(13424678668484892783)
XLA Ops:
  7.2 3.2 fusion
  14.4 11.0 %collective-permute-done = bf16[256,1024]{1,0:T(8,128)(2,1)} collective-permute-done((bf16[256,1024]{1,0:T(8,128)(2,1)S(1)}, bf16[256,1024]{1,0:T(8,128)(2,1)}, u32[]{:S(2)}, u32[]{:S(2)}) %collective-permute-start) | collective-permute-done | bytes 524320 | tf_op jit(solution)/shard_map/ppermute | solution.py:23
  26.5 10.2 %collective-permute-done.1 = bf16[256,1024]{1,0:T(8,128)(2,1)} collective-permute-done((bf16[256,1024]{1,0:T(8,128)(2,1)S(1)}, bf16[256,1024]{1,0:T(8,128)(2,1)}, u32[]{:S(2)}, u32[]{:S(2)}) %collective-permute-start.1) | collective-permute-done | bytes 524320 | tf_op jit(solution)/shard_map/ppermute | solution.py:23
  38.2 6.8 %fusion.23 = f32[512,4096]{1,0:T(8,128)} fusion(bf16[512,1024]{1,0:T(8,128)(2,1)S(1)} %bitcast.71, bf16[4096,1024]{1,0:T(8,128)(2,1)S(1)} %copy-done.2), kind=kOutput, calls=%fused_computation.54 | convolution fusion | flops 4294967296 | bytes 17825792 | tf_op jit(solution)/shard_map/dot_general | solution.py:60
  50.9 9.0 %collective-permute-done.4 = bf16[256,1024]{1,0:T(8,128)(2,1)} collective-permute-done((bf16[256,1024]{1,0:T(8,128)(2,1)}, bf16[256,1024]{1,0:T(8,128)(2,1)}, u32[]{:S(2)}, u32[]{:S(2)}) %collective-permute-start.4) | collective-permute-done | bytes 524320 | tf_op jit(solution)/shard_map/ppermute | solution.py:23
  61.9 9.9 %collective-permute-done.5 = bf16[256,1024]{1,0:T(8,128)(2,1)} collective-permute-done((bf16[256,1024]{1,0:T(8,128)(2,1)}, bf16[256,1024]{1,0:T(8,128)(2,1)}, u32[]{:S(2)}, u32[]{:S(2)}) %collective-permute-start.5) | collective-permute-done | bytes 524320 | tf_op jit(solution)/shard_map/ppermute | solution.py:23
  75.5 11.5 %convolution_add_fusion = f32[512,4096]{1,0:T(8,128)} fusion(f32[512,4096]{1,0:T(8,128)} %collective-permute-done.3, bf16[512,1024]{1,0:T(8,128)(2,1)S(1)} %bitcast.70, bf16[4096,1024]{1,0:T(8,128)(2,1)} %param.13), kind=kOutput, calls=%fused_computation.3 | convolution fusion | flops 4297064448 | bytes 26214400 | tf_op jit(solution)/shard_map/dot_general | solution.py:65
  87.0 4.3 %all-gather.4.cloned.1.call-done = bf16[1024,4096]{1,0:T(8,128)(2,1)} async-done(((bf16[128,4096]{1,0:T(8,128)(2,1)}), bf16[1024,4096]{1,0:T(8,128)(2,1)}) %all-gather.4.cloned.1.call-update) | async-done | bytes 8388624 | tf_op jit(solution)/shard_map/all_gather | solution.py:46
  91.3 4.7 %fusion.10 = (bf16[128,4096]{1,0:T(8,128)(2,1)}, bf16[128,4096]{1,0:T(8,128)(2,1)}, bf16[128,4096]{1,0:T(8,128)(2,1)}) fusion(f32[4,128,4096]{2,1,0:T(8,128)} %bitcast.66, s32[]{:T(128)S(6)} %select_n.115, s32[]{:T(128)S(6)} %select_n.119, s32[]{:T(128)S(6)} %select_n.117), kind=kLoop, calls=%fused_computation.24 | loop fusion | bytes 6291468 | tf_op jit(solution)/shard_map/convert_element_type | solution.py:74
  101.5 21.9 %collective-permute-done.7 = bf16[128,4096]{1,0:T(8,128)(2,1)} collective-permute-done((bf16[128,4096]{1,0:T(8,128)(2,1)}, bf16[128,4096]{1,0:T(8,128)(2,1)}, u32[]{:S(2)}, u32[]{:S(2)}) %collective-permute-start.7) | collective-permute-done | bytes 1048608 | tf_op jit(solution)/shard_map/ppermute | solution.py:74
  123.3 65.8 %collective-permute-done.9 = bf16[128,4096]{1,0:T(8,128)(2,1)} collective-permute-done((bf16[128,4096]{1,0:T(8,128)(2,1)}, bf16[128,4096]{1,0:T(8,128)(2,1)}, u32[]{:S(2)}, u32[]{:S(2)}) %collective-permute-start.9) | collective-permute-done | bytes 1048608 | tf_op jit(solution)/shard_map/ppermute | solution.py:74
  191.6 5.8 %fusion.3 = (bf16[128,4096]{1,0:T(8,128)(2,1)}, f32[128,4096]{1,0:T(8,128)}) fusion(bf16[128,4096]{1,0:T(8,128)(2,1)} %param.10, bf16[128,4096]{1,0:T(8,128)(2,1)S(1)} %copy-done, bf16[128,4096]{1,0:T(8,128)(2,1)} %collective-permute-done.9, bf16[128,4096]{1,0:T(8,128)(2,1)} %collective-permute-done.8, bf16[128,4096]{1,0:T(8,128)(2,1)} %collective-permute-done.7, ...), kind=kLoop, calls=%fused_computation.12 | loop fusion | flops 9437184 | bytes 10485764 | tf_op jit(solution)/shard_map/convert_element_type | solution.py:79
  197.7 3.2 multiply_convert_fusion.3
  200.9 14.8 %multiply_convert_fusion = bf16[4096,1024]{1,0:T(8,128)(2,1)} fusion(bf16[1024,4096]{1,0:T(8,128)(2,1)} %all-gather.4.cloned.1.call-done, bf16[1024,1024]{1,0:T(8,128)(2,1)S(1)} %constant_dynamic-update-slice_fusion.4), kind=kOutput, calls=%fused_computation | convolution fusion | flops 8598323200 | bytes 18874368 | tf_op jit(solution)/shard_map/dot_general | solution.py:83
  215.7 60.9 %all-gather.6.cloned.1.call-done = bf16[1024,4096]{1,0:T(8,128)(2,1)} async-done(((bf16[128,4096]{1,0:T(8,128)(2,1)}), bf16[1024,4096]{1,0:T(8,128)(2,1)}) %all-gather.6.cloned.1.call-update) | async-done | bytes 8388624 | tf_op jit(solution)/shard_map/all_gather | solution.py:86
  276.6 12.8 %fusion.25 = f32[1024,1024]{1,0:T(8,128)S(1)} fusion(bf16[1024,4096]{1,0:T(8,128)(2,1)} %all-gather.6.cloned.1.call-done, bf16[1024,4096]{1,0:T(8,128)(2,1)} %param.11), kind=kOutput, calls=%fused_computation.56 | convolution fusion | flops 8589934592 | bytes 20971520 | tf_op jit(solution)/shard_map/dot_general | solution.py:92
  293.3 13.7 %fusion.24 = f32[1024,4096]{1,0:T(8,128)} fusion(bf16[1024,1024]{1,0:T(8,128)(2,1)} %constant_dynamic-update-slice_fusion, bf16[1024,4096]{1,0:T(8,128)(2,1)S(1)} %copy-done.3), kind=kOutput, calls=%fused_computation.55 | convolution fusion | flops 8589934592 | bytes 27262976 | tf_op jit(solution)/shard_map/dot_general | solution.py:88
  306.9 8.8 %collective-permute-done.10 = f32[256,1024]{1,0:T(8,128)S(1)} collective-permute-done((f32[256,1024]{1,0:T(8,128)S(1)}, f32[256,1024]{1,0:T(8,128)S(1)}, u32[]{:S(2)}, u32[]{:S(2)}) %collective-permute-start.10) | collective-permute-done | bytes 1048608 | tf_op jit(solution)/shard_map/ppermute | solution.py:35
  315.7 22.8 %collective-permute-done.12 = f32[256,1024]{1,0:T(8,128)S(1)} collective-permute-done((f32[256,1024]{1,0:T(8,128)S(1)}, f32[256,1024]{1,0:T(8,128)S(1)}, u32[]{:S(2)}, u32[]{:S(2)}) %collective-permute-start.12) | collective-permute-done | bytes 1048608 | tf_op jit(solution)/shard_map/ppermute | solution.py:35
  339.4 19.4 %all-gather.8.cloned.1.call-done = bf16[1024,4096]{1,0:T(8,128)(2,1)} async-done(((bf16[128,4096]{1,0:T(8,128)(2,1)}), bf16[1024,4096]{1,0:T(8,128)(2,1)}) %all-gather.8.cloned.1.call-update) | async-done | bytes 8388624 | tf_op jit(solution)/shard_map/all_gather | solution.py:87
  358.8 12.6 %fusion.26 = f32[1024,1024]{1,0:T(8,128)S(1)} fusion(bf16[1024,4096]{1,0:T(8,128)(2,1)} %all-gather.8.cloned.1.call-done, bf16[1024,4096]{1,0:T(8,128)(2,1)} %param.12), kind=kOutput, calls=%fused_computation.57 | convolution fusion | flops 8589934592 | bytes 20971520 | tf_op jit(solution)/shard_map/dot_general | solution.py:95
  375.3 15.6 %multiply_convert_fusion.1 = bf16[1024,4096]{1,0:T(8,128)(2,1)} fusion(bf16[1024,1024]{1,0:T(8,128)(2,1)} %constant_dynamic-update-slice_fusion, bf16[1024,4096]{1,0:T(8,128)(2,1)} %all-gather.8.cloned.1.call-done), kind=kOutput, calls=%fused_computation.1 | convolution fusion | flops 8598323200 | bytes 18874368 | tf_op jit(solution)/shard_map/dot_general | solution.py:100
  390.9 4.0 multiply_convert_fusion.2
  394.9 3.2 collective-permute-done.15
  (61 shorter events, 36.3 us)
Async XLA Ops:
  7.2 84.2 %all-gather.4.cloned.1.call-start = ((), (), s32[]{:S(2)}) async-start(), calls=%async_computation | async-start | bytes 9437184 | tf_op jit(solution)/shard_map/all_gather | solution.py:46
  10.4 266.2 %all-gather.6.cloned.1.call-start = ((), (), s32[]{:S(2)}) async-start(), calls=%async_computation.1 | async-start | bytes 9437184 | tf_op jit(solution)/shard_map/all_gather | solution.py:86
  10.5 15.0 %collective-permute-start = (bf16[256,1024]{1,0:T(8,128)(2,1)S(1)}, bf16[256,1024]{1,0:T(8,128)(2,1)}, u32[]{:S(2)}, u32[]{:S(2)}) collective-permute-start(bf16[256,1024]{1,0:T(8,128)(2,1)S(1)} %copy-done.1), channel_id=1, source_target_pairs={{0,1},{1,2},{2,3},{3,0},{4,5},{5,6},{6,7},{7,4},{8,9},{9,10},{10,1... | collective-permute-start | bytes 1572872 | tf_op jit(solution)/shard_map/ppermute | solution.py:23
  12.0 24.7 %collective-permute-start.1 = (bf16[256,1024]{1,0:T(8,128)(2,1)S(1)}, bf16[256,1024]{1,0:T(8,128)(2,1)}, u32[]{:S(2)}, u32[]{:S(2)}) collective-permute-start(bf16[256,1024]{1,0:T(8,128)(2,1)S(1)} %copy-done.1), channel_id=1, source_target_pairs={{0,2},{1,3},{2,0},{3,1},{4,6},{5,7},{6,4},{7,5},{8,10},{9,11},{10,... | collective-permute-start | bytes 1572872 | tf_op jit(solution)/shard_map/ppermute | solution.py:23
  12.5 25.3 %collective-permute-start.2 = (bf16[256,1024]{1,0:T(8,128)(2,1)S(1)}, bf16[256,1024]{1,0:T(8,128)(2,1)S(1)}, u32[]{:S(2)}, u32[]{:S(2)}) collective-permute-start(bf16[256,1024]{1,0:T(8,128)(2,1)S(1)} %copy-done.1), channel_id=1, source_target_pairs={{0,3},{1,0},{2,1},{3,2},{4,7},{5,4},{6,5},{7,6},{8,11},{9,8},{10,9... | collective-permute-start | bytes 1572872 | tf_op jit(solution)/shard_map/ppermute | solution.py:23
  14.4 23.8 %copy-start.2 = (bf16[4096,1024]{1,0:T(8,128)(2,1)S(1)}, bf16[4096,1024]{1,0:T(8,128)(2,1)}, u32[]{:S(2)}) copy-start(bf16[4096,1024]{1,0:T(8,128)(2,1)} %param.13) | copy-start | bytes 25165828
  45.0 30.5 %collective-permute-start.3 = (f32[512,4096]{1,0:T(8,128)}, f32[512,4096]{1,0:T(8,128)}, u32[]{:S(2)}, u32[]{:S(2)}) collective-permute-start(f32[512,4096]{1,0:T(8,128)} %fusion.23), channel_id=1, source_target_pairs={{0,4},{4,0},{1,5},{5,1},{2,6},{6,2},{3,7},{7,3},{8,12},{12,8},{9,1... | collective-permute-start | bytes 25165832 | tf_op jit(solution)/shard_map/ppermute | solution.py:64
  45.0 15.0 %collective-permute-start.4 = (bf16[256,1024]{1,0:T(8,128)(2,1)}, bf16[256,1024]{1,0:T(8,128)(2,1)}, u32[]{:S(2)}, u32[]{:S(2)}) collective-permute-start(bf16[256,1024]{1,0:T(8,128)(2,1)} %param.7), channel_id=1, source_target_pairs={{0,1},{1,2},{2,3},{3,0},{4,5},{5,6},{6,7},{7,4},{8,9},{9,10},{10,1... | collective-permute-start | bytes 1572872 | tf_op jit(solution)/shard_map/ppermute | solution.py:23
  46.2 25.6 %collective-permute-start.5 = (bf16[256,1024]{1,0:T(8,128)(2,1)}, bf16[256,1024]{1,0:T(8,128)(2,1)}, u32[]{:S(2)}, u32[]{:S(2)}) collective-permute-start(bf16[256,1024]{1,0:T(8,128)(2,1)} %param.7), channel_id=1, source_target_pairs={{0,2},{1,3},{2,0},{3,1},{4,6},{5,7},{6,4},{7,5},{8,10},{9,11},{10,... | collective-permute-start | bytes 1572872 | tf_op jit(solution)/shard_map/ppermute | solution.py:23
  46.7 27.0 %collective-permute-start.6 = (bf16[256,1024]{1,0:T(8,128)(2,1)}, bf16[256,1024]{1,0:T(8,128)(2,1)}, u32[]{:S(2)}, u32[]{:S(2)}) collective-permute-start(bf16[256,1024]{1,0:T(8,128)(2,1)} %param.7), channel_id=1, source_target_pairs={{0,3},{1,0},{2,1},{3,2},{4,7},{5,4},{6,5},{7,6},{8,11},{9,8},{10,9... | collective-permute-start | bytes 1572872 | tf_op jit(solution)/shard_map/ppermute | solution.py:23
  91.3 100.3 %copy-start = (bf16[128,4096]{1,0:T(8,128)(2,1)S(1)}, bf16[128,4096]{1,0:T(8,128)(2,1)}, u32[]{:S(2)}) copy-start(bf16[128,4096]{1,0:T(8,128)(2,1)} %param.9) | copy-start | bytes 3145732
  96.1 27.3 %collective-permute-start.7 = (bf16[128,4096]{1,0:T(8,128)(2,1)}, bf16[128,4096]{1,0:T(8,128)(2,1)}, u32[]{:S(2)}, u32[]{:S(2)}) collective-permute-start(bf16[128,4096]{1,0:T(8,128)(2,1)} %get-tuple-element.30), channel_id=1, source_target_pairs={{0,8},{8,16},{16,24},{24,0},{1,9},{9,17},{17,25},{25,1},{2,10},{10... | collective-permute-start | bytes 3145736 | tf_op jit(solution)/shard_map/ppermute | solution.py:74
  98.5 90.6 %collective-permute-start.9 = (bf16[128,4096]{1,0:T(8,128)(2,1)}, bf16[128,4096]{1,0:T(8,128)(2,1)}, u32[]{:S(2)}, u32[]{:S(2)}) collective-permute-start(bf16[128,4096]{1,0:T(8,128)(2,1)} %get-tuple-element.31), channel_id=1, source_target_pairs={{0,16},{8,24},{16,0},{24,8},{1,17},{9,25},{17,1},{25,9},{2,18},{10... | collective-permute-start | bytes 3145736 | tf_op jit(solution)/shard_map/ppermute | solution.py:74
  101.5 90.2 %collective-permute-start.8 = (bf16[128,4096]{1,0:T(8,128)(2,1)}, bf16[128,4096]{1,0:T(8,128)(2,1)}, u32[]{:S(2)}, u32[]{:S(2)}) collective-permute-start(bf16[128,4096]{1,0:T(8,128)(2,1)} %get-tuple-element.32), channel_id=1, source_target_pairs={{0,24},{8,0},{16,8},{24,16},{1,25},{9,1},{17,9},{25,17},{2,26},{10... | collective-permute-start | bytes 3145736 | tf_op jit(solution)/shard_map/ppermute | solution.py:74
  197.5 161.4 %all-gather.8.cloned.1.call-start = ((), (), s32[]{:S(2)}) async-start(), calls=%async_computation.2 | async-start | bytes 9437184 | tf_op jit(solution)/shard_map/all_gather | solution.py:87
  289.7 26.0 %collective-permute-start.10 = (f32[256,1024]{1,0:T(8,128)S(1)}, f32[256,1024]{1,0:T(8,128)S(1)}, u32[]{:S(2)}, u32[]{:S(2)}) collective-permute-start(f32[256,1024]{1,0:T(8,128)S(1)} %get-tuple-element.36), channel_id=1, source_target_pairs={{0,1},{1,2},{2,3},{3,0},{4,5},{5,6},{6,7},{7,4},{8,9},{9,10},{10,1... | collective-permute-start | bytes 3145736 | tf_op jit(solution)/shard_map/ppermute | solution.py:35
  291.2 47.3 %collective-permute-start.12 = (f32[256,1024]{1,0:T(8,128)S(1)}, f32[256,1024]{1,0:T(8,128)S(1)}, u32[]{:S(2)}, u32[]{:S(2)}) collective-permute-start(f32[256,1024]{1,0:T(8,128)S(1)} %get-tuple-element.37), channel_id=1, source_target_pairs={{0,3},{1,0},{2,1},{3,2},{4,7},{5,4},{6,5},{7,6},{8,11},{9,8},{10,9... | collective-permute-start | bytes 3145736 | tf_op jit(solution)/shard_map/ppermute | solution.py:35
  291.8 47.2 %collective-permute-start.11 = (f32[256,1024]{1,0:T(8,128)S(1)}, f32[256,1024]{1,0:T(8,128)S(1)}, u32[]{:S(2)}, u32[]{:S(2)}) collective-permute-start(f32[256,1024]{1,0:T(8,128)S(1)} %get-tuple-element.38), channel_id=1, source_target_pairs={{0,2},{1,3},{2,0},{3,1},{4,6},{5,7},{6,4},{7,5},{8,10},{9,11},{10,... | collective-permute-start | bytes 3145736 | tf_op jit(solution)/shard_map/ppermute | solution.py:35
  371.5 19.4 %slice-start = ((s8[16777216]{0:T(1024)(128)(4,1)}), s8[4194304]{0:T(1024)(128)(4,1)S(1)}, s32[]{:S(2)}) async-start(s8[16777216]{0:T(1024)(128)(4,1)} %bitcast.61), calls=%async_computation.3 | async-start | bytes 8388608
  371.8 23.2 %collective-permute-start.13 = (bf16[256,1024]{1,0:T(8,128)(2,1)S(1)}, bf16[256,1024]{1,0:T(8,128)(2,1)S(1)}, u32[]{:S(2)}, u32[]{:S(2)}) collective-permute-start(bf16[256,1024]{1,0:T(8,128)(2,1)S(1)} %get-tuple-element.33), channel_id=1, source_target_pairs={{0,1},{1,2},{2,3},{3,0},{4,5},{5,6},{6,7},{7,4},{8,9},{9,10},{10,1... | collective-permute-start | bytes 1572872 | tf_op jit(solution)/shard_map/ppermute | solution.py:35
  373.3 24.9 %collective-permute-start.15 = (bf16[256,1024]{1,0:T(8,128)(2,1)S(1)}, bf16[256,1024]{1,0:T(8,128)(2,1)S(1)}, u32[]{:S(2)}, u32[]{:S(2)}) collective-permute-start(bf16[256,1024]{1,0:T(8,128)(2,1)S(1)} %get-tuple-element.34), channel_id=1, source_target_pairs={{0,3},{1,0},{2,1},{3,2},{4,7},{5,4},{6,5},{7,6},{8,11},{9,8},{10,9... | collective-permute-start | bytes 1572872 | tf_op jit(solution)/shard_map/ppermute | solution.py:35
  373.8 17.0 %slice-start.2 = ((s8[16777216]{0:T(1024)(128)(4,1)}), s8[4194304]{0:T(1024)(128)(4,1)S(1)}, s32[]{:S(2)}) async-start(s8[16777216]{0:T(1024)(128)(4,1)} %bitcast.61), calls=%async_computation.5 | async-start | bytes 8388608
  373.8 17.0 %slice-start.3 = ((s8[16777216]{0:T(1024)(128)(4,1)}), s8[4194304]{0:T(1024)(128)(4,1)S(1)}, s32[]{:S(2)}) async-start(s8[16777216]{0:T(1024)(128)(4,1)} %bitcast.61), calls=%async_computation.6 | async-start | bytes 8388608
  373.8 24.7 %collective-permute-start.14 = (bf16[256,1024]{1,0:T(8,128)(2,1)S(1)}, bf16[256,1024]{1,0:T(8,128)(2,1)S(1)}, u32[]{:S(2)}, u32[]{:S(2)}) collective-permute-start(bf16[256,1024]{1,0:T(8,128)(2,1)S(1)} %get-tuple-element.35), channel_id=1, source_target_pairs={{0,2},{1,3},{2,0},{3,1},{4,6},{5,7},{6,4},{7,5},{8,10},{9,11},{10,... | collective-permute-start | bytes 1572872 | tf_op jit(solution)/shard_map/ppermute | solution.py:35
  (3 other events, 37.0 us)
Sparse Core Ops, SparseCore 0:
  10.6 80.7 all-gather.3
  197.6 78.9 all-gather.5
  278.2 80.5 all-gather.7
